TPU v7x, 32 devices: a whole 2x2x4 slice. The times are simulated.
32 devices in a mesh: group: 2 (over y), tm: 4 (over z), member: 2 (over x), sub: 2 (over core).
Axes of the slice: x: 2, y: 2, z: 4, core: 2. Of those that a mesh axis runs over, the one named last changes fastest.
Arguments:
- slices: float32 [8, 4, 2, 256, 256], P(('group', 'member', 'sub'), 'tm'), parts along dimension 0, may hold values from -1 to 1, as said below
- controls: float32 [4, 2, 256, 256], replicated, as said below
- target: float32 [4, 256, 256], P('group'), parts along dimension 0, may hold values from -1 to 1, as said below
Outputs:
- gradient: float32 [8, 4], P(('group', 'tm')), parts along dimension 0
There are 2 independent parts, one for each index of `group`. A program takes and returns all parts, laid end to end along the dimension named above; an argument that names none is the same for every part. Nothing has to cross between parts.
Inputs may be any that keep to these rules, and one draw needn't show every extreme that they name: Each slices[m, k] is a unitary matrix. `controls`: each control generator is Hermitian. The target is a unitary matrix.
All inputs are finite; a program needn't handle non-finite values.
Results may differ from a plain program's by a relative error of at most 0.0003.
Values sent between devices are 32-bit elements; how exact they have to be, the bound alone decides.
No kernel may reach another device: no remote copies, remote signals or barrier semaphores. Data moves between devices by JAX's collectives and lax.ppermute only.
A program may use at most 64 MiB of HBM per device.

v0:
```python
import jax
import jax.numpy as jnp
from jax import lax
from jax.sharding import PartitionSpec as P

HIGH = lax.Precision.HIGHEST


def cmul(left, right):
    real_part = jnp.matmul(left[..., 0, :, :], right[..., 0, :, :], precision=HIGH) - jnp.matmul(
        left[..., 1, :, :], right[..., 1, :, :], precision=HIGH
    )
    imag_part = jnp.matmul(left[..., 0, :, :], right[..., 1, :, :], precision=HIGH) + jnp.matmul(
        left[..., 1, :, :], right[..., 0, :, :], precision=HIGH
    )
    return jnp.stack([real_part, imag_part], axis=-3)


def cdagger(matrix):
    return jnp.stack(
        [jnp.swapaxes(matrix[..., 0, :, :], -1, -2), -jnp.swapaxes(matrix[..., 1, :, :], -1, -2)],
        axis=-3,
    )


def local_suffixes(identity_b):
    pieces = [identity_b]
    return jnp.stack(pieces, axis=1)


def tree_product(matrices):
    while matrices.shape[0] > 1:
        earlier_half = matrices[0::2]
        later_half = matrices[1::2]
        matrices = cmul(later_half, earlier_half)
    return matrices[0]


def per_device(slices, controls, target):
    members_here = slices.shape[0]
    order = slices.shape[-1]
    identity = jnp.stack(
        [jnp.eye(order, dtype=jnp.float32), jnp.zeros((order, order), jnp.float32)]
    )
    identity_b = jnp.broadcast_to(identity, (members_here, 2, order, order))
    target_dag = cdagger(target)
    current = slices[:, 0]
    prefixes = [current]
    local_prefix = jnp.stack(prefixes, axis=1)
    blocks = lax.axis_size("tm")
    position = lax.axis_index("tm")
    gathered = lax.all_gather(current, "tm", axis=0, tiled=True)
    gathered = gathered.reshape((blocks, members_here, 2, order, order))
    block_ids = jnp.arange(blocks, dtype=jnp.int32)[:, None, None, None, None]
    early_set = jnp.where(block_ids < position, gathered, identity_b[None])
    late_set = jnp.where(block_ids > position, gathered, identity_b[None])
    carry_in = tree_product(early_set)
    carry_out = tree_product(late_set)
    forward = cmul(local_prefix, carry_in[:, None])
    backward = cmul(carry_out[:, None], local_suffixes(identity_b))
    costate = cmul(cmul(forward, target_dag), backward)
    over_re = jnp.trace(costate[:, 0, 0], axis1=-2, axis2=-1)
    over_im = jnp.trace(costate[:, 0, 1], axis1=-2, axis2=-1)
    s_re = jnp.einsum(
        "mkab,jab->mkj", costate[:, :, 0], controls[:, 0], precision=HIGH
    ) + jnp.einsum("mkab,jab->mkj", costate[:, :, 1], controls[:, 1], precision=HIGH)
    s_im = jnp.einsum(
        "mkab,jab->mkj", costate[:, :, 1], controls[:, 0], precision=HIGH
    ) - jnp.einsum("mkab,jab->mkj", costate[:, :, 0], controls[:, 1], precision=HIGH)
    terms = over_re[:, None, None] * s_im - over_im[:, None, None] * s_re
    partial_value = jnp.sum(terms, axis=0)
    total = lax.psum(partial_value, ("member", "sub"))
    member_count = members_here * lax.axis_size("member") * lax.axis_size("sub")
    return total * (2.0 / member_count)


def solution(mesh):
    placed = (P(("group", "member", "sub"), "tm", None, None, None), P(), P("group", None, None))
    return jax.shard_map(
        per_device, mesh=mesh, in_specs=placed, out_specs=P(("group", "tm"), None), check_vma=False
    )
```

profile of v0, /device:TPU:0, one launch (start us, length us, event | category | flops | bytes accessed | tf_op | source)
XLA Modules:
  0.0 112.9 jit_solution(17755203991981334427)
XLA Ops:
  6.5 0.7 all-gather.3.cloned.1.call-update
  7.4 1.8 %slice_bitcast_fusion.1 = (f32[4,256,256]{2,1,0:T(8,128)S(1)}, f32[4,256,256]{2,1,0:T(8,128)S(1)}) fusion(f32[4,2,256,256]{3,2,1,0:T(8,128)} %param.4), kind=kLoop, calls=%fused_computation.31 | loop fusion | bytes 4194304 | tf_op jit(solution)/shard_map/squeeze | solution.py:68
  9.2 48.4 %all-gather.3.cloned.1.call-done = f32[4,1,2,256,256]{4,3,0,2,1:T(8,128)} async-done(((f32[1,1,2,256,256]{4,3,0,2,1:T(8,128)}), f32[4,1,2,256,256]{4,3,0,2,1:T(8,128)}) %all-gather.3.cloned.1.call-update) | async-done | bytes 2097168 | tf_op jit(solution)/shard_map/all_gather | solution.py:52
  57.6 2.1 %fusion.1 = (f32[4,1,2,256,256]{4,3,0,2,1:T(8,128)S(1)}, f32[4,1,2,256,256]{4,3,0,2,1:T(8,128)S(1)}) fusion(f32[4,1,2,256,256]{4,3,0,2,1:T(8,128)} %all-gather.3.cloned.1.call-done, f32[2,256,256]{2,1,0:T(8,128)S(1)} %get-tuple-element.14, pred[4]{0:T(512)(128)(4,1)S(1)} %get-tuple-element.19, pred[4]{0:T(512)(128)(4,1)S(1)} %get-tuple-element.20), kind=kLoop, calls=%fused_computation.3 | loop fusion | flops 1048576 | bytes 6815752 | tf_op jit(solution)/shard_map/jit(_where)/select_n | solution.py:56
  59.9 0.7 fusion.14
  60.6 0.7 fusion.15
  61.2 0.7 convolution_add_fusion
  61.9 0.7 convolution_subtract_fusion
  64.5 0.7 fusion.12
  65.2 0.7 fusion.13
  65.9 0.7 convolution_add_fusion.1
  66.5 0.7 convolution_subtract_fusion.1
  68.8 0.6 fusion.26
  70.0 0.6 convolution_subtract_fusion.6
  71.2 0.8 fusion.20
  73.0 0.6 convolution_add_fusion.6
  73.6 0.6 convolution_add_fusion.4
  75.6 1.0 select_reduce_fusion
  76.5 1.0 select_reduce_fusion.1
  77.5 5.0 %convolution_bitcast_fusion = f32[4]{0:T(128)S(1)} fusion(f32[4,256,256]{2,1,0:T(8,128)S(1)} %get-tuple-element.8, f32[256,256,1]{1,0,2:T(8,128)S(1)} %bitcast.155), kind=kOutput, calls=%fused_computation.20 | convolution fusion | flops 3145728 | bytes 1310736 | tf_op jit(solution)/shard_map/mkab,jab->mkj/dot_general | solution.py:66
  82.5 5.0 %convolution_bitcast_fusion.2 = f32[4]{0:T(128)S(1)} fusion(f32[4,256,256]{2,1,0:T(8,128)S(1)} %get-tuple-element.8, f32[256,256,1]{1,0,2:T(8,128)S(1)} %bitcast.157), kind=kOutput, calls=%fused_computation.22 | convolution fusion | flops 3145728 | bytes 1310736 | tf_op jit(solution)/shard_map/mkab,jab->mkj/dot_general | solution.py:69
  87.5 5.6 %fusion.7 = f32[4]{0:T(128)S(1)} fusion(f32[4]{0:T(128)S(1)} %convolution_bitcast_fusion, f32[4,256,256]{2,1,0:T(8,128)S(1)} %get-tuple-element.7, f32[256,256,1]{1,0,2:T(8,128)S(1)} %bitcast.158, f32[]{:T(128)} %get-tuple-element.15), kind=kOutput, calls=%fused_computation.29 | convolution fusion | flops 3145736 | bytes 1310756 | tf_op jit(solution)/shard_map/mkab,jab->mkj/dot_general | solution.py:64
  93.1 5.6 %fusion.5 = f32[1,4]{1,0:T(1,128)S(1)} fusion(f32[4]{0:T(128)S(1)} %fusion.7, f32[4]{0:T(128)S(1)} %convolution_bitcast_fusion.2, f32[4,256,256]{2,1,0:T(8,128)S(1)} %get-tuple-element.7, f32[256,256,1]{1,0,2:T(8,128)S(1)} %bitcast.156, f32[]{:T(128)} %get-tuple-element.17), kind=kOutput, calls=%fused_computation.27 | convolution fusion | flops 3145740 | bytes 1310772 | tf_op jit(solution)/shard_map/mkab,jab->mkj/dot_general | solution.py:67
  98.7 6.8 %psum.7 = f32[1,4]{1,0:T(1,128)S(1)} all-reduce(f32[1,4]{1,0:T(1,128)S(1)} %fusion.5), channel_id=1, replica_groups=mesh['group'=2,'tm'=4,'member'=2,'sub'=2] {'member','sub'}, use_global_device_ids=true, to_apply=%region_2.3 | all-reduce | flops 4 | bytes 32 | tf_op jit(solution)/shard_map/psum | solution.py:72
  (28 shorter events, 7.8 us)
Async XLA Ops:
  6.5 51.1 %all-gather.3.cloned.1.call-start = ((), (), s32[]{:S(2)}) async-start(), calls=%async_computation | async-start | bytes 2621440 | tf_op jit(solution)/shard_map/all_gather | solution.py:52
  67.2 1.6 %copy-start = (f32[1,1,2,256,256]{4,3,2,1,0:T(8,128)S(1)}, f32[1,1,2,256,256]{4,3,2,1,0:T(8,128)}, u32[]{:S(2)}) copy-start(f32[1,1,2,256,256]{4,3,2,1,0:T(8,128)} %param.3) | copy-start | bytes 1572868
  68.4 2.2 %copy-start.1 = (f32[2,256,256]{2,1,0:T(8,128)S(1)}, f32[2,256,256]{2,1,0:T(8,128)}, u32[]{:S(2)}) copy-start(f32[2,256,256]{2,1,0:T(8,128)} %param.5) | copy-start | bytes 1572868
Sparse Core Ops, SparseCore 0:
  8.9 48.6 all-gather.2
where the time goes:
time: 113 us
  waiting for transfers between devices  49.1 us (43%)
  matrix products  38.3 us (34%)
  between operations  13.7 us (12%)
  blocking collectives  6.82 us (6%)
  other arithmetic  2.67 us (2%)
  local copies, waits for them, and re-layouts  2.22 us (2%)
    all_gather x1, waiting for transfers between devices, per_device(): gathered = lax.all_gather(current, 'tm', axis=0, tiled=True)  48.4 us
    psum x1, blocking collectives, per_device(): total = lax.psum(partial_value, ('member', 'sub'))  6.82 us
    dot_general x1, matrix products, per_device(): jnp.einsum('mkab,jab->mkj', costate[:, :, 1], controls[:, 0], precision=H...  5.59 us
    dot_general x1, matrix products, per_device(): jnp.einsum('mkab,jab->mkj', costate[:, :, 0], controls[:, 0], precision=H...  5.59 us
    dot_general x1, matrix products, per_device(): jnp.einsum('mkab,jab->mkj', costate[:, :, 0], controls[:, 1], precision=H...  4.99 us
    dot_general x1, matrix products, per_device(): jnp.einsum('mkab,jab->mkj', costate[:, :, 1], controls[:, 1], precision=H...  4.97 us
    dot_general x8, matrix products, cmul(): jnp.matmul(left[..., 1, :, :], right[..., 1, :, :], precision=HIGH)  4.55 us
    dot_general x8, matrix products, cmul(): jnp.matmul(left[..., 1, :, :], right[..., 0, :, :], precision=HIGH)  4.55 us
  transfers between devices with their start and end apart: 1, of which 1 were waited for; matrix products, arithmetic and copies ran while one was open for 2% of the time, Pallas kernels for 0%

commit v1 on v0

v1 whole, which is shorter than its diff:
```python
import jax
import jax.numpy as jnp
from jax import lax
from jax.sharding import PartitionSpec as P

HIGH = lax.Precision.HIGHEST
CHUNKS = 4


def block_left(u):
    top = jnp.concatenate([u[:, 0], -u[:, 1]], axis=-1)
    bottom = jnp.concatenate([u[:, 1], u[:, 0]], axis=-1)
    return jnp.concatenate([top, bottom], axis=-2)


def block_right(u):
    top = jnp.concatenate([u[:, 0], u[:, 1]], axis=-1)
    bottom = jnp.concatenate([-u[:, 1], u[:, 0]], axis=-1)
    return jnp.concatenate([top, bottom], axis=-2)


def per_device(slices, controls, target):
    members_here = slices.shape[0]
    order = slices.shape[-1]
    chunks = CHUNKS
    width = order // chunks
    blocks = lax.axis_size("tm")
    position = lax.axis_index("tm")
    unit = slices[:, 0]
    left_op = block_left(unit)
    right_op = block_right(unit)
    target_dag = jnp.concatenate([target[0].T, -target[1].T], axis=-1)
    right_pairs = [(i, i + 1) for i in range(blocks - 1)]
    left_pairs = [(i + 1, i) for i in range(blocks - 1)]
    is_first = position == 0
    is_last = position == blocks - 1

    fwd_buf = jnp.zeros((chunks + 2, members_here, 2 * order, width), jnp.float32)
    bwd_buf = jnp.zeros((chunks + 2, members_here, width, 2 * order), jnp.float32)
    fwd_out = None
    bwd_out = None
    steps = chunks + blocks - 1
    for step in range(steps):
        if step == 0:
            fwd_in = jnp.zeros((members_here, 2 * order, width), jnp.float32)
            bwd_in = jnp.zeros((members_here, width, 2 * order), jnp.float32)
        else:
            fwd_in = lax.ppermute(fwd_out, "tm", right_pairs)
            bwd_in = lax.ppermute(bwd_out, "tm", left_pairs)
        if step < chunks:
            cols = slice(step * width, (step + 1) * width)
            own_cols = jnp.concatenate([unit[:, 0, :, cols], unit[:, 1, :, cols]], axis=-2)
            rows = jnp.broadcast_to(target_dag[None, step * width:(step + 1) * width], bwd_in.shape)
            fwd_new = jnp.where(
                is_first, own_cols,
                jnp.einsum("mab,mbw->maw", left_op, fwd_in, precision=HIGH),
            )
            bwd_in = jnp.where(is_last, rows, bwd_in)
        else:
            fwd_new = jnp.einsum("mab,mbw->maw", left_op, fwd_in, precision=HIGH)
        fwd_chunk = jnp.clip(step - position, -1, chunks) + 1
        bwd_chunk = jnp.clip(step - (blocks - 1 - position), -1, chunks) + 1
        fwd_buf = lax.dynamic_update_index_in_dim(fwd_buf, fwd_new, fwd_chunk, 0)
        bwd_buf = lax.dynamic_update_index_in_dim(bwd_buf, bwd_in, bwd_chunk, 0)
        fwd_out = fwd_new
        if step < steps - 1:
            bwd_out = jnp.einsum("mwa,mab->mwb", bwd_in, right_op, precision=HIGH)

    fwd_all = fwd_buf[1:chunks + 1].reshape(chunks, members_here, 2, order, width)
    bwd_all = bwd_buf[1:chunks + 1].reshape(chunks, members_here, width, 2, order)
    parts = jnp.einsum("cmpaw,cmwqb->mpqab", fwd_all, bwd_all, precision=HIGH)
    q_re = parts[:, 0, 0] - parts[:, 1, 1]
    q_im = parts[:, 0, 1] + parts[:, 1, 0]
    eye = jnp.eye(order, dtype=bool)
    over_re = jnp.sum(jnp.where(eye, q_re, 0.0), axis=(-2, -1))
    over_im = jnp.sum(jnp.where(eye, q_im, 0.0), axis=(-2, -1))
    h_re = controls[None, :, 0]
    h_im = controls[None, :, 1]
    s_re = jnp.sum(q_re[:, None] * h_re + q_im[:, None] * h_im, axis=(-2, -1))
    s_im = jnp.sum(q_im[:, None] * h_re - q_re[:, None] * h_im, axis=(-2, -1))
    terms = over_re[:, None] * s_im - over_im[:, None] * s_re
    partial_value = jnp.sum(terms, axis=0, keepdims=True)
    total = lax.psum(partial_value, ("member", "sub"))
    member_count = members_here * lax.axis_size("member") * lax.axis_size("sub")
    return total * (2.0 / member_count)


def solution(mesh):
    placed = (P(("group", "member", "sub"), "tm", None, None, None), P(), P("group", None, None))
    return jax.shard_map(
        per_device, mesh=mesh, in_specs=placed, out_specs=P(("group", "tm"), None), check_vma=False
    )
```

time: 113 us -> 67.8 us (0.60)
  waiting for transfers between devices: 49.1 us -> 5.2 us
  starting transfers between devices: 0.01 us -> 35.6 us
  matrix products: 38.3 us -> 14.6 us
  between operations: 13.7 us -> 0.42 us
  blocking collectives: 6.82 us -> 5.67 us
    all_gather x1 -> x0, waiting for transfers between devices: 48.4 us -> none  [per_device(): gathered = lax.all_gather(current, 'tm', axis=0, tiled=True)]
    ppermute x0 -> x12, starting transfers between devices: none -> 35.6 us  [the longest x6 27.7 us: per_device(): fwd_in = lax.ppermute(fwd_out, 'tm', right_pairs)]
    dot_general x36 -> x14, matrix products: 38.3 us -> 14.6 us  [the longest x6 7.37 us: per_device(): bwd_out = jnp.einsum('mwa,mab->mwb', bwd_in, right_op, precision=HIGH)]
    ppermute x0 -> x12, waiting for transfers between devices: none -> 5.2 us  [the longest x6 5.19 us: per_device(): bwd_in = lax.ppermute(bwd_out, 'tm', left_pairs)]
    select_n x1 -> x0, other arithmetic: 2.05 us -> none  [per_device(): late_set = jnp.where(block_ids > position, gathered, identity_b[None])]
    squeeze x1, local copies, waits for them, and re-layouts: 1.77 us -> 0.04 us  [block_right(): top = jnp.concatenate([u[:, 0], u[:, 1]], axis=-1)]
    unnamed x4 -> x7, local copies, waits for them, and re-layouts: 0.01 us -> 1.51 us
    sub x0 -> x1, other arithmetic: none -> 1.21 us  [per_device(): terms = over_re[:, None] * s_im - over_im[:, None] * s_re]
  transfers between devices with their start and end apart: 1 -> 12, of which waited for: 1 -> 6; matrix products, arithmetic and copies ran while one was open for 2% -> 19% of each run, Pallas kernels for 0% -> 0%
where the time goes in v1:
time: 67.8 us; the launch traced here: 67.3 us
  starting transfers between devices  35.6 us (53%)
  matrix products  14.6 us (22%)
  blocking collectives  5.67 us (8%)
  waiting for transfers between devices  5.2 us (8%)
  other arithmetic  3.03 us (4%)
  local copies, waits for them, and re-layouts  2.83 us (4%)
    ppermute x6, starting transfers between devices, per_device(): fwd_in = lax.ppermute(fwd_out, 'tm', right_pairs)  27.7 us
    ppermute x6, starting transfers between devices, per_device(): bwd_in = lax.ppermute(bwd_out, 'tm', left_pairs)  7.9 us
    dot_general x6, matrix products, per_device(): bwd_out = jnp.einsum('mwa,mab->mwb', bwd_in, right_op, precision=HIGH)  7.37 us
    psum x1, blocking collectives, per_device(): total = lax.psum(partial_value, ('member', 'sub'))  5.67 us
    ppermute x6, waiting for transfers between devices, per_device(): bwd_in = lax.ppermute(bwd_out, 'tm', left_pairs)  5.19 us
    dot_general x4, matrix products, per_device(): jnp.einsum('mab,mbw->maw', left_op, fwd_in, precision=HIGH)  3.83 us
    dot_general x3, matrix products, per_device(): fwd_new = jnp.einsum('mab,mbw->maw', left_op, fwd_in, precision=HIGH)  2.39 us
    unnamed x7, local copies, waits for them, and re-layouts  1.51 us
  transfers between devices with their start and end apart: 12, of which 6 were waited for; matrix products, arithmetic and copies ran while one was open for 19% of the time, Pallas kernels for 0%

profile of v1, /device:TPU:0, one launch (start us, length us, event | category | flops | bytes accessed | tf_op | source)
XLA Modules:
  0.0 67.3 jit_solution(10513889786539971524)
XLA Ops:
  0.0 1.2 %copy.15 = f32[1,1,2,256,256]{3,4,2,1,0:T(8,128)S(1)} copy(f32[1,1,2,256,256]{4,3,2,1,0:T(8,128)} %param.3) | data formatting | bytes 1048576 | tf_op args[0]
  1.5 1.5 %bitcast_dynamic-update-slice_fusion.5 = (f32[6,1,512,64]{2,3,0,1:T(8,128)S(1)}, f32[512,64]{0,1:T(8,128)}) fusion(f32[6,1,512,64]{2,3,0,1:T(8,128)S(1)} %broadcast_in_dim.93, s32[]{:T(128)S(6)} %select_n.127, f32[1,256,256]{1,2,0:T(8,128)S(1)} %get-tuple-element.28, f32[1,256,256]{1,2,0:T(8,128)S(1)} %get-tuple-element.27, f32[1,256,256]{1,2,0:T(8,128)S(1)} %fusion.40, ...), kind=kOutput, calls=%fused_computation.66 | convolution fusion | flops 202178560 | bytes 1179653 | tf_op jit(solution)/shard_map/mab,mbw->maw/dot_general | solution.py:56
  2.9 4.9 %collective-permute-start.6 = (f32[1,512,64]{1,2,0:T(8,128)}, f32[1,512,64]{1,2,0:T(8,128)S(1)}, u32[]{:S(2)}, u32[]{:S(2)}) collective-permute-start(f32[1,512,64]{1,2,0:T(8,128)} %bitcast.44), channel_id=1, source_target_pairs={{0,4},{4,8},{8,12},{1,5},{5,9},{9,13},{2,6},{6,10},{10,14},{3,7},{... | collective-permute-start | bytes 393224 | tf_op jit(solution)/shard_map/ppermute | solution.py:48
  8.2 1.8 %convolution_bitcast_fusion.7 = f32[1,64,512]{2,1,0:T(8,128)} fusion(f32[256,256]{1,0:T(8,128)S(1)} %bitcast.251, f32[256,256]{1,0:T(8,128)S(1)} %negate_bitcast_fusion, pred[]{:T(512)S(6)} %eq.16, f32[1,256,256]{1,2,0:T(8,128)S(1)} %get-tuple-element.28, f32[1,256,256]{1,2,0:T(8,128)S(1)} %fusion.40, f32[1,256,256]{1,2,0:T(8,128)S(1)} %get-tuple-element.27), kind=kOutput, calls=%fused_computation.12 | convolution fusion | flops 202178560 | bytes 1441793 | tf_op jit(solution)/shard_map/mwa,mab->mwb/dot_general | solution.py:67
  10.0 1.3 %collective-permute-start = (f32[1,64,512]{2,1,0:T(8,128)}, f32[1,64,512]{2,1,0:T(8,128)S(1)}, u32[]{:S(2)}, u32[]{:S(2)}) collective-permute-start(f32[1,64,512]{2,1,0:T(8,128)} %convolution_bitcast_fusion.7), channel_id=1, source_target_pairs={{4,0},{8,4},{12,8},{5,1},{9,5},{13,9},{6,2},{10,6},{14,10},{7,3},{... | collective-permute-start | bytes 393224 | tf_op jit(solution)/shard_map/ppermute | solution.py:49
  12.2 4.6 %collective-permute-start.7 = (f32[1,512,64]{1,2,0:T(8,128)S(1)}, f32[1,512,64]{1,2,0:T(8,128)S(1)}, u32[]{:S(2)}, u32[]{:S(2)}) collective-permute-start(f32[1,512,64]{1,2,0:T(8,128)S(1)} %bitcast.262), channel_id=1, source_target_pairs={{0,4},{4,8},{8,12},{1,5},{5,9},{9,13},{2,6},{6,10},{10,14},{3,7},{... | collective-permute-start | bytes 393224 | tf_op jit(solution)/shard_map/ppermute | solution.py:48
  17.1 1.1 %convolution_bitcast_fusion.6 = f32[1,64,512]{2,1,0:T(8,128)S(1)} fusion(f32[1,64,512]{2,1,0:T(8,128)S(1)} %get-tuple-element.16, f32[1,256,256]{1,2,0:T(8,128)S(1)} %get-tuple-element.28, f32[1,256,256]{1,2,0:T(8,128)S(1)} %fusion.40, f32[1,256,256]{1,2,0:T(8,128)S(1)} %get-tuple-element.27), kind=kOutput, calls=%fused_computation.11 | convolution fusion | flops 202113024 | bytes 1048576 | tf_op jit(solution)/shard_map/mwa,mab->mwb/dot_general | solution.py:67
  18.2 1.3 %collective-permute-start.1 = (f32[1,64,512]{2,1,0:T(8,128)S(1)}, f32[1,64,512]{2,1,0:T(8,128)S(1)}, u32[]{:S(2)}, u32[]{:S(2)}) collective-permute-start(f32[1,64,512]{2,1,0:T(8,128)S(1)} %convolution_bitcast_fusion.6), channel_id=1, source_target_pairs={{4,0},{8,4},{12,8},{5,1},{9,5},{13,9},{6,2},{10,6},{14,10},{7,3},{... | collective-permute-start | bytes 393224 | tf_op jit(solution)/shard_map/ppermute | solution.py:49
  20.3 4.6 %collective-permute-start.8 = (f32[1,512,64]{1,2,0:T(8,128)S(1)}, f32[1,512,64]{1,2,0:T(8,128)S(1)}, u32[]{:S(2)}, u32[]{:S(2)}) collective-permute-start(f32[1,512,64]{1,2,0:T(8,128)S(1)} %bitcast.261), channel_id=1, source_target_pairs={{0,4},{4,8},{8,12},{1,5},{5,9},{9,13},{2,6},{6,10},{10,14},{3,7},{... | collective-permute-start | bytes 393224 | tf_op jit(solution)/shard_map/ppermute | solution.py:48
  25.1 1.1 %convolution_bitcast_fusion.5 = f32[1,64,512]{2,1,0:T(8,128)S(1)} fusion(f32[1,64,512]{2,1,0:T(8,128)S(1)} %get-tuple-element.14, f32[1,256,256]{1,2,0:T(8,128)S(1)} %get-tuple-element.28, f32[1,256,256]{1,2,0:T(8,128)S(1)} %fusion.40, f32[1,256,256]{1,2,0:T(8,128)S(1)} %get-tuple-element.27), kind=kOutput, calls=%fused_computation.10 | convolution fusion | flops 202113024 | bytes 1048576 | tf_op jit(solution)/shard_map/mwa,mab->mwb/dot_general | solution.py:67
  26.2 1.3 %collective-permute-start.2 = (f32[1,64,512]{2,1,0:T(8,128)S(1)}, f32[1,64,512]{2,1,0:T(8,128)S(1)}, u32[]{:S(2)}, u32[]{:S(2)}) collective-permute-start(f32[1,64,512]{2,1,0:T(8,128)S(1)} %convolution_bitcast_fusion.5), channel_id=1, source_target_pairs={{4,0},{8,4},{12,8},{5,1},{9,5},{13,9},{6,2},{10,6},{14,10},{7,3},{... | collective-permute-start | bytes 393224 | tf_op jit(solution)/shard_map/ppermute | solution.py:49
  28.3 4.6 %collective-permute-start.9 = (f32[1,512,64]{1,2,0:T(8,128)S(1)}, f32[1,512,64]{1,2,0:T(8,128)S(1)}, u32[]{:S(2)}, u32[]{:S(2)}) collective-permute-start(f32[1,512,64]{1,2,0:T(8,128)S(1)} %bitcast.260), channel_id=1, source_target_pairs={{0,4},{4,8},{8,12},{1,5},{5,9},{9,13},{2,6},{6,10},{10,14},{3,7},{... | collective-permute-start | bytes 393224 | tf_op jit(solution)/shard_map/ppermute | solution.py:48
  33.1 1.1 %convolution_bitcast_fusion.4 = f32[1,64,512]{2,1,0:T(8,128)S(1)} fusion(f32[1,64,512]{2,1,0:T(8,128)S(1)} %get-tuple-element.12, f32[1,256,256]{1,2,0:T(8,128)S(1)} %get-tuple-element.28, f32[1,256,256]{1,2,0:T(8,128)S(1)} %fusion.40, f32[1,256,256]{1,2,0:T(8,128)S(1)} %get-tuple-element.27), kind=kOutput, calls=%fused_computation.9 | convolution fusion | flops 202113024 | bytes 1048576 | tf_op jit(solution)/shard_map/mwa,mab->mwb/dot_general | solution.py:67
  34.2 1.3 %collective-permute-start.3 = (f32[1,64,512]{2,1,0:T(8,128)S(1)}, f32[1,64,512]{2,1,0:T(8,128)S(1)}, u32[]{:S(2)}, u32[]{:S(2)}) collective-permute-start(f32[1,64,512]{2,1,0:T(8,128)S(1)} %convolution_bitcast_fusion.4), channel_id=1, source_target_pairs={{4,0},{8,4},{12,8},{5,1},{9,5},{13,9},{6,2},{10,6},{14,10},{7,3},{... | collective-permute-start | bytes 393224 | tf_op jit(solution)/shard_map/ppermute | solution.py:49
  36.3 4.6 %collective-permute-start.10 = (f32[1,512,64]{1,2,0:T(8,128)S(1)}, f32[1,512,64]{1,2,0:T(8,128)S(1)}, u32[]{:S(2)}, u32[]{:S(2)}) collective-permute-start(f32[1,512,64]{1,2,0:T(8,128)S(1)} %bitcast.263), channel_id=1, source_target_pairs={{0,4},{4,8},{8,12},{1,5},{5,9},{9,13},{2,6},{6,10},{10,14},{3,7},{... | collective-permute-start | bytes 393224 | tf_op jit(solution)/shard_map/ppermute | solution.py:48
  41.1 1.1 %convolution_bitcast_fusion.3 = f32[1,64,512]{2,1,0:T(8,128)S(1)} fusion(f32[1,64,512]{2,1,0:T(8,128)S(1)} %collective-permute-done.3, f32[1,256,256]{1,2,0:T(8,128)S(1)} %get-tuple-element.28, f32[1,256,256]{1,2,0:T(8,128)S(1)} %fusion.40, f32[1,256,256]{1,2,0:T(8,128)S(1)} %get-tuple-element.27), kind=kOutput, calls=%fused_computation.8 | convolution fusion | flops 202113024 | bytes 1048576 | tf_op jit(solution)/shard_map/mwa,mab->mwb/dot_general | solution.py:67
  42.2 1.3 %collective-permute-start.4 = (f32[1,64,512]{2,1,0:T(8,128)S(1)}, f32[1,64,512]{2,1,0:T(8,128)S(1)}, u32[]{:S(2)}, u32[]{:S(2)}) collective-permute-start(f32[1,64,512]{2,1,0:T(8,128)S(1)} %convolution_bitcast_fusion.3), channel_id=1, source_target_pairs={{4,0},{8,4},{12,8},{5,1},{9,5},{13,9},{6,2},{10,6},{14,10},{7,3},{... | collective-permute-start | bytes 393224 | tf_op jit(solution)/shard_map/ppermute | solution.py:49
  44.3 4.5 %collective-permute-start.11 = (f32[1,512,64]{1,2,0:T(8,128)S(1)}, f32[1,512,64]{1,2,0:T(8,128)S(1)}, u32[]{:S(2)}, u32[]{:S(2)}) collective-permute-start(f32[1,512,64]{1,2,0:T(8,128)S(1)} %bitcast.264), channel_id=1, source_target_pairs={{0,4},{4,8},{8,12},{1,5},{5,9},{9,13},{2,6},{6,10},{10,14},{3,7},{... | collective-permute-start | bytes 393224 | tf_op jit(solution)/shard_map/ppermute | solution.py:48
  49.0 1.1 %convolution_bitcast_fusion.2 = f32[1,64,512]{2,1,0:T(8,128)S(1)} fusion(f32[1,64,512]{2,1,0:T(8,128)S(1)} %collective-permute-done.4, f32[1,256,256]{1,2,0:T(8,128)S(1)} %get-tuple-element.28, f32[1,256,256]{1,2,0:T(8,128)S(1)} %fusion.40, f32[1,256,256]{1,2,0:T(8,128)S(1)} %get-tuple-element.27), kind=kOutput, calls=%fused_computation.7 | convolution fusion | flops 202113024 | bytes 1048576 | tf_op jit(solution)/shard_map/mwa,mab->mwb/dot_general | solution.py:67
  50.2 1.5 %collective-permute-start.5 = (f32[1,64,512]{2,1,0:T(8,128)S(1)}, f32[1,64,512]{2,1,0:T(8,128)S(1)}, u32[]{:S(2)}, u32[]{:S(2)}) collective-permute-start(f32[1,64,512]{2,1,0:T(8,128)S(1)} %convolution_bitcast_fusion.2), channel_id=1, source_target_pairs={{4,0},{8,4},{12,8},{5,1},{9,5},{13,9},{6,2},{10,6},{14,10},{7,3},{... | collective-permute-start | bytes 393224 | tf_op jit(solution)/shard_map/ppermute | solution.py:49
  52.9 4.2 %collective-permute-done.5 = f32[1,64,512]{2,1,0:T(8,128)S(1)} collective-permute-done((f32[1,64,512]{2,1,0:T(8,128)S(1)}, f32[1,64,512]{2,1,0:T(8,128)S(1)}, u32[]{:S(2)}, u32[]{:S(2)}) %collective-permute-start.5) | collective-permute-done | bytes 131104 | tf_op jit(solution)/shard_map/ppermute | solution.py:49
  57.4 1.0 %convolution_bitcast_fusion = f32[1,2,2,256,256]{3,4,1,2,0:T(8,128)S(1)} fusion(f32[4,64,2,256,1]{3,2,1,0,4:T(2,128)S(1)} %bitcast.259, f32[4,2,256,64]{2,1,3,0:T(2,128)S(1)} %reshape.278), kind=kOutput, calls=%fused_computation.4 | convolution fusion | flops 805306368 | bytes 2097152 | tf_op jit(solution)/shard_map/cmpaw,cmwqb->mpqab/dot_general | solution.py:71
  59.9 1.2 %subtract_bitcast_fusion = f32[1,4]{1,0:T(1,128)S(1)} fusion(f32[4]{0:T(128)S(1)} %get-tuple-element.6, f32[4]{0:T(128)S(1)} %get-tuple-element.5, f32[]{:T(128)} %get-tuple-element.9, f32[]{:T(128)} %get-tuple-element.17), kind=kLoop, calls=%fused_computation.96 | loop fusion | flops 12 | bytes 56 | tf_op jit(solution)/shard_map/sub | solution.py:81
  61.2 5.7 %psum.7 = f32[1,4]{1,0:T(1,128)S(1)} all-reduce(f32[1,4]{1,0:T(1,128)S(1)} %subtract_bitcast_fusion), channel_id=1, replica_groups=mesh['group'=2,'tm'=4,'member'=2,'sub'=2] {'member','sub'}, use_global_device_ids=true, to_apply=%region_4.5 | all-reduce | flops 4 | bytes 32 | tf_op jit(solution)/shard_map/psum | solution.py:83
  (46 shorter events, 9.2 us)
Async XLA Ops:
  1.3 6.6 %copy-start.1 = (f32[2,256,256]{2,1,0:T(8,128)S(1)}, f32[2,256,256]{2,1,0:T(8,128)}, u32[]{:S(2)}) copy-start(f32[2,256,256]{2,1,0:T(8,128)} %param.5) | copy-start | bytes 1572868
  2.9 8.5 %collective-permute-start.6 = (f32[1,512,64]{1,2,0:T(8,128)}, f32[1,512,64]{1,2,0:T(8,128)S(1)}, u32[]{:S(2)}, u32[]{:S(2)}) collective-permute-start(f32[1,512,64]{1,2,0:T(8,128)} %bitcast.44), channel_id=1, source_target_pairs={{0,4},{4,8},{8,12},{1,5},{5,9},{9,13},{2,6},{6,10},{10,14},{3,7},{... | collective-permute-start | bytes 393224 | tf_op jit(solution)/shard_map/ppermute | solution.py:48
  10.0 7.1 %collective-permute-start = (f32[1,64,512]{2,1,0:T(8,128)}, f32[1,64,512]{2,1,0:T(8,128)S(1)}, u32[]{:S(2)}, u32[]{:S(2)}) collective-permute-start(f32[1,64,512]{2,1,0:T(8,128)} %convolution_bitcast_fusion.7), channel_id=1, source_target_pairs={{4,0},{8,4},{12,8},{5,1},{9,5},{13,9},{6,2},{10,6},{14,10},{7,3},{... | collective-permute-start | bytes 393224 | tf_op jit(solution)/shard_map/ppermute | solution.py:49
  12.2 7.3 %collective-permute-start.7 = (f32[1,512,64]{1,2,0:T(8,128)S(1)}, f32[1,512,64]{1,2,0:T(8,128)S(1)}, u32[]{:S(2)}, u32[]{:S(2)}) collective-permute-start(f32[1,512,64]{1,2,0:T(8,128)S(1)} %bitcast.262), channel_id=1, source_target_pairs={{0,4},{4,8},{8,12},{1,5},{5,9},{9,13},{2,6},{6,10},{10,14},{3,7},{... | collective-permute-start | bytes 393224 | tf_op jit(solution)/shard_map/ppermute | solution.py:48
  18.2 6.9 %collective-permute-start.1 = (f32[1,64,512]{2,1,0:T(8,128)S(1)}, f32[1,64,512]{2,1,0:T(8,128)S(1)}, u32[]{:S(2)}, u32[]{:S(2)}) collective-permute-start(f32[1,64,512]{2,1,0:T(8,128)S(1)} %convolution_bitcast_fusion.6), channel_id=1, source_target_pairs={{4,0},{8,4},{12,8},{5,1},{9,5},{13,9},{6,2},{10,6},{14,10},{7,3},{... | collective-permute-start | bytes 393224 | tf_op jit(solution)/shard_map/ppermute | solution.py:49
  20.3 7.2 %collective-permute-start.8 = (f32[1,512,64]{1,2,0:T(8,128)S(1)}, f32[1,512,64]{1,2,0:T(8,128)S(1)}, u32[]{:S(2)}, u32[]{:S(2)}) collective-permute-start(f32[1,512,64]{1,2,0:T(8,128)S(1)} %bitcast.261), channel_id=1, source_target_pairs={{0,4},{4,8},{8,12},{1,5},{5,9},{9,13},{2,6},{6,10},{10,14},{3,7},{... | collective-permute-start | bytes 393224 | tf_op jit(solution)/shard_map/ppermute | solution.py:48
  26.2 6.9 %collective-permute-start.2 = (f32[1,64,512]{2,1,0:T(8,128)S(1)}, f32[1,64,512]{2,1,0:T(8,128)S(1)}, u32[]{:S(2)}, u32[]{:S(2)}) collective-permute-start(f32[1,64,512]{2,1,0:T(8,128)S(1)} %convolution_bitcast_fusion.5), channel_id=1, source_target_pairs={{4,0},{8,4},{12,8},{5,1},{9,5},{13,9},{6,2},{10,6},{14,10},{7,3},{... | collective-permute-start | bytes 393224 | tf_op jit(solution)/shard_map/ppermute | solution.py:49
  28.3 7.2 %collective-permute-start.9 = (f32[1,512,64]{1,2,0:T(8,128)S(1)}, f32[1,512,64]{1,2,0:T(8,128)S(1)}, u32[]{:S(2)}, u32[]{:S(2)}) collective-permute-start(f32[1,512,64]{1,2,0:T(8,128)S(1)} %bitcast.260), channel_id=1, source_target_pairs={{0,4},{4,8},{8,12},{1,5},{5,9},{9,13},{2,6},{6,10},{10,14},{3,7},{... | collective-permute-start | bytes 393224 | tf_op jit(solution)/shard_map/ppermute | solution.py:48
  34.2 6.9 %collective-permute-start.3 = (f32[1,64,512]{2,1,0:T(8,128)S(1)}, f32[1,64,512]{2,1,0:T(8,128)S(1)}, u32[]{:S(2)}, u32[]{:S(2)}) collective-permute-start(f32[1,64,512]{2,1,0:T(8,128)S(1)} %convolution_bitcast_fusion.4), channel_id=1, source_target_pairs={{4,0},{8,4},{12,8},{5,1},{9,5},{13,9},{6,2},{10,6},{14,10},{7,3},{... | collective-permute-start | bytes 393224 | tf_op jit(solution)/shard_map/ppermute | solution.py:49
  36.3 7.2 %collective-permute-start.10 = (f32[1,512,64]{1,2,0:T(8,128)S(1)}, f32[1,512,64]{1,2,0:T(8,128)S(1)}, u32[]{:S(2)}, u32[]{:S(2)}) collective-permute-start(f32[1,512,64]{1,2,0:T(8,128)S(1)} %bitcast.263), channel_id=1, source_target_pairs={{0,4},{4,8},{8,12},{1,5},{5,9},{9,13},{2,6},{6,10},{10,14},{3,7},{... | collective-permute-start | bytes 393224 | tf_op jit(solution)/shard_map/ppermute | solution.py:48
  42.2 6.9 %collective-permute-start.4 = (f32[1,64,512]{2,1,0:T(8,128)S(1)}, f32[1,64,512]{2,1,0:T(8,128)S(1)}, u32[]{:S(2)}, u32[]{:S(2)}) collective-permute-start(f32[1,64,512]{2,1,0:T(8,128)S(1)} %convolution_bitcast_fusion.3), channel_id=1, source_target_pairs={{4,0},{8,4},{12,8},{5,1},{9,5},{13,9},{6,2},{10,6},{14,10},{7,3},{... | collective-permute-start | bytes 393224 | tf_op jit(solution)/shard_map/ppermute | solution.py:49
  44.3 7.4 %collective-permute-start.11 = (f32[1,512,64]{1,2,0:T(8,128)S(1)}, f32[1,512,64]{1,2,0:T(8,128)S(1)}, u32[]{:S(2)}, u32[]{:S(2)}) collective-permute-start(f32[1,512,64]{1,2,0:T(8,128)S(1)} %bitcast.264), channel_id=1, source_target_pairs={{0,4},{4,8},{8,12},{1,5},{5,9},{9,13},{2,6},{6,10},{10,14},{3,7},{... | collective-permute-start | bytes 393224 | tf_op jit(solution)/shard_map/ppermute | solution.py:48
  50.2 6.9 %collective-permute-start.5 = (f32[1,64,512]{2,1,0:T(8,128)S(1)}, f32[1,64,512]{2,1,0:T(8,128)S(1)}, u32[]{:S(2)}, u32[]{:S(2)}) collective-permute-start(f32[1,64,512]{2,1,0:T(8,128)S(1)} %convolution_bitcast_fusion.2), channel_id=1, source_target_pairs={{4,0},{8,4},{12,8},{5,1},{9,5},{13,9},{6,2},{10,6},{14,10},{7,3},{... | collective-permute-start | bytes 393224 | tf_op jit(solution)/shard_map/ppermute | solution.py:49
  57.4 2.0 %copy-start = (f32[4,2,256,256]{3,2,1,0:T(8,128)S(1)}, f32[4,2,256,256]{3,2,1,0:T(8,128)}, u32[]{:S(2)}) copy-start(f32[4,2,256,256]{3,2,1,0:T(8,128)} %param.4) | copy-start | bytes 6291460

commit v2 on v1

--- a/solution.py
+++ b/solution.py
@@ -3,7 +3,7 @@
 from jax import lax
 from jax.sharding import PartitionSpec as P
 
-HIGH = lax.Precision.HIGHEST
+HIGH = lax.Precision.HIGH
 CHUNKS = 4
 
 
@@ -17,6 +17,20 @@
     top = jnp.concatenate([u[:, 0], u[:, 1]], axis=-1)
     bottom = jnp.concatenate([-u[:, 1], u[:, 0]], axis=-1)
     return jnp.concatenate([top, bottom], axis=-2)
+
+
+def butterfly_sum(value, axes):
+    for axis in axes:
+        size = lax.axis_size(axis)
+        if size & (size - 1):
+            value = lax.psum(value, axis)
+            continue
+        distance = 1
+        while distance < size:
+            pairs = [(i, i ^ distance) for i in range(size)]
+            value = value + lax.ppermute(value, axis, pairs)
+            distance *= 2
+    return value
 
 
 def per_device(slices, controls, target):
@@ -51,10 +65,13 @@
             cols = slice(step * width, (step + 1) * width)
             own_cols = jnp.concatenate([unit[:, 0, :, cols], unit[:, 1, :, cols]], axis=-2)
             rows = jnp.broadcast_to(target_dag[None, step * width:(step + 1) * width], bwd_in.shape)
-            fwd_new = jnp.where(
-                is_first, own_cols,
-                jnp.einsum("mab,mbw->maw", left_op, fwd_in, precision=HIGH),
-            )
+            if step == 0:
+                fwd_new = own_cols
+            else:
+                fwd_new = jnp.where(
+                    is_first, own_cols,
+                    jnp.einsum("mab,mbw->maw", left_op, fwd_in, precision=HIGH),
+                )
             bwd_in = jnp.where(is_last, rows, bwd_in)
         else:
             fwd_new = jnp.einsum("mab,mbw->maw", left_op, fwd_in, precision=HIGH)
@@ -80,7 +97,7 @@
     s_im = jnp.sum(q_im[:, None] * h_re - q_re[:, None] * h_im, axis=(-2, -1))
     terms = over_re[:, None] * s_im - over_im[:, None] * s_re
     partial_value = jnp.sum(terms, axis=0, keepdims=True)
-    total = lax.psum(partial_value, ("member", "sub"))
+    total = butterfly_sum(partial_value, ("sub", "member"))
     member_count = members_here * lax.axis_size("member") * lax.axis_size("sub")
     return total * (2.0 / member_count)
 

time: 67.8 us -> 63.2 us (0.932)
  matrix products: 14.6 us -> 8.36 us
  waiting for transfers between devices: 5.2 us -> 10.9 us
  blocking collectives: 5.67 us -> 0 us
  starting transfers between devices: 35.6 us -> 37.1 us
    psum x1 -> x0, blocking collectives: 5.67 us -> none  [per_device(): total = lax.psum(partial_value, ('member', 'sub'))]
    ppermute x0 -> x2, waiting for transfers between devices: none -> 3.16 us  [butterfly_sum(): value = value + lax.ppermute(value, axis, pairs)]
    dot_general x6, matrix products: 7.37 us -> 4.29 us  [per_device(): bwd_out = jnp.einsum('mwa,mab->mwb', bwd_in, right_op, precision=HIGH)]
    dot_general x4 -> x3, matrix products: 3.83 us -> 2.18 us  [per_device(): jnp.einsum('mab,mbw->maw', left_op, fwd_in, precision=HIGH)]
    ppermute x0 -> x2, starting transfers between devices: none -> 1.56 us  [butterfly_sum(): value = value + lax.ppermute(value, axis, pairs)]
    ppermute x6, waiting for transfers between devices: 5.19 us -> 6.61 us  [per_device(): bwd_in = lax.ppermute(bwd_out, 'tm', left_pairs)]
    dot_general x3, matrix products: 2.39 us -> 1.27 us  [per_device(): fwd_new = jnp.einsum('mab,mbw->maw', left_op, fwd_in, precision=HIGH)]
    ppermute x6, waiting for transfers between devices: 0.02 us -> 1.09 us  [per_device(): fwd_in = lax.ppermute(fwd_out, 'tm', right_pairs)]
  transfers between devices with their start and end apart: 12 -> 14, of which waited for: 6 -> 10; matrix products, arithmetic and copies ran while one was open for 19% -> 14% of each run, Pallas kernels for 0% -> 0%
where the time goes in v2:
time: 63.2 us; the launch traced here: 62.7 us
  starting transfers between devices  37.1 us (59%)
  waiting for transfers between devices  10.9 us (17%)
  matrix products  8.36 us (13%)
  other arithmetic  3.03 us (5%)
  local copies, waits for them, and re-layouts  2.92 us (5%)
    ppermute x6, starting transfers between devices, per_device(): fwd_in = lax.ppermute(fwd_out, 'tm', right_pairs)  27.8 us
    ppermute x6, starting transfers between devices, per_device(): bwd_in = lax.ppermute(bwd_out, 'tm', left_pairs)  7.72 us
    ppermute x6, waiting for transfers between devices, per_device(): bwd_in = lax.ppermute(bwd_out, 'tm', left_pairs)  6.61 us
    dot_general x6, matrix products, per_device(): bwd_out = jnp.einsum('mwa,mab->mwb', bwd_in, right_op, precision=HIGH)  4.29 us
    ppermute x2, waiting for transfers between devices, butterfly_sum(): value = value + lax.ppermute(value, axis, pairs)  3.16 us
    dot_general x3, matrix products, per_device(): jnp.einsum('mab,mbw->maw', left_op, fwd_in, precision=HIGH)  2.18 us
    unnamed x7, local copies, waits for them, and re-layouts  1.6 us
    ppermute x2, starting transfers between devices, butterfly_sum(): value = value + lax.ppermute(value, axis, pairs)  1.56 us
  transfers between devices with their start and end apart: 14, of which 10 were waited for; matrix products, arithmetic and copies ran while one was open for 14% of the time, Pallas kernels for 0%

profile of v2, /device:TPU:0, one launch (start us, length us, event | category | flops | bytes accessed | tf_op | source)
XLA Modules:
  0.0 62.7 jit_solution(12851771476950213094)
XLA Ops:
  0.0 1.3 %copy.15 = f32[1,1,2,256,256]{3,4,2,1,0:T(8,128)S(1)} copy(f32[1,1,2,256,256]{4,3,2,1,0:T(8,128)} %param.3) | data formatting | bytes 1048576 | tf_op args[0]
  1.4 5.6 %collective-permute-start.6 = (f32[1,512,64]{1,2,0:T(8,128)S(1)}, f32[1,512,64]{1,2,0:T(8,128)}, u32[]{:S(2)}, u32[]{:S(2)}) collective-permute-start(f32[1,512,64]{1,2,0:T(8,128)S(1)} %pad_maximum_fusion.5), channel_id=1, source_target_pairs={{0,4},{4,8},{8,12},{1,5},{5,9},{9,13},{2,6},{6,10},{10,14},{3,7},{... | collective-permute-start | bytes 393224 | tf_op jit(solution)/shard_map/ppermute | solution.py:62
  7.4 1.3 %convolution_bitcast_fusion.7 = f32[1,64,512]{2,1,0:T(8,128)} fusion(f32[256,256]{1,0:T(8,128)S(1)} %bitcast.247, f32[256,256]{1,0:T(8,128)S(1)} %negate_bitcast_fusion, pred[]{:T(512)S(6)} %eq.16, f32[1,256,256]{1,2,0:T(8,128)S(1)} %get-tuple-element.28, f32[1,256,256]{1,2,0:T(8,128)S(1)} %fusion.38, f32[1,256,256]{1,2,0:T(8,128)S(1)} %get-tuple-element.27), kind=kOutput, calls=%fused_computation.12 | convolution fusion | flops 101515264 | bytes 1441793 | tf_op jit(solution)/shard_map/mwa,mab->mwb/dot_general | solution.py:84
  8.6 1.3 %collective-permute-start = (f32[1,64,512]{2,1,0:T(8,128)}, f32[1,64,512]{2,1,0:T(8,128)S(1)}, u32[]{:S(2)}, u32[]{:S(2)}) collective-permute-start(f32[1,64,512]{2,1,0:T(8,128)} %convolution_bitcast_fusion.7), channel_id=1, source_target_pairs={{4,0},{8,4},{12,8},{5,1},{9,5},{13,9},{6,2},{10,6},{14,10},{7,3},{... | collective-permute-start | bytes 393224 | tf_op jit(solution)/shard_map/ppermute | solution.py:63
  10.2 1.3 %bitcast_dynamic-update-slice_fusion.4 = (f32[6,1,512,64]{2,3,0,1:T(8,128)S(1)}, f32[512,64]{0,1:T(8,128)S(1)}) fusion(f32[6,1,512,64]{2,3,0,1:T(8,128)S(1)} %bitcast_dynamic-update-slice_fusion.5, s32[]{:T(128)S(6)} %select_n.121, f32[1,512,64]{1,2,0:T(8,128)} %collective-permute-done.6, f32[1,256,256]{1,2,0:T(8,128)S(1)} %get-tuple-element.28, ...), kind=kOutput, calls=%fused_computation.65 | convolution fusion | flops 101515264 | bytes 1310725 | tf_op jit(solution)/shard_map/mab,mbw->maw/dot_general | solution.py:73
  11.5 4.6 %collective-permute-start.7 = (f32[1,512,64]{1,2,0:T(8,128)S(1)}, f32[1,512,64]{1,2,0:T(8,128)S(1)}, u32[]{:S(2)}, u32[]{:S(2)}) collective-permute-start(f32[1,512,64]{1,2,0:T(8,128)S(1)} %bitcast.258), channel_id=1, source_target_pairs={{0,4},{4,8},{8,12},{1,5},{5,9},{9,13},{2,6},{6,10},{10,14},{3,7},{... | collective-permute-start | bytes 393224 | tf_op jit(solution)/shard_map/ppermute | solution.py:62
  16.8 1.3 %collective-permute-start.1 = (f32[1,64,512]{2,1,0:T(8,128)S(1)}, f32[1,64,512]{2,1,0:T(8,128)S(1)}, u32[]{:S(2)}, u32[]{:S(2)}) collective-permute-start(f32[1,64,512]{2,1,0:T(8,128)S(1)} %convolution_bitcast_fusion.6), channel_id=1, source_target_pairs={{4,0},{8,4},{12,8},{5,1},{9,5},{13,9},{6,2},{10,6},{14,10},{7,3},{... | collective-permute-start | bytes 393224 | tf_op jit(solution)/shard_map/ppermute | solution.py:63
  19.0 4.4 %collective-permute-start.8 = (f32[1,512,64]{1,2,0:T(8,128)S(1)}, f32[1,512,64]{1,2,0:T(8,128)S(1)}, u32[]{:S(2)}, u32[]{:S(2)}) collective-permute-start(f32[1,512,64]{1,2,0:T(8,128)S(1)} %bitcast.257), channel_id=1, source_target_pairs={{0,4},{4,8},{8,12},{1,5},{5,9},{9,13},{2,6},{6,10},{10,14},{3,7},{... | collective-permute-start | bytes 393224 | tf_op jit(solution)/shard_map/ppermute | solution.py:62
  23.6 0.6 convolution_bitcast_fusion.5
  24.3 1.3 %collective-permute-start.2 = (f32[1,64,512]{2,1,0:T(8,128)S(1)}, f32[1,64,512]{2,1,0:T(8,128)S(1)}, u32[]{:S(2)}, u32[]{:S(2)}) collective-permute-start(f32[1,64,512]{2,1,0:T(8,128)S(1)} %convolution_bitcast_fusion.5), channel_id=1, source_target_pairs={{4,0},{8,4},{12,8},{5,1},{9,5},{13,9},{6,2},{10,6},{14,10},{7,3},{... | collective-permute-start | bytes 393224 | tf_op jit(solution)/shard_map/ppermute | solution.py:63
  26.3 4.4 %collective-permute-start.9 = (f32[1,512,64]{1,2,0:T(8,128)S(1)}, f32[1,512,64]{1,2,0:T(8,128)S(1)}, u32[]{:S(2)}, u32[]{:S(2)}) collective-permute-start(f32[1,512,64]{1,2,0:T(8,128)S(1)} %bitcast.256), channel_id=1, source_target_pairs={{0,4},{4,8},{8,12},{1,5},{5,9},{9,13},{2,6},{6,10},{10,14},{3,7},{... | collective-permute-start | bytes 393224 | tf_op jit(solution)/shard_map/ppermute | solution.py:62
  31.7 1.3 %collective-permute-start.3 = (f32[1,64,512]{2,1,0:T(8,128)S(1)}, f32[1,64,512]{2,1,0:T(8,128)S(1)}, u32[]{:S(2)}, u32[]{:S(2)}) collective-permute-start(f32[1,64,512]{2,1,0:T(8,128)S(1)} %convolution_bitcast_fusion.4), channel_id=1, source_target_pairs={{4,0},{8,4},{12,8},{5,1},{9,5},{13,9},{6,2},{10,6},{14,10},{7,3},{... | collective-permute-start | bytes 393224 | tf_op jit(solution)/shard_map/ppermute | solution.py:63
  33.6 4.4 %collective-permute-start.10 = (f32[1,512,64]{1,2,0:T(8,128)S(1)}, f32[1,512,64]{1,2,0:T(8,128)S(1)}, u32[]{:S(2)}, u32[]{:S(2)}) collective-permute-start(f32[1,512,64]{1,2,0:T(8,128)S(1)} %bitcast.259), channel_id=1, source_target_pairs={{0,4},{4,8},{8,12},{1,5},{5,9},{9,13},{2,6},{6,10},{10,14},{3,7},{... | collective-permute-start | bytes 393224 | tf_op jit(solution)/shard_map/ppermute | solution.py:62
  39.2 1.3 %collective-permute-start.4 = (f32[1,64,512]{2,1,0:T(8,128)S(1)}, f32[1,64,512]{2,1,0:T(8,128)S(1)}, u32[]{:S(2)}, u32[]{:S(2)}) collective-permute-start(f32[1,64,512]{2,1,0:T(8,128)S(1)} %convolution_bitcast_fusion.3), channel_id=1, source_target_pairs={{4,0},{8,4},{12,8},{5,1},{9,5},{13,9},{6,2},{10,6},{14,10},{7,3},{... | collective-permute-start | bytes 393224 | tf_op jit(solution)/shard_map/ppermute | solution.py:63
  41.0 4.6 %collective-permute-start.11 = (f32[1,512,64]{1,2,0:T(8,128)S(1)}, f32[1,512,64]{1,2,0:T(8,128)S(1)}, u32[]{:S(2)}, u32[]{:S(2)}) collective-permute-start(f32[1,512,64]{1,2,0:T(8,128)S(1)} %bitcast.260), channel_id=1, source_target_pairs={{0,4},{4,8},{8,12},{1,5},{5,9},{9,13},{2,6},{6,10},{10,14},{3,7},{... | collective-permute-start | bytes 393224 | tf_op jit(solution)/shard_map/ppermute | solution.py:62
  45.5 0.7 %collective-permute-done.4 = f32[1,64,512]{2,1,0:T(8,128)S(1)} collective-permute-done((f32[1,64,512]{2,1,0:T(8,128)S(1)}, f32[1,64,512]{2,1,0:T(8,128)S(1)}, u32[]{:S(2)}, u32[]{:S(2)}) %collective-permute-start.4) | collective-permute-done | bytes 131104 | tf_op jit(solution)/shard_map/ppermute | solution.py:63
  46.9 1.3 %collective-permute-start.5 = (f32[1,64,512]{2,1,0:T(8,128)S(1)}, f32[1,64,512]{2,1,0:T(8,128)S(1)}, u32[]{:S(2)}, u32[]{:S(2)}) collective-permute-start(f32[1,64,512]{2,1,0:T(8,128)S(1)} %convolution_bitcast_fusion.2), channel_id=1, source_target_pairs={{4,0},{8,4},{12,8},{5,1},{9,5},{13,9},{6,2},{10,6},{14,10},{7,3},{... | collective-permute-start | bytes 393224 | tf_op jit(solution)/shard_map/ppermute | solution.py:63
  49.0 4.7 %collective-permute-done.5 = f32[1,64,512]{2,1,0:T(8,128)S(1)} collective-permute-done((f32[1,64,512]{2,1,0:T(8,128)S(1)}, f32[1,64,512]{2,1,0:T(8,128)S(1)}, u32[]{:S(2)}, u32[]{:S(2)}) %collective-permute-start.5) | collective-permute-done | bytes 131104 | tf_op jit(solution)/shard_map/ppermute | solution.py:63
  54.2 0.6 convolution_bitcast_fusion
  54.8 0.6 %select_reduce_fusion = (f32[]{:T(128)}, f32[256,256]{0,1:T(8,128)S(1)}, f32[]{:T(128)}, f32[256,256]{0,1:T(8,128)S(1)}) fusion(f32[1,2,2,256,256]{3,4,1,2,0:T(8,128)S(1)} %convolution_bitcast_fusion), kind=kLoop, calls=%fused_computation.45 | loop fusion | flops 458750 | bytes 1572872 | tf_op jit(solution)/shard_map/reduce_sum | solution.py:93
  56.3 1.2 %subtract_bitcast_fusion = f32[1,4]{1,0:T(1,128)S(1)} fusion(f32[4]{0:T(128)S(1)} %get-tuple-element.6, f32[4]{0:T(128)S(1)} %get-tuple-element.5, f32[]{:T(128)} %get-tuple-element.9, f32[]{:T(128)} %get-tuple-element.17), kind=kLoop, calls=%fused_computation.96 | loop fusion | flops 12 | bytes 56 | tf_op jit(solution)/shard_map/sub | solution.py:98
  57.5 1.1 %collective-permute-done.12 = f32[1,4]{1,0:T(1,128)S(1)} collective-permute-done((f32[1,4]{1,0:T(1,128)S(1)}, f32[1,4]{1,0:T(1,128)S(1)}, u32[]{:S(2)}, u32[]{:S(2)}) %collective-permute-start.12) | collective-permute-done | bytes 48 | tf_op jit(solution)/shard_map/ppermute | solution.py:31
  58.6 1.5 %collective-permute-start.13 = (f32[1,4]{1,0:T(1,128)S(1)}, f32[1,4]{1,0:T(1,128)S(1)}, u32[]{:S(2)}, u32[]{:S(2)}) collective-permute-start(f32[1,4]{1,0:T(1,128)S(1)} %add.176), channel_id=1, source_target_pairs={{0,2},{2,0},{1,3},{3,1},{4,6},{6,4},{5,7},{7,5},{8,10},{10,8},{9,1... | collective-permute-start | bytes 56 | tf_op jit(solution)/shard_map/ppermute | solution.py:31
  60.1 2.0 %collective-permute-done.13 = f32[1,4]{1,0:T(1,128)S(1)} collective-permute-done((f32[1,4]{1,0:T(1,128)S(1)}, f32[1,4]{1,0:T(1,128)S(1)}, u32[]{:S(2)}, u32[]{:S(2)}) %collective-permute-start.13) | collective-permute-done | bytes 48 | tf_op jit(solution)/shard_map/ppermute | solution.py:31
  (51 shorter events, 9.7 us)
Async XLA Ops:
  0.0 7.0 %copy-start.1 = (f32[2,256,256]{2,1,0:T(8,128)S(1)}, f32[2,256,256]{2,1,0:T(8,128)}, u32[]{:S(2)}) copy-start(f32[2,256,256]{2,1,0:T(8,128)} %param.5) | copy-start | bytes 1572868
  1.4 8.8 %collective-permute-start.6 = (f32[1,512,64]{1,2,0:T(8,128)S(1)}, f32[1,512,64]{1,2,0:T(8,128)}, u32[]{:S(2)}, u32[]{:S(2)}) collective-permute-start(f32[1,512,64]{1,2,0:T(8,128)S(1)} %pad_maximum_fusion.5), channel_id=1, source_target_pairs={{0,4},{4,8},{8,12},{1,5},{5,9},{9,13},{2,6},{6,10},{10,14},{3,7},{... | collective-permute-start | bytes 393224 | tf_op jit(solution)/shard_map/ppermute | solution.py:62
  8.6 7.5 %collective-permute-start = (f32[1,64,512]{2,1,0:T(8,128)}, f32[1,64,512]{2,1,0:T(8,128)S(1)}, u32[]{:S(2)}, u32[]{:S(2)}) collective-permute-start(f32[1,64,512]{2,1,0:T(8,128)} %convolution_bitcast_fusion.7), channel_id=1, source_target_pairs={{4,0},{8,4},{12,8},{5,1},{9,5},{13,9},{6,2},{10,6},{14,10},{7,3},{... | collective-permute-start | bytes 393224 | tf_op jit(solution)/shard_map/ppermute | solution.py:63
  11.5 7.1 %collective-permute-start.7 = (f32[1,512,64]{1,2,0:T(8,128)S(1)}, f32[1,512,64]{1,2,0:T(8,128)S(1)}, u32[]{:S(2)}, u32[]{:S(2)}) collective-permute-start(f32[1,512,64]{1,2,0:T(8,128)S(1)} %bitcast.258), channel_id=1, source_target_pairs={{0,4},{4,8},{8,12},{1,5},{5,9},{9,13},{2,6},{6,10},{10,14},{3,7},{... | collective-permute-start | bytes 393224 | tf_op jit(solution)/shard_map/ppermute | solution.py:62
  16.8 6.9 %collective-permute-start.1 = (f32[1,64,512]{2,1,0:T(8,128)S(1)}, f32[1,64,512]{2,1,0:T(8,128)S(1)}, u32[]{:S(2)}, u32[]{:S(2)}) collective-permute-start(f32[1,64,512]{2,1,0:T(8,128)S(1)} %convolution_bitcast_fusion.6), channel_id=1, source_target_pairs={{4,0},{8,4},{12,8},{5,1},{9,5},{13,9},{6,2},{10,6},{14,10},{7,3},{... | collective-permute-start | bytes 393224 | tf_op jit(solution)/shard_map/ppermute | solution.py:63
  19.0 6.9 %collective-permute-start.8 = (f32[1,512,64]{1,2,0:T(8,128)S(1)}, f32[1,512,64]{1,2,0:T(8,128)S(1)}, u32[]{:S(2)}, u32[]{:S(2)}) collective-permute-start(f32[1,512,64]{1,2,0:T(8,128)S(1)} %bitcast.257), channel_id=1, source_target_pairs={{0,4},{4,8},{8,12},{1,5},{5,9},{9,13},{2,6},{6,10},{10,14},{3,7},{... | collective-permute-start | bytes 393224 | tf_op jit(solution)/shard_map/ppermute | solution.py:62
  24.3 6.9 %collective-permute-start.2 = (f32[1,64,512]{2,1,0:T(8,128)S(1)}, f32[1,64,512]{2,1,0:T(8,128)S(1)}, u32[]{:S(2)}, u32[]{:S(2)}) collective-permute-start(f32[1,64,512]{2,1,0:T(8,128)S(1)} %convolution_bitcast_fusion.5), channel_id=1, source_target_pairs={{4,0},{8,4},{12,8},{5,1},{9,5},{13,9},{6,2},{10,6},{14,10},{7,3},{... | collective-permute-start | bytes 393224 | tf_op jit(solution)/shard_map/ppermute | solution.py:63
  26.3 6.9 %collective-permute-start.9 = (f32[1,512,64]{1,2,0:T(8,128)S(1)}, f32[1,512,64]{1,2,0:T(8,128)S(1)}, u32[]{:S(2)}, u32[]{:S(2)}) collective-permute-start(f32[1,512,64]{1,2,0:T(8,128)S(1)} %bitcast.256), channel_id=1, source_target_pairs={{0,4},{4,8},{8,12},{1,5},{5,9},{9,13},{2,6},{6,10},{10,14},{3,7},{... | collective-permute-start | bytes 393224 | tf_op jit(solution)/shard_map/ppermute | solution.py:62
  31.7 6.9 %collective-permute-start.3 = (f32[1,64,512]{2,1,0:T(8,128)S(1)}, f32[1,64,512]{2,1,0:T(8,128)S(1)}, u32[]{:S(2)}, u32[]{:S(2)}) collective-permute-start(f32[1,64,512]{2,1,0:T(8,128)S(1)} %convolution_bitcast_fusion.4), channel_id=1, source_target_pairs={{4,0},{8,4},{12,8},{5,1},{9,5},{13,9},{6,2},{10,6},{14,10},{7,3},{... | collective-permute-start | bytes 393224 | tf_op jit(solution)/shard_map/ppermute | solution.py:63
  33.6 6.9 %collective-permute-start.10 = (f32[1,512,64]{1,2,0:T(8,128)S(1)}, f32[1,512,64]{1,2,0:T(8,128)S(1)}, u32[]{:S(2)}, u32[]{:S(2)}) collective-permute-start(f32[1,512,64]{1,2,0:T(8,128)S(1)} %bitcast.259), channel_id=1, source_target_pairs={{0,4},{4,8},{8,12},{1,5},{5,9},{9,13},{2,6},{6,10},{10,14},{3,7},{... | collective-permute-start | bytes 393224 | tf_op jit(solution)/shard_map/ppermute | solution.py:62
  39.2 7.1 %collective-permute-start.4 = (f32[1,64,512]{2,1,0:T(8,128)S(1)}, f32[1,64,512]{2,1,0:T(8,128)S(1)}, u32[]{:S(2)}, u32[]{:S(2)}) collective-permute-start(f32[1,64,512]{2,1,0:T(8,128)S(1)} %convolution_bitcast_fusion.3), channel_id=1, source_target_pairs={{4,0},{8,4},{12,8},{5,1},{9,5},{13,9},{6,2},{10,6},{14,10},{7,3},{... | collective-permute-start | bytes 393224 | tf_op jit(solution)/shard_map/ppermute | solution.py:63
  41.0 7.2 %collective-permute-start.11 = (f32[1,512,64]{1,2,0:T(8,128)S(1)}, f32[1,512,64]{1,2,0:T(8,128)S(1)}, u32[]{:S(2)}, u32[]{:S(2)}) collective-permute-start(f32[1,512,64]{1,2,0:T(8,128)S(1)} %bitcast.260), channel_id=1, source_target_pairs={{0,4},{4,8},{8,12},{1,5},{5,9},{9,13},{2,6},{6,10},{10,14},{3,7},{... | collective-permute-start | bytes 393224 | tf_op jit(solution)/shard_map/ppermute | solution.py:62
  46.9 6.9 %collective-permute-start.5 = (f32[1,64,512]{2,1,0:T(8,128)S(1)}, f32[1,64,512]{2,1,0:T(8,128)S(1)}, u32[]{:S(2)}, u32[]{:S(2)}) collective-permute-start(f32[1,64,512]{2,1,0:T(8,128)S(1)} %convolution_bitcast_fusion.2), channel_id=1, source_target_pairs={{4,0},{8,4},{12,8},{5,1},{9,5},{13,9},{6,2},{10,6},{14,10},{7,3},{... | collective-permute-start | bytes 393224 | tf_op jit(solution)/shard_map/ppermute | solution.py:63
  54.1 1.6 %copy-start = (f32[4,2,256,256]{3,2,1,0:T(8,128)S(1)}, f32[4,2,256,256]{3,2,1,0:T(8,128)}, u32[]{:S(2)}) copy-start(f32[4,2,256,256]{3,2,1,0:T(8,128)} %param.4) | copy-start | bytes 6291460
  57.5 1.2 %collective-permute-start.12 = (f32[1,4]{1,0:T(1,128)S(1)}, f32[1,4]{1,0:T(1,128)S(1)}, u32[]{:S(2)}, u32[]{:S(2)}) collective-permute-start(f32[1,4]{1,0:T(1,128)S(1)} %subtract_bitcast_fusion), channel_id=1, source_target_pairs={{0,1},{1,0},{2,3},{3,2},{4,5},{5,4},{6,7},{7,6},{8,9},{9,8},{10,11... | collective-permute-start | bytes 56 | tf_op jit(solution)/shard_map/ppermute | solution.py:31
  58.6 3.5 %collective-permute-start.13 = (f32[1,4]{1,0:T(1,128)S(1)}, f32[1,4]{1,0:T(1,128)S(1)}, u32[]{:S(2)}, u32[]{:S(2)}) collective-permute-start(f32[1,4]{1,0:T(1,128)S(1)} %add.176), channel_id=1, source_target_pairs={{0,2},{2,0},{1,3},{3,1},{4,6},{6,4},{5,7},{7,5},{8,10},{10,8},{9,1... | collective-permute-start | bytes 56 | tf_op jit(solution)/shard_map/ppermute | solution.py:31

commit v3 on v2

--- a/solution.py
+++ b/solution.py
@@ -4,7 +4,7 @@
 from jax.sharding import PartitionSpec as P
 
 HIGH = lax.Precision.HIGH
-CHUNKS = 4
+CHUNKS = 2
 
 
 def block_left(u):

time: 63.2 us -> 61 us (0.965)
  starting transfers between devices: 37.1 us -> 27.8 us
  matrix products: 8.36 us -> 12.8 us
  local copies, waits for them, and re-layouts: 2.92 us -> 4.45 us
  other arithmetic: 3.03 us -> 4.1 us
    ppermute x6 -> x4, starting transfers between devices: 27.8 us -> 21.1 us  [per_device(): fwd_in = lax.ppermute(fwd_out, 'tm', right_pairs)]
    dot_general x3, matrix products: 1.27 us -> 6.17 us  [per_device(): fwd_new = jnp.einsum('mab,mbw->maw', left_op, fwd_in, precision=HIGH)]
    ppermute x6 -> x4, waiting for transfers between devices: 1.09 us -> 4.01 us  [per_device(): fwd_in = lax.ppermute(fwd_out, 'tm', right_pairs)]
    ppermute x6 -> x4, waiting for transfers between devices: 6.61 us -> 3.81 us  [per_device(): bwd_in = lax.ppermute(bwd_out, 'tm', left_pairs)]
    ppermute x6 -> x4, starting transfers between devices: 7.72 us -> 5.16 us  [per_device(): bwd_in = lax.ppermute(bwd_out, 'tm', left_pairs)]
    concatenate x1, local copies, waits for them, and re-layouts: 0.04 us -> 1.87 us  [per_device(): jnp.concatenate([unit[:, 0, :, cols], unit[:, 1, :, cols]], axis=-2)]
    unnamed x7 -> x18, local copies, waits for them, and re-layouts: 1.6 us -> 0.29 us
    squeeze x1, local copies, waits for them, and re-layouts: 0.03 us -> 1.06 us  [block_right(): top = jnp.concatenate([u[:, 0], u[:, 1]], axis=-1)]
  transfers between devices with their start and end apart: 14 -> 10, of which waited for: 10 -> 7; matrix products, arithmetic and copies ran while one was open for 14% -> 25% of each run, Pallas kernels for 0% -> 0%
where the time goes in v3:
time: 61 us; the launch traced here: 60.5 us
  starting transfers between devices  27.8 us (46%)
  matrix products  12.8 us (21%)
  waiting for transfers between devices  11 us (18%)
  local copies, waits for them, and re-layouts  4.45 us (7%)
  other arithmetic  4.1 us (7%)
    ppermute x4, starting transfers between devices, per_device(): fwd_in = lax.ppermute(fwd_out, 'tm', right_pairs)  21.1 us
    dot_general x3, matrix products, per_device(): fwd_new = jnp.einsum('mab,mbw->maw', left_op, fwd_in, precision=HIGH)  6.17 us
    ppermute x4, starting transfers between devices, per_device(): bwd_in = lax.ppermute(bwd_out, 'tm', left_pairs)  5.16 us
    ppermute x4, waiting for transfers between devices, per_device(): fwd_in = lax.ppermute(fwd_out, 'tm', right_pairs)  4.01 us
    ppermute x4, waiting for transfers between devices, per_device(): bwd_in = lax.ppermute(bwd_out, 'tm', left_pairs)  3.81 us
    dot_general x4, matrix products, per_device(): bwd_out = jnp.einsum('mwa,mab->mwb', bwd_in, right_op, precision=HIGH)  3.46 us
    ppermute x2, waiting for transfers between devices, butterfly_sum(): value = value + lax.ppermute(value, axis, pairs)  3.15 us
    dot_general x1, matrix products, per_device(): jnp.einsum('mab,mbw->maw', left_op, fwd_in, precision=HIGH)  2.53 us
  transfers between devices with their start and end apart: 10, of which 7 were waited for; matrix products, arithmetic and copies ran while one was open for 25% of the time, Pallas kernels for 0%

profile of v3, /device:TPU:0, one launch (start us, length us, event | category | flops | bytes accessed | tf_op | source)
XLA Modules:
  0.0 60.5 jit_solution(8725839515509896192)
XLA Ops:
  0.0 1.9 %slice_bitcast_fusion.5 = (f32[256,128]{1,0:T(8,128)S(1)}, f32[256,128]{1,0:T(8,128)}, f32[1,256,128]{2,1,0:T(8,128)S(1)}, f32[1,256,128]{2,1,0:T(8,128)S(1)}) fusion(f32[1,2,256,256]{3,2,1,0:T(8,128)} %bitcast.163), kind=kLoop, calls=%fused_computation.61 | loop fusion | bytes 1048576 | tf_op jit(solution)/shard_map/concatenate | solution.py:66
  1.9 5.7 %collective-permute-start.4 = (f32[1,512,128]{2,1,0:T(8,128)S(1)}, f32[1,512,128]{2,1,0:T(8,128)}, u32[]{:S(2)}, u32[]{:S(2)}) collective-permute-start(f32[1,512,128]{2,1,0:T(8,128)S(1)} %pad_maximum_fusion.5), channel_id=1, source_target_pairs={{0,4},{4,8},{8,12},{1,5},{5,9},{9,13},{2,6},{6,10},{10,14},{3,7},{... | collective-permute-start | bytes 786440 | tf_op jit(solution)/shard_map/ppermute | solution.py:62
  7.5 1.1 %slice_bitcast_fusion.2 = (f32[1,256,256]{2,1,0:T(8,128)S(1)}, f32[1,256,256]{2,1,0:T(8,128)S(1)}) fusion(f32[1,2,256,256]{3,2,1,0:T(8,128)} %bitcast.164), kind=kLoop, calls=%fused_computation.37 | loop fusion | bytes 1048576 | tf_op jit(solution)/shard_map/squeeze | solution.py:17
  9.0 1.1 %convolution_bitcast_fusion.5 = f32[1,128,512]{2,1,0:T(8,128)} fusion(f32[1,256,256]{2,1,0:T(8,128)S(1)} %get-tuple-element.18, f32[1,256,256]{2,1,0:T(8,128)S(1)} %fusion.47, f32[1,256,256]{2,1,0:T(8,128)S(1)} %get-tuple-element.17, f32[256,256]{1,0:T(8,128)S(1)} %bitcast.166, f32[256,256]{1,0:T(8,128)S(1)} %negate_bitcast_fusion, pred[]{:T(512)S(6)} %eq.16), kind=kOutput, calls=%fused_computation.10 | convolution fusion | flops 202244096 | bytes 1572865 | tf_op jit(solution)/shard_map/mwa,mab->mwb/dot_general | solution.py:84
  10.2 1.3 %collective-permute-start = (f32[1,128,512]{2,1,0:T(8,128)}, f32[1,128,512]{2,1,0:T(8,128)}, u32[]{:S(2)}, u32[]{:S(2)}) collective-permute-start(f32[1,128,512]{2,1,0:T(8,128)} %convolution_bitcast_fusion.5), channel_id=1, source_target_pairs={{4,0},{8,4},{12,8},{5,1},{9,5},{13,9},{6,2},{10,6},{14,10},{7,3},{... | collective-permute-start | bytes 786440 | tf_op jit(solution)/shard_map/ppermute | solution.py:63
  12.4 2.5 %bitcast_dynamic-update-slice_fusion.2 = (f32[4,1,512,128]{3,2,0,1:T(8,128)S(1)}, f32[512,128]{1,0:T(8,128)}) fusion(f32[4,1,512,128]{3,2,0,1:T(8,128)S(1)} %bitcast_dynamic-update-slice_fusion.3, s32[]{:T(128)S(6)} %select_n.83, f32[1,512,128]{2,1,0:T(8,128)} %collective-permute-done.4, f32[1,256,256]{2,1,0:T(8,128)} %copy-done.5, ...), kind=kOutput, calls=%fused_computation.45 | convolution fusion | flops 202244096 | bytes 1835013 | tf_op jit(solution)/shard_map/mab,mbw->maw/dot_general | solution.py:73
  14.9 5.2 %collective-permute-start.5 = (f32[1,512,128]{2,1,0:T(8,128)}, f32[1,512,128]{2,1,0:T(8,128)}, u32[]{:S(2)}, u32[]{:S(2)}) collective-permute-start(f32[1,512,128]{2,1,0:T(8,128)} %bitcast.33), channel_id=1, source_target_pairs={{0,4},{4,8},{8,12},{1,5},{5,9},{9,13},{2,6},{6,10},{10,14},{3,7},{... | collective-permute-start | bytes 786440 | tf_op jit(solution)/shard_map/ppermute | solution.py:62
  20.1 1.0 %fusion.18 = f32[1,128,512]{2,1,0:T(8,128)S(1)} fusion(f32[1,128,512]{2,1,0:T(8,128)} %collective-permute-done, f32[256,256]{1,0:T(8,128)S(1)} %negate_bitcast_fusion, f32[256,256]{1,0:T(8,128)S(1)} %bitcast.168, pred[]{:T(512)S(6)} %eq.16), kind=kLoop, calls=%fused_computation.41 | loop fusion | flops 131072 | bytes 1048577 | tf_op jit(solution)/shard_map/jit(_where)/select_n | solution.py:75
  21.3 1.5 %convolution_bitcast_fusion.4 = f32[1,128,512]{2,1,0:T(8,128)S(1)} fusion(f32[1,128,512]{2,1,0:T(8,128)S(1)} %fusion.18, f32[1,256,256]{2,1,0:T(8,128)} %copy-done.5, f32[1,256,256]{2,1,0:T(8,128)S(1)} %fusion.47, f32[1,256,256]{2,1,0:T(8,128)S(1)} %copy-done.4), kind=kOutput, calls=%fused_computation.9 | convolution fusion | flops 202113024 | bytes 1310720 | tf_op jit(solution)/shard_map/mwa,mab->mwb/dot_general | solution.py:84
  22.8 1.3 %collective-permute-start.1 = (f32[1,128,512]{2,1,0:T(8,128)S(1)}, f32[1,128,512]{2,1,0:T(8,128)S(1)}, u32[]{:S(2)}, u32[]{:S(2)}) collective-permute-start(f32[1,128,512]{2,1,0:T(8,128)S(1)} %convolution_bitcast_fusion.4), channel_id=1, source_target_pairs={{4,0},{8,4},{12,8},{5,1},{9,5},{13,9},{6,2},{10,6},{14,10},{7,3},{... | collective-permute-start | bytes 786440 | tf_op jit(solution)/shard_map/ppermute | solution.py:63
  24.4 2.4 %bitcast_dynamic-update-slice_fusion.1 = (f32[4,1,512,128]{3,2,0,1:T(8,128)S(1)}, f32[512,128]{1,0:T(8,128)}) fusion(f32[4,1,512,128]{3,2,0,1:T(8,128)S(1)} %get-tuple-element.21, s32[]{:T(128)S(6)} %select_n.85, f32[1,512,128]{2,1,0:T(8,128)} %collective-permute-done.5, f32[1,256,256]{2,1,0:T(8,128)} %copy-done.5, f32[1,256,256]{2,1,0:T(8,128)S(1)} %copy-done.4, ...), kind=kOutput, calls=%fused_computation.44 | convolution fusion | flops 202113024 | bytes 1572868 | tf_op jit(solution)/shard_map/mab,mbw->maw/dot_general | solution.py:77
  26.8 5.1 %collective-permute-start.6 = (f32[1,512,128]{2,1,0:T(8,128)}, f32[1,512,128]{2,1,0:T(8,128)}, u32[]{:S(2)}, u32[]{:S(2)}) collective-permute-start(f32[1,512,128]{2,1,0:T(8,128)} %bitcast.37), channel_id=1, source_target_pairs={{0,4},{4,8},{8,12},{1,5},{5,9},{9,13},{2,6},{6,10},{10,14},{3,7},{... | collective-permute-start | bytes 786440 | tf_op jit(solution)/shard_map/ppermute | solution.py:62
  32.4 1.3 %collective-permute-start.2 = (f32[1,128,512]{2,1,0:T(8,128)S(1)}, f32[1,128,512]{2,1,0:T(8,128)S(1)}, u32[]{:S(2)}, u32[]{:S(2)}) collective-permute-start(f32[1,128,512]{2,1,0:T(8,128)S(1)} %convolution_bitcast_fusion.3), channel_id=1, source_target_pairs={{4,0},{8,4},{12,8},{5,1},{9,5},{13,9},{6,2},{10,6},{14,10},{7,3},{... | collective-permute-start | bytes 786440 | tf_op jit(solution)/shard_map/ppermute | solution.py:63
  33.8 1.7 %collective-permute-done.6 = f32[1,512,128]{2,1,0:T(8,128)} collective-permute-done((f32[1,512,128]{2,1,0:T(8,128)}, f32[1,512,128]{2,1,0:T(8,128)}, u32[]{:S(2)}, u32[]{:S(2)}) %collective-permute-start.6) | collective-permute-done | bytes 262176 | tf_op jit(solution)/shard_map/ppermute | solution.py:62
  35.5 2.2 %bitcast_dynamic-update-slice_fusion = (f32[4,1,512,128]{3,2,0,1:T(8,128)S(1)}, f32[512,128]{1,0:T(8,128)}) fusion(f32[4,1,512,128]{3,2,0,1:T(8,128)S(1)} %get-tuple-element.23, s32[]{:T(128)S(6)} %select_n.86, f32[1,512,128]{2,1,0:T(8,128)} %collective-permute-done.6, f32[1,256,256]{2,1,0:T(8,128)S(1)} %copy-done.6, f32[1,256,256]{2,1,0:T(8,128)S(1)} %copy-done.4, ...), kind=kOutput, calls=%fused_computation.43 | convolution fusion | flops 202113024 | bytes 1572868 | tf_op jit(solution)/shard_map/mab,mbw->maw/dot_general | solution.py:77
  37.7 5.1 %collective-permute-start.7 = (f32[1,512,128]{2,1,0:T(8,128)}, f32[1,512,128]{2,1,0:T(8,128)}, u32[]{:S(2)}, u32[]{:S(2)}) collective-permute-start(f32[1,512,128]{2,1,0:T(8,128)} %bitcast.41), channel_id=1, source_target_pairs={{0,4},{4,8},{8,12},{1,5},{5,9},{9,13},{2,6},{6,10},{10,14},{3,7},{... | collective-permute-start | bytes 786440 | tf_op jit(solution)/shard_map/ppermute | solution.py:62
  43.4 1.3 %collective-permute-start.3 = (f32[1,128,512]{2,1,0:T(8,128)S(1)}, f32[1,128,512]{2,1,0:T(8,128)S(1)}, u32[]{:S(2)}, u32[]{:S(2)}) collective-permute-start(f32[1,128,512]{2,1,0:T(8,128)S(1)} %convolution_bitcast_fusion.2), channel_id=1, source_target_pairs={{4,0},{8,4},{12,8},{5,1},{9,5},{13,9},{6,2},{10,6},{14,10},{7,3},{... | collective-permute-start | bytes 786440 | tf_op jit(solution)/shard_map/ppermute | solution.py:63
  44.7 1.6 %collective-permute-done.7 = f32[1,512,128]{2,1,0:T(8,128)} collective-permute-done((f32[1,512,128]{2,1,0:T(8,128)}, f32[1,512,128]{2,1,0:T(8,128)}, u32[]{:S(2)}, u32[]{:S(2)}) %collective-permute-start.7) | collective-permute-done | bytes 262176 | tf_op jit(solution)/shard_map/ppermute | solution.py:62
  46.3 1.5 %fusion = f32[4,1,512,128]{3,2,0,1:T(8,128)S(1)} fusion(f32[4,1,512,128]{3,2,0,1:T(8,128)S(1)} %get-tuple-element.25, s32[]{:T(128)S(6)} %select_n.87, f32[1,512,128]{2,1,0:T(8,128)} %collective-permute-done.7, f32[1,256,256]{2,1,0:T(8,128)S(1)} %copy-done.7, f32[1,256,256]{2,1,0:T(8,128)S(1)} %copy-done.4, f32[1,256,256]{2,1,0:T(8,128)S(1)} %fusion.47), kind=kOutput, calls=%fused_computation.6 | convolution fusion | flops 202113024 | bytes 1310724 | tf_op jit(solution)/shard_map/mab,mbw->maw/dot_general | solution.py:77
  47.9 3.8 %collective-permute-done.3 = f32[1,128,512]{2,1,0:T(8,128)S(1)} collective-permute-done((f32[1,128,512]{2,1,0:T(8,128)S(1)}, f32[1,128,512]{2,1,0:T(8,128)S(1)}, u32[]{:S(2)}, u32[]{:S(2)}) %collective-permute-start.3) | collective-permute-done | bytes 262176 | tf_op jit(solution)/shard_map/ppermute | solution.py:63
  54.0 1.3 %subtract_bitcast_fusion = f32[1,4]{1,0:T(1,128)S(1)} fusion(f32[4]{0:T(128)S(1)} %get-tuple-element.6, f32[4]{0:T(128)S(1)} %get-tuple-element.5, f32[]{:T(128)} %get-tuple-element.9, f32[]{:T(128)} %get-tuple-element.11), kind=kLoop, calls=%fused_computation.71 | loop fusion | flops 12 | bytes 56 | tf_op jit(solution)/shard_map/sub | solution.py:98
  55.4 1.1 %collective-permute-done.8 = f32[1,4]{1,0:T(1,128)S(1)} collective-permute-done((f32[1,4]{1,0:T(1,128)S(1)}, f32[1,4]{1,0:T(1,128)S(1)}, u32[]{:S(2)}, u32[]{:S(2)}) %collective-permute-start.8) | collective-permute-done | bytes 48 | tf_op jit(solution)/shard_map/ppermute | solution.py:31
  56.5 1.5 %collective-permute-start.9 = (f32[1,4]{1,0:T(1,128)S(1)}, f32[1,4]{1,0:T(1,128)S(1)}, u32[]{:S(2)}, u32[]{:S(2)}) collective-permute-start(f32[1,4]{1,0:T(1,128)S(1)} %add.136), channel_id=1, source_target_pairs={{0,2},{2,0},{1,3},{3,1},{4,6},{6,4},{5,7},{7,5},{8,10},{10,8},{9,1... | collective-permute-start | bytes 56 | tf_op jit(solution)/shard_map/ppermute | solution.py:31
  58.0 2.0 %collective-permute-done.9 = f32[1,4]{1,0:T(1,128)S(1)} collective-permute-done((f32[1,4]{1,0:T(1,128)S(1)}, f32[1,4]{1,0:T(1,128)S(1)}, u32[]{:S(2)}, u32[]{:S(2)}) %collective-permute-start.9) | collective-permute-done | bytes 48 | tf_op jit(solution)/shard_map/ppermute | solution.py:31
  (53 shorter events, 5.6 us)
Async XLA Ops:
  0.0 8.6 %copy-start = (f32[1,1,2,256,256]{4,3,2,1,0:T(8,128)S(1)}, f32[1,1,2,256,256]{4,3,2,1,0:T(8,128)}, u32[]{:S(2)}) copy-start(f32[1,1,2,256,256]{4,3,2,1,0:T(8,128)} %param.3) | copy-start | bytes 1572868
  0.0 8.7 %copy-start.2 = (f32[2,256,256]{2,1,0:T(8,128)S(1)}, f32[2,256,256]{2,1,0:T(8,128)}, u32[]{:S(2)}) copy-start(f32[2,256,256]{2,1,0:T(8,128)} %param.5) | copy-start | bytes 1572868
  1.9 10.5 %collective-permute-start.4 = (f32[1,512,128]{2,1,0:T(8,128)S(1)}, f32[1,512,128]{2,1,0:T(8,128)}, u32[]{:S(2)}, u32[]{:S(2)}) collective-permute-start(f32[1,512,128]{2,1,0:T(8,128)S(1)} %pad_maximum_fusion.5), channel_id=1, source_target_pairs={{0,4},{4,8},{8,12},{1,5},{5,9},{9,13},{2,6},{6,10},{10,14},{3,7},{... | collective-permute-start | bytes 786440 | tf_op jit(solution)/shard_map/ppermute | solution.py:62
  8.6 1.6 %copy-start.3 = (f32[1,256,256]{2,1,0:T(8,128)}, f32[1,256,256]{2,1,0:T(8,128)S(1)}, u32[]{:S(2)}) copy-start(f32[1,256,256]{2,1,0:T(8,128)S(1)} %get-tuple-element.17) | copy-start | bytes 786436
  8.6 3.0 %copy-start.5 = (f32[1,256,256]{2,1,0:T(8,128)}, f32[1,256,256]{2,1,0:T(8,128)S(1)}, u32[]{:S(2)}) copy-start(f32[1,256,256]{2,1,0:T(8,128)S(1)} %get-tuple-element.18) | copy-start | bytes 786436
  10.2 10.0 %collective-permute-start = (f32[1,128,512]{2,1,0:T(8,128)}, f32[1,128,512]{2,1,0:T(8,128)}, u32[]{:S(2)}, u32[]{:S(2)}) collective-permute-start(f32[1,128,512]{2,1,0:T(8,128)} %convolution_bitcast_fusion.5), channel_id=1, source_target_pairs={{4,0},{8,4},{12,8},{5,1},{9,5},{13,9},{6,2},{10,6},{14,10},{7,3},{... | collective-permute-start | bytes 786440 | tf_op jit(solution)/shard_map/ppermute | solution.py:63
  11.9 9.4 %copy-start.4 = (f32[1,256,256]{2,1,0:T(8,128)S(1)}, f32[1,256,256]{2,1,0:T(8,128)}, u32[]{:S(2)}) copy-start(f32[1,256,256]{2,1,0:T(8,128)} %copy-done.3) | copy-start | bytes 786436
  14.9 9.5 %collective-permute-start.5 = (f32[1,512,128]{2,1,0:T(8,128)}, f32[1,512,128]{2,1,0:T(8,128)}, u32[]{:S(2)}, u32[]{:S(2)}) collective-permute-start(f32[1,512,128]{2,1,0:T(8,128)} %bitcast.33), channel_id=1, source_target_pairs={{0,4},{4,8},{8,12},{1,5},{5,9},{9,13},{2,6},{6,10},{10,14},{3,7},{... | collective-permute-start | bytes 786440 | tf_op jit(solution)/shard_map/ppermute | solution.py:62
  21.3 10.7 %copy-start.6 = (f32[1,256,256]{2,1,0:T(8,128)S(1)}, f32[1,256,256]{2,1,0:T(8,128)}, u32[]{:S(2)}) copy-start(f32[1,256,256]{2,1,0:T(8,128)} %copy-done.5) | copy-start | bytes 786436
  22.8 9.1 %collective-permute-start.1 = (f32[1,128,512]{2,1,0:T(8,128)S(1)}, f32[1,128,512]{2,1,0:T(8,128)S(1)}, u32[]{:S(2)}, u32[]{:S(2)}) collective-permute-start(f32[1,128,512]{2,1,0:T(8,128)S(1)} %convolution_bitcast_fusion.4), channel_id=1, source_target_pairs={{4,0},{8,4},{12,8},{5,1},{9,5},{13,9},{6,2},{10,6},{14,10},{7,3},{... | collective-permute-start | bytes 786440 | tf_op jit(solution)/shard_map/ppermute | solution.py:63
  26.8 8.7 %collective-permute-start.6 = (f32[1,512,128]{2,1,0:T(8,128)}, f32[1,512,128]{2,1,0:T(8,128)}, u32[]{:S(2)}, u32[]{:S(2)}) collective-permute-start(f32[1,512,128]{2,1,0:T(8,128)} %bitcast.37), channel_id=1, source_target_pairs={{0,4},{4,8},{8,12},{1,5},{5,9},{9,13},{2,6},{6,10},{10,14},{3,7},{... | collective-permute-start | bytes 786440 | tf_op jit(solution)/shard_map/ppermute | solution.py:62
  32.4 10.4 %collective-permute-start.2 = (f32[1,128,512]{2,1,0:T(8,128)S(1)}, f32[1,128,512]{2,1,0:T(8,128)S(1)}, u32[]{:S(2)}, u32[]{:S(2)}) collective-permute-start(f32[1,128,512]{2,1,0:T(8,128)S(1)} %convolution_bitcast_fusion.3), channel_id=1, source_target_pairs={{4,0},{8,4},{12,8},{5,1},{9,5},{13,9},{6,2},{10,6},{14,10},{7,3},{... | collective-permute-start | bytes 786440 | tf_op jit(solution)/shard_map/ppermute | solution.py:63
  37.7 8.6 %collective-permute-start.7 = (f32[1,512,128]{2,1,0:T(8,128)}, f32[1,512,128]{2,1,0:T(8,128)}, u32[]{:S(2)}, u32[]{:S(2)}) collective-permute-start(f32[1,512,128]{2,1,0:T(8,128)} %bitcast.41), channel_id=1, source_target_pairs={{0,4},{4,8},{8,12},{1,5},{5,9},{9,13},{2,6},{6,10},{10,14},{3,7},{... | collective-permute-start | bytes 786440 | tf_op jit(solution)/shard_map/ppermute | solution.py:62
  42.9 3.3 %copy-start.7 = (f32[1,256,256]{2,1,0:T(8,128)S(1)}, f32[1,256,256]{2,1,0:T(8,128)}, u32[]{:S(2)}) copy-start(f32[1,256,256]{2,1,0:T(8,128)} %copy-done.5) | copy-start | bytes 786436
  43.4 8.3 %collective-permute-start.3 = (f32[1,128,512]{2,1,0:T(8,128)S(1)}, f32[1,128,512]{2,1,0:T(8,128)S(1)}, u32[]{:S(2)}, u32[]{:S(2)}) collective-permute-start(f32[1,128,512]{2,1,0:T(8,128)S(1)} %convolution_bitcast_fusion.2), channel_id=1, source_target_pairs={{4,0},{8,4},{12,8},{5,1},{9,5},{13,9},{6,2},{10,6},{14,10},{7,3},{... | collective-permute-start | bytes 786440 | tf_op jit(solution)/shard_map/ppermute | solution.py:63
  51.8 1.6 %copy-start.1 = (f32[4,2,256,256]{3,2,1,0:T(8,128)S(1)}, f32[4,2,256,256]{3,2,1,0:T(8,128)}, u32[]{:S(2)}) copy-start(f32[4,2,256,256]{3,2,1,0:T(8,128)} %param.4) | copy-start | bytes 6291460
  55.3 1.2 %collective-permute-start.8 = (f32[1,4]{1,0:T(1,128)S(1)}, f32[1,4]{1,0:T(1,128)S(1)}, u32[]{:S(2)}, u32[]{:S(2)}) collective-permute-start(f32[1,4]{1,0:T(1,128)S(1)} %subtract_bitcast_fusion), channel_id=1, source_target_pairs={{0,1},{1,0},{2,3},{3,2},{4,5},{5,4},{6,7},{7,6},{8,9},{9,8},{10,11... | collective-permute-start | bytes 56 | tf_op jit(solution)/shard_map/ppermute | solution.py:31
  56.5 3.5 %collective-permute-start.9 = (f32[1,4]{1,0:T(1,128)S(1)}, f32[1,4]{1,0:T(1,128)S(1)}, u32[]{:S(2)}, u32[]{:S(2)}) collective-permute-start(f32[1,4]{1,0:T(1,128)S(1)} %add.136), channel_id=1, source_target_pairs={{0,2},{2,0},{1,3},{3,1},{4,6},{6,4},{5,7},{7,5},{8,10},{10,8},{9,1... | collective-permute-start | bytes 56 | tf_op jit(solution)/shard_map/ppermute | solution.py:31

commit v4 on v3

--- a/solution.py
+++ b/solution.py
@@ -49,8 +49,8 @@
     is_first = position == 0
     is_last = position == blocks - 1
 
-    fwd_buf = jnp.zeros((chunks + 2, members_here, 2 * order, width), jnp.float32)
-    bwd_buf = jnp.zeros((chunks + 2, members_here, width, 2 * order), jnp.float32)
+    fwd_steps = []
+    bwd_steps = []
     fwd_out = None
     bwd_out = None
     steps = chunks + blocks - 1
@@ -75,16 +75,16 @@
             bwd_in = jnp.where(is_last, rows, bwd_in)
         else:
             fwd_new = jnp.einsum("mab,mbw->maw", left_op, fwd_in, precision=HIGH)
-        fwd_chunk = jnp.clip(step - position, -1, chunks) + 1
-        bwd_chunk = jnp.clip(step - (blocks - 1 - position), -1, chunks) + 1
-        fwd_buf = lax.dynamic_update_index_in_dim(fwd_buf, fwd_new, fwd_chunk, 0)
-        bwd_buf = lax.dynamic_update_index_in_dim(bwd_buf, bwd_in, bwd_chunk, 0)
+        fwd_steps.append(fwd_new)
+        bwd_steps.append(bwd_in)
         fwd_out = fwd_new
         if step < steps - 1:
             bwd_out = jnp.einsum("mwa,mab->mwb", bwd_in, right_op, precision=HIGH)
 
-    fwd_all = fwd_buf[1:chunks + 1].reshape(chunks, members_here, 2, order, width)
-    bwd_all = bwd_buf[1:chunks + 1].reshape(chunks, members_here, width, 2, order)
+    fwd_all = lax.dynamic_slice_in_dim(jnp.stack(fwd_steps), position, chunks, 0)
+    bwd_all = lax.dynamic_slice_in_dim(jnp.stack(bwd_steps), blocks - 1 - position, chunks, 0)
+    fwd_all = fwd_all.reshape(chunks, members_here, 2, order, width)
+    bwd_all = bwd_all.reshape(chunks, members_here, width, 2, order)
     parts = jnp.einsum("cmpaw,cmwqb->mpqab", fwd_all, bwd_all, precision=HIGH)
     q_re = parts[:, 0, 0] - parts[:, 1, 1]
     q_im = parts[:, 0, 1] + parts[:, 1, 0]

time: 61 us -> 58.9 us (0.966)
  matrix products: 12.8 us -> 7.91 us
  waiting for transfers between devices: 11 us -> 14.5 us
  starting transfers between devices: 27.8 us -> 27 us
    dot_general x3, matrix products: 6.17 us -> 3.4 us  [per_device(): fwd_new = jnp.einsum('mab,mbw->maw', left_op, fwd_in, precision=HIGH)]
    ppermute x4, waiting for transfers between devices: 3.81 us -> 6.26 us  [per_device(): bwd_in = lax.ppermute(bwd_out, 'tm', left_pairs)]
    unnamed x18 -> x22, local copies, waits for them, and re-layouts: 0.29 us -> 2.02 us
    concatenate x1, local copies, waits for them, and re-layouts: 1.87 us -> 0.7 us  [per_device(): jnp.concatenate([unit[:, 0, :, cols], unit[:, 1, :, cols]], axis=-2)]
    dot_general x4, matrix products: 3.46 us -> 2.35 us  [per_device(): bwd_out = jnp.einsum('mwa,mab->mwb', bwd_in, right_op, precision=HIGH)]
    neg x1, other arithmetic: 0.02 us -> 1.07 us  [block_right(): bottom = jnp.concatenate([-u[:, 1], u[:, 0]], axis=-1)]
    dot_general x1, matrix products: 2.53 us -> 1.53 us  [per_device(): jnp.einsum('mab,mbw->maw', left_op, fwd_in, precision=HIGH)]
    select_n x1 -> x0, other arithmetic: 0.98 us -> none  [per_device(): bwd_in = jnp.where(is_last, rows, bwd_in)]
  transfers between devices with their start and end apart: 10 -> 10, of which waited for: 7 -> 8; matrix products, arithmetic and copies ran while one was open for 25% -> 10% of each run, Pallas kernels for 0% -> 0%
where the time goes in v4:
time: 58.9 us; the launch traced here: 58.4 us
  starting transfers between devices  27 us (46%)
  waiting for transfers between devices  14.5 us (25%)
  matrix products  7.91 us (13%)
  local copies, waits for them, and re-layouts  4.44 us (8%)
  other arithmetic  4.19 us (7%)
    ppermute x4, starting transfers between devices, per_device(): fwd_in = lax.ppermute(fwd_out, 'tm', right_pairs)  20.3 us
    ppermute x4, waiting for transfers between devices, per_device(): bwd_in = lax.ppermute(bwd_out, 'tm', left_pairs)  6.26 us
    ppermute x4, starting transfers between devices, per_device(): bwd_in = lax.ppermute(bwd_out, 'tm', left_pairs)  5.29 us
    ppermute x4, waiting for transfers between devices, per_device(): fwd_in = lax.ppermute(fwd_out, 'tm', right_pairs)  4.92 us
    dot_general x3, matrix products, per_device(): fwd_new = jnp.einsum('mab,mbw->maw', left_op, fwd_in, precision=HIGH)  3.4 us
    ppermute x2, waiting for transfers between devices, butterfly_sum(): value = value + lax.ppermute(value, axis, pairs)  3.31 us
    dot_general x4, matrix products, per_device(): bwd_out = jnp.einsum('mwa,mab->mwb', bwd_in, right_op, precision=HIGH)  2.35 us
    unnamed x22, local copies, waits for them, and re-layouts  2.02 us
  transfers between devices with their start and end apart: 10, of which 8 were waited for; matrix products, arithmetic and copies ran while one was open for 10% of the time, Pallas kernels for 0%

profile of v4, /device:TPU:0, one launch (start us, length us, event | category | flops | bytes accessed | tf_op | source)
XLA Modules:
  0.0 58.4 jit_solution(6172478725647398576)
XLA Ops:
  0.0 1.1 %slice_bitcast_fusion.2 = (f32[1,256,256]{2,1,0:T(8,128)S(1)}, f32[1,256,256]{2,1,0:T(8,128)S(1)}) fusion(f32[1,2,256,256]{3,2,1,0:T(8,128)} %bitcast.158), kind=kLoop, calls=%fused_computation.37 | loop fusion | bytes 1048576 | tf_op jit(solution)/shard_map/squeeze | solution.py:17
  1.1 1.1 %fusion.46 = f32[1,256,256]{2,1,0:T(8,128)S(1)} fusion(f32[1,2,256,256]{3,2,1,0:T(8,128)} %bitcast.159), kind=kLoop, calls=%fused_computation.82 | loop fusion | flops 65536 | bytes 524288 | tf_op jit(solution)/shard_map/neg | solution.py:18
  2.6 1.1 %convolution_bitcast_fusion.5 = f32[1,128,512]{2,1,0:T(8,128)} fusion(f32[1,256,256]{2,1,0:T(8,128)S(1)} %get-tuple-element.20, f32[1,256,256]{2,1,0:T(8,128)S(1)} %fusion.46, f32[1,256,256]{2,1,0:T(8,128)S(1)} %get-tuple-element.19, f32[256,256]{1,0:T(8,128)S(1)} %bitcast.161, f32[256,256]{1,0:T(8,128)S(1)} %negate_bitcast_fusion, pred[]{:T(512)S(6)} %eq.16), kind=kOutput, calls=%fused_computation.10 | convolution fusion | flops 202244096 | bytes 1572865 | tf_op jit(solution)/shard_map/mwa,mab->mwb/dot_general | solution.py:82
  3.7 1.3 %collective-permute-start = (f32[1,128,512]{2,1,0:T(8,128)}, f32[1,128,512]{2,1,0:T(8,128)S(1)}, u32[]{:S(2)}, u32[]{:S(2)}) collective-permute-start(f32[1,128,512]{2,1,0:T(8,128)} %convolution_bitcast_fusion.5), channel_id=1, source_target_pairs={{4,0},{8,4},{12,8},{5,1},{9,5},{13,9},{6,2},{10,6},{14,10},{7,3},{... | collective-permute-start | bytes 786440 | tf_op jit(solution)/shard_map/ppermute | solution.py:63
  5.7 6.3 %collective-permute-start.4 = (f32[1,512,128]{2,1,0:T(8,128)S(1)}, f32[1,512,128]{2,1,0:T(8,128)}, u32[]{:S(2)}, u32[]{:S(2)}) collective-permute-start(f32[1,512,128]{2,1,0:T(8,128)S(1)} %pad_maximum_fusion.5), channel_id=1, source_target_pairs={{0,4},{4,8},{8,12},{1,5},{5,9},{9,13},{2,6},{6,10},{10,14},{3,7},{... | collective-permute-start | bytes 786440 | tf_op jit(solution)/shard_map/ppermute | solution.py:62
  12.1 3.1 %collective-permute-done = f32[1,128,512]{2,1,0:T(8,128)S(1)} collective-permute-done((f32[1,128,512]{2,1,0:T(8,128)}, f32[1,128,512]{2,1,0:T(8,128)S(1)}, u32[]{:S(2)}, u32[]{:S(2)}) %collective-permute-start) | collective-permute-done | bytes 262176 | tf_op jit(solution)/shard_map/ppermute | solution.py:63
  15.2 1.1 %copy-done.3 = f32[5,1,128,512]{3,2,1,0:T(8,128)} copy-done((f32[5,1,128,512]{3,2,1,0:T(8,128)}, f32[5,1,128,512]{3,2,1,0:T(8,128)S(1)}, u32[]{:S(2)}) %copy-start.3) | copy-done | bytes 1310744
  16.7 1.3 %collective-permute-start.1 = (f32[1,128,512]{2,1,0:T(8,128)S(1)}, f32[1,128,512]{2,1,0:T(8,128)S(1)}, u32[]{:S(2)}, u32[]{:S(2)}) collective-permute-start(f32[1,128,512]{2,1,0:T(8,128)S(1)} %convolution_bitcast_fusion.4), channel_id=1, source_target_pairs={{4,0},{8,4},{12,8},{5,1},{9,5},{13,9},{6,2},{10,6},{14,10},{7,3},{... | collective-permute-start | bytes 786440 | tf_op jit(solution)/shard_map/ppermute | solution.py:63
  18.0 1.5 %bitcast_dynamic-update-slice_fusion.2 = (f32[5,1,512,128]{3,2,1,0:T(8,128)S(1)}, f32[512,128]{1,0:T(8,128)S(1)}) fusion(f32[5,1,512,128]{3,2,1,0:T(8,128)S(1)} %bitcast_dynamic-update-slice_fusion.3, f32[1,512,128]{2,1,0:T(8,128)} %collective-permute-done.4, f32[1,256,256]{2,1,0:T(8,128)S(1)} %copy-done.6, f32[1,256,256]{2,1,0:T(8,128)S(1)} %get-tuple-element.19, ...), kind=kOutput, calls=%fused_computation.50 | convolution fusion | flops 202244096 | bytes 1835009 | tf_op jit(solution)/shard_map/mab,mbw->maw/dot_general | solution.py:73
  19.5 4.6 %collective-permute-start.5 = (f32[1,512,128]{2,1,0:T(8,128)S(1)}, f32[1,512,128]{2,1,0:T(8,128)S(1)}, u32[]{:S(2)}, u32[]{:S(2)}) collective-permute-start(f32[1,512,128]{2,1,0:T(8,128)S(1)} %bitcast.166), channel_id=1, source_target_pairs={{0,4},{4,8},{8,12},{1,5},{5,9},{9,13},{2,6},{6,10},{10,14},{3,7},{... | collective-permute-start | bytes 786440 | tf_op jit(solution)/shard_map/ppermute | solution.py:62
  24.1 2.0 %collective-permute-done.1 = f32[1,128,512]{2,1,0:T(8,128)S(1)} collective-permute-done((f32[1,128,512]{2,1,0:T(8,128)S(1)}, f32[1,128,512]{2,1,0:T(8,128)S(1)}, u32[]{:S(2)}, u32[]{:S(2)}) %collective-permute-start.1) | collective-permute-done | bytes 262176 | tf_op jit(solution)/shard_map/ppermute | solution.py:63
  26.5 1.4 %collective-permute-start.2 = (f32[1,128,512]{2,1,0:T(8,128)S(1)}, f32[1,128,512]{2,1,0:T(8,128)S(1)}, u32[]{:S(2)}, u32[]{:S(2)}) collective-permute-start(f32[1,128,512]{2,1,0:T(8,128)S(1)} %convolution_bitcast_fusion.3), channel_id=1, source_target_pairs={{4,0},{8,4},{12,8},{5,1},{9,5},{13,9},{6,2},{10,6},{14,10},{7,3},{... | collective-permute-start | bytes 786440 | tf_op jit(solution)/shard_map/ppermute | solution.py:63
  27.9 0.9 %collective-permute-done.5 = f32[1,512,128]{2,1,0:T(8,128)S(1)} collective-permute-done((f32[1,512,128]{2,1,0:T(8,128)S(1)}, f32[1,512,128]{2,1,0:T(8,128)S(1)}, u32[]{:S(2)}, u32[]{:S(2)}) %collective-permute-start.5) | collective-permute-done | bytes 262176 | tf_op jit(solution)/shard_map/ppermute | solution.py:62
  29.4 4.4 %collective-permute-start.6 = (f32[1,512,128]{2,1,0:T(8,128)S(1)}, f32[1,512,128]{2,1,0:T(8,128)S(1)}, u32[]{:S(2)}, u32[]{:S(2)}) collective-permute-start(f32[1,512,128]{2,1,0:T(8,128)S(1)} %bitcast.167), channel_id=1, source_target_pairs={{0,4},{4,8},{8,12},{1,5},{5,9},{9,13},{2,6},{6,10},{10,14},{3,7},{... | collective-permute-start | bytes 786440 | tf_op jit(solution)/shard_map/ppermute | solution.py:62
  33.8 1.2 %collective-permute-done.2 = f32[1,128,512]{2,1,0:T(8,128)S(1)} collective-permute-done((f32[1,128,512]{2,1,0:T(8,128)S(1)}, f32[1,128,512]{2,1,0:T(8,128)S(1)}, u32[]{:S(2)}, u32[]{:S(2)}) %collective-permute-start.2) | collective-permute-done | bytes 262176 | tf_op jit(solution)/shard_map/ppermute | solution.py:63
  35.5 1.3 %collective-permute-start.3 = (f32[1,128,512]{2,1,0:T(8,128)S(1)}, f32[1,128,512]{2,1,0:T(8,128)S(1)}, u32[]{:S(2)}, u32[]{:S(2)}) collective-permute-start(f32[1,128,512]{2,1,0:T(8,128)S(1)} %convolution_bitcast_fusion.2), channel_id=1, source_target_pairs={{4,0},{8,4},{12,8},{5,1},{9,5},{13,9},{6,2},{10,6},{14,10},{7,3},{... | collective-permute-start | bytes 786440 | tf_op jit(solution)/shard_map/ppermute | solution.py:63
  37.7 1.3 %bitcast_dynamic-update-slice_fusion = (f32[5,1,512,128]{3,2,1,0:T(8,128)S(1)}, f32[512,128]{1,0:T(8,128)}) fusion(f32[5,1,512,128]{3,2,1,0:T(8,128)S(1)} %get-tuple-element.25, f32[1,512,128]{2,1,0:T(8,128)S(1)} %collective-permute-done.6, f32[1,256,256]{2,1,0:T(8,128)S(1)} %copy-done.6, f32[1,256,256]{2,1,0:T(8,128)S(1)} %get-tuple-element.19, ...), kind=kOutput, calls=%fused_computation.44 | convolution fusion | flops 202113024 | bytes 1572864 | tf_op jit(solution)/shard_map/mab,mbw->maw/dot_general | solution.py:77
  38.9 5.1 %collective-permute-start.7 = (f32[1,512,128]{2,1,0:T(8,128)}, f32[1,512,128]{2,1,0:T(8,128)}, u32[]{:S(2)}, u32[]{:S(2)}) collective-permute-start(f32[1,512,128]{2,1,0:T(8,128)} %bitcast.37), channel_id=1, source_target_pairs={{0,4},{4,8},{8,12},{1,5},{5,9},{9,13},{2,6},{6,10},{10,14},{3,7},{... | collective-permute-start | bytes 786440 | tf_op jit(solution)/shard_map/ppermute | solution.py:62
  44.3 3.2 %collective-permute-done.7 = f32[1,512,128]{2,1,0:T(8,128)} collective-permute-done((f32[1,512,128]{2,1,0:T(8,128)}, f32[1,512,128]{2,1,0:T(8,128)}, u32[]{:S(2)}, u32[]{:S(2)}) %collective-permute-start.7) | collective-permute-done | bytes 262176 | tf_op jit(solution)/shard_map/ppermute | solution.py:62
  47.5 1.5 %fusion = f32[5,1,512,128]{3,2,1,0:T(8,128)S(1)} fusion(f32[5,1,512,128]{3,2,1,0:T(8,128)S(1)} %get-tuple-element.27, f32[1,512,128]{2,1,0:T(8,128)} %collective-permute-done.7, f32[1,256,256]{2,1,0:T(8,128)S(1)} %copy-done.7, f32[1,256,256]{2,1,0:T(8,128)S(1)} %get-tuple-element.19, f32[1,256,256]{2,1,0:T(8,128)S(1)} %fusion.46), kind=kOutput, calls=%fused_computation.6 | convolution fusion | flops 202113024 | bytes 1310720 | tf_op jit(solution)/shard_map/mab,mbw->maw/dot_general | solution.py:77
  51.9 1.3 %subtract_bitcast_fusion = f32[1,4]{1,0:T(1,128)S(1)} fusion(f32[4]{0:T(128)S(1)} %get-tuple-element.6, f32[4]{0:T(128)S(1)} %get-tuple-element.5, f32[]{:T(128)} %get-tuple-element.9, f32[]{:T(128)} %get-tuple-element.13), kind=kLoop, calls=%fused_computation.70 | loop fusion | flops 12 | bytes 56 | tf_op jit(solution)/shard_map/sub | solution.py:98
  53.2 1.1 %collective-permute-done.8 = f32[1,4]{1,0:T(1,128)S(1)} collective-permute-done((f32[1,4]{1,0:T(1,128)S(1)}, f32[1,4]{1,0:T(1,128)S(1)}, u32[]{:S(2)}, u32[]{:S(2)}) %collective-permute-start.8) | collective-permute-done | bytes 48 | tf_op jit(solution)/shard_map/ppermute | solution.py:31
  54.3 1.3 %collective-permute-start.9 = (f32[1,4]{1,0:T(1,128)S(1)}, f32[1,4]{1,0:T(1,128)S(1)}, u32[]{:S(2)}, u32[]{:S(2)}) collective-permute-start(f32[1,4]{1,0:T(1,128)S(1)} %add.43), channel_id=1, source_target_pairs={{0,2},{2,0},{1,3},{3,1},{4,6},{6,4},{5,7},{7,5},{8,10},{10,8},{9,1... | collective-permute-start | bytes 56 | tf_op jit(solution)/shard_map/ppermute | solution.py:31
  55.7 2.2 %collective-permute-done.9 = f32[1,4]{1,0:T(1,128)S(1)} collective-permute-done((f32[1,4]{1,0:T(1,128)S(1)}, f32[1,4]{1,0:T(1,128)S(1)}, u32[]{:S(2)}, u32[]{:S(2)}) %collective-permute-start.9) | collective-permute-done | bytes 48 | tf_op jit(solution)/shard_map/ppermute | solution.py:31
  (47 shorter events, 7.5 us)
Async XLA Ops:
  0.0 2.2 %copy-start.2 = (f32[2,256,256]{2,1,0:T(8,128)S(1)}, f32[2,256,256]{2,1,0:T(8,128)}, u32[]{:S(2)}) copy-start(f32[2,256,256]{2,1,0:T(8,128)} %param.5) | copy-start | bytes 1572868
  1.1 1.5 %copy-start.5 = (f32[1,256,256]{2,1,0:T(8,128)}, f32[1,256,256]{2,1,0:T(8,128)S(1)}, u32[]{:S(2)}) copy-start(f32[1,256,256]{2,1,0:T(8,128)S(1)} %get-tuple-element.20) | copy-start | bytes 786436
  2.6 2.4 %copy-start = (f32[1,1,2,256,256]{4,3,2,1,0:T(8,128)S(1)}, f32[1,1,2,256,256]{4,3,2,1,0:T(8,128)}, u32[]{:S(2)}) copy-start(f32[1,1,2,256,256]{4,3,2,1,0:T(8,128)} %param.3) | copy-start | bytes 1572868
  3.7 11.4 %collective-permute-start = (f32[1,128,512]{2,1,0:T(8,128)}, f32[1,128,512]{2,1,0:T(8,128)S(1)}, u32[]{:S(2)}, u32[]{:S(2)}) collective-permute-start(f32[1,128,512]{2,1,0:T(8,128)} %convolution_bitcast_fusion.5), channel_id=1, source_target_pairs={{4,0},{8,4},{12,8},{5,1},{9,5},{13,9},{6,2},{10,6},{14,10},{7,3},{... | collective-permute-start | bytes 786440 | tf_op jit(solution)/shard_map/ppermute | solution.py:63
  5.7 12.2 %collective-permute-start.4 = (f32[1,512,128]{2,1,0:T(8,128)S(1)}, f32[1,512,128]{2,1,0:T(8,128)}, u32[]{:S(2)}, u32[]{:S(2)}) collective-permute-start(f32[1,512,128]{2,1,0:T(8,128)S(1)} %pad_maximum_fusion.5), channel_id=1, source_target_pairs={{0,4},{4,8},{8,12},{1,5},{5,9},{9,13},{2,6},{6,10},{10,14},{3,7},{... | collective-permute-start | bytes 786440 | tf_op jit(solution)/shard_map/ppermute | solution.py:62
  12.0 4.2 %copy-start.6 = (f32[1,256,256]{2,1,0:T(8,128)S(1)}, f32[1,256,256]{2,1,0:T(8,128)}, u32[]{:S(2)}) copy-start(f32[1,256,256]{2,1,0:T(8,128)} %copy-done.5) | copy-start | bytes 786436
  12.1 5.9 %copy-start.8 = (f32[256,128]{1,0:T(8,128)S(1)}, f32[256,128]{1,0:T(8,128)}, u32[]{:S(2)}) copy-start(f32[256,128]{1,0:T(8,128)} %get-tuple-element.16) | copy-start | bytes 393220
  15.2 1.1 %copy-start.3 = (f32[5,1,128,512]{3,2,1,0:T(8,128)}, f32[5,1,128,512]{3,2,1,0:T(8,128)S(1)}, u32[]{:S(2)}) copy-start(f32[5,1,128,512]{3,2,1,0:T(8,128)S(1)} %get-tuple-element.11) | copy-start | bytes 3932164
  16.7 9.4 %collective-permute-start.1 = (f32[1,128,512]{2,1,0:T(8,128)S(1)}, f32[1,128,512]{2,1,0:T(8,128)S(1)}, u32[]{:S(2)}, u32[]{:S(2)}) collective-permute-start(f32[1,128,512]{2,1,0:T(8,128)S(1)} %convolution_bitcast_fusion.4), channel_id=1, source_target_pairs={{4,0},{8,4},{12,8},{5,1},{9,5},{13,9},{6,2},{10,6},{14,10},{7,3},{... | collective-permute-start | bytes 786440 | tf_op jit(solution)/shard_map/ppermute | solution.py:63
  19.5 9.3 %collective-permute-start.5 = (f32[1,512,128]{2,1,0:T(8,128)S(1)}, f32[1,512,128]{2,1,0:T(8,128)S(1)}, u32[]{:S(2)}, u32[]{:S(2)}) collective-permute-start(f32[1,512,128]{2,1,0:T(8,128)S(1)} %bitcast.166), channel_id=1, source_target_pairs={{0,4},{4,8},{8,12},{1,5},{5,9},{9,13},{2,6},{6,10},{10,14},{3,7},{... | collective-permute-start | bytes 786440 | tf_op jit(solution)/shard_map/ppermute | solution.py:62
  26.5 7.3 %copy-start.4 = (f32[5,1,128,512]{3,2,1,0:T(8,128)S(1)}, f32[5,1,128,512]{3,2,1,0:T(8,128)}, u32[]{:S(2)}) copy-start(f32[5,1,128,512]{3,2,1,0:T(8,128)} %copy-done.3) | copy-start | bytes 3932164
  26.5 8.6 %collective-permute-start.2 = (f32[1,128,512]{2,1,0:T(8,128)S(1)}, f32[1,128,512]{2,1,0:T(8,128)S(1)}, u32[]{:S(2)}, u32[]{:S(2)}) collective-permute-start(f32[1,128,512]{2,1,0:T(8,128)S(1)} %convolution_bitcast_fusion.3), channel_id=1, source_target_pairs={{4,0},{8,4},{12,8},{5,1},{9,5},{13,9},{6,2},{10,6},{14,10},{7,3},{... | collective-permute-start | bytes 786440 | tf_op jit(solution)/shard_map/ppermute | solution.py:63
  29.4 8.3 %collective-permute-start.6 = (f32[1,512,128]{2,1,0:T(8,128)S(1)}, f32[1,512,128]{2,1,0:T(8,128)S(1)}, u32[]{:S(2)}, u32[]{:S(2)}) collective-permute-start(f32[1,512,128]{2,1,0:T(8,128)S(1)} %bitcast.167), channel_id=1, source_target_pairs={{0,4},{4,8},{8,12},{1,5},{5,9},{9,13},{2,6},{6,10},{10,14},{3,7},{... | collective-permute-start | bytes 786440 | tf_op jit(solution)/shard_map/ppermute | solution.py:62
  35.5 8.6 %collective-permute-start.3 = (f32[1,128,512]{2,1,0:T(8,128)S(1)}, f32[1,128,512]{2,1,0:T(8,128)S(1)}, u32[]{:S(2)}, u32[]{:S(2)}) collective-permute-start(f32[1,128,512]{2,1,0:T(8,128)S(1)} %convolution_bitcast_fusion.2), channel_id=1, source_target_pairs={{4,0},{8,4},{12,8},{5,1},{9,5},{13,9},{6,2},{10,6},{14,10},{7,3},{... | collective-permute-start | bytes 786440 | tf_op jit(solution)/shard_map/ppermute | solution.py:63
  38.9 8.6 %collective-permute-start.7 = (f32[1,512,128]{2,1,0:T(8,128)}, f32[1,512,128]{2,1,0:T(8,128)}, u32[]{:S(2)}, u32[]{:S(2)}) collective-permute-start(f32[1,512,128]{2,1,0:T(8,128)} %bitcast.37), channel_id=1, source_target_pairs={{0,4},{4,8},{8,12},{1,5},{5,9},{9,13},{2,6},{6,10},{10,14},{3,7},{... | collective-permute-start | bytes 786440 | tf_op jit(solution)/shard_map/ppermute | solution.py:62
  44.0 3.5 %copy-start.7 = (f32[1,256,256]{2,1,0:T(8,128)S(1)}, f32[1,256,256]{2,1,0:T(8,128)}, u32[]{:S(2)}) copy-start(f32[1,256,256]{2,1,0:T(8,128)} %copy-done.5) | copy-start | bytes 786436
  49.7 1.6 %copy-start.1 = (f32[4,2,256,256]{3,2,1,0:T(8,128)S(1)}, f32[4,2,256,256]{3,2,1,0:T(8,128)}, u32[]{:S(2)}) copy-start(f32[4,2,256,256]{3,2,1,0:T(8,128)} %param.4) | copy-start | bytes 6291460
  53.2 1.2 %collective-permute-start.8 = (f32[1,4]{1,0:T(1,128)S(1)}, f32[1,4]{1,0:T(1,128)S(1)}, u32[]{:S(2)}, u32[]{:S(2)}) collective-permute-start(f32[1,4]{1,0:T(1,128)S(1)} %subtract_bitcast_fusion), channel_id=1, source_target_pairs={{0,1},{1,0},{2,3},{3,2},{4,5},{5,4},{6,7},{7,6},{8,9},{9,8},{10,11... | collective-permute-start | bytes 56 | tf_op jit(solution)/shard_map/ppermute | solution.py:31
  54.3 3.5 %collective-permute-start.9 = (f32[1,4]{1,0:T(1,128)S(1)}, f32[1,4]{1,0:T(1,128)S(1)}, u32[]{:S(2)}, u32[]{:S(2)}) collective-permute-start(f32[1,4]{1,0:T(1,128)S(1)} %add.43), channel_id=1, source_target_pairs={{0,2},{2,0},{1,3},{3,1},{4,6},{6,4},{5,7},{7,5},{8,10},{10,8},{9,1... | collective-permute-start | bytes 56 | tf_op jit(solution)/shard_map/ppermute | solution.py:31

commit v5 on v4

--- a/solution.py
+++ b/solution.py
@@ -33,6 +33,15 @@
     return value
 
 
+def member_sum(value):
+    axes = ("member", "sub")
+    count = lax.axis_size("member") * lax.axis_size("sub")
+    if count != 4:
+        return butterfly_sum(value, ("sub", "member"))
+    got = [lax.ppermute(value, axes, [(i, i ^ d) for i in range(4)]) for d in (1, 2, 3)]
+    return (value + got[0]) + (got[1] + got[2])
+
+
 def per_device(slices, controls, target):
     members_here = slices.shape[0]
     order = slices.shape[-1]
@@ -56,25 +65,26 @@
     steps = chunks + blocks - 1
     for step in range(steps):
         if step == 0:
-            fwd_in = jnp.zeros((members_here, 2 * order, width), jnp.float32)
+            fwd_in = jnp.zeros((members_here, width, 2 * order), jnp.float32)
             bwd_in = jnp.zeros((members_here, width, 2 * order), jnp.float32)
         else:
             fwd_in = lax.ppermute(fwd_out, "tm", right_pairs)
             bwd_in = lax.ppermute(bwd_out, "tm", left_pairs)
         if step < chunks:
             cols = slice(step * width, (step + 1) * width)
-            own_cols = jnp.concatenate([unit[:, 0, :, cols], unit[:, 1, :, cols]], axis=-2)
+            own_cols = jnp.swapaxes(
+                jnp.concatenate([unit[:, 0, :, cols], unit[:, 1, :, cols]], axis=-2), -1, -2)
             rows = jnp.broadcast_to(target_dag[None, step * width:(step + 1) * width], bwd_in.shape)
             if step == 0:
                 fwd_new = own_cols
             else:
                 fwd_new = jnp.where(
                     is_first, own_cols,
-                    jnp.einsum("mab,mbw->maw", left_op, fwd_in, precision=HIGH),
+                    jnp.einsum("mwb,mab->mwa", fwd_in, left_op, precision=HIGH),
                 )
             bwd_in = jnp.where(is_last, rows, bwd_in)
         else:
-            fwd_new = jnp.einsum("mab,mbw->maw", left_op, fwd_in, precision=HIGH)
+            fwd_new = jnp.einsum("mwb,mab->mwa", fwd_in, left_op, precision=HIGH)
         fwd_steps.append(fwd_new)
         bwd_steps.append(bwd_in)
         fwd_out = fwd_new
@@ -83,9 +93,9 @@
 
     fwd_all = lax.dynamic_slice_in_dim(jnp.stack(fwd_steps), position, chunks, 0)
     bwd_all = lax.dynamic_slice_in_dim(jnp.stack(bwd_steps), blocks - 1 - position, chunks, 0)
-    fwd_all = fwd_all.reshape(chunks, members_here, 2, order, width)
+    fwd_all = fwd_all.reshape(chunks, members_here, width, 2, order)
     bwd_all = bwd_all.reshape(chunks, members_here, width, 2, order)
-    parts = jnp.einsum("cmpaw,cmwqb->mpqab", fwd_all, bwd_all, precision=HIGH)
+    parts = jnp.einsum("cmwpa,cmwqb->mpqab", fwd_all, bwd_all, precision=HIGH)
     q_re = parts[:, 0, 0] - parts[:, 1, 1]
     q_im = parts[:, 0, 1] + parts[:, 1, 0]
     eye = jnp.eye(order, dtype=bool)
@@ -97,7 +107,7 @@
     s_im = jnp.sum(q_im[:, None] * h_re - q_re[:, None] * h_im, axis=(-2, -1))
     terms = over_re[:, None] * s_im - over_im[:, None] * s_re
     partial_value = jnp.sum(terms, axis=0, keepdims=True)
-    total = butterfly_sum(partial_value, ("sub", "member"))
+    total = member_sum(partial_value)
     member_count = members_here * lax.axis_size("member") * lax.axis_size("sub")
     return total * (2.0 / member_count)
 

time: 58.9 us -> 58.6 us (level)
  waiting for transfers between devices: 14.5 us -> 13.4 us
  other arithmetic: 4.19 us -> 3.14 us
  starting transfers between devices: 27 us -> 27.9 us
  local copies, waits for them, and re-layouts: 4.44 us -> 5.14 us
    ppermute x4, waiting for transfers between devices: 4.92 us -> 3.13 us  [per_device(): fwd_in = lax.ppermute(fwd_out, 'tm', right_pairs)]
    unnamed x22 -> x21, local copies, waits for them, and re-layouts: 2.02 us -> 3.61 us
    ppermute x4, waiting for transfers between devices: 6.26 us -> 7.58 us  [per_device(): bwd_in = lax.ppermute(bwd_out, 'tm', left_pairs)]
    squeeze x1, local copies, waits for them, and re-layouts: 1.12 us -> 0.04 us  [block_right(): top = jnp.concatenate([u[:, 0], u[:, 1]], axis=-1)]
    neg x1, other arithmetic: 1.07 us -> 0.02 us  [block_right(): bottom = jnp.concatenate([-u[:, 1], u[:, 0]], axis=-1)]
    dot_general x4, matrix products: 2.35 us -> 3.28 us  [per_device(): bwd_out = jnp.einsum('mwa,mab->mwb', bwd_in, right_op, precision=HIGH)]
    ppermute x2 -> x3, starting transfers between devices: 1.41 us -> 2.2 us  [member_sum(): lax.ppermute(value, axes, [(i, i ^ d) for i in range(4)])]
    squeeze x0 -> x1, local copies, waits for them, and re-layouts: none -> 0.72 us  [per_device(): unit[:, 0, :, cols]]
  transfers between devices with their start and end apart: 10 -> 11, of which waited for: 8 -> 8; matrix products, arithmetic and copies ran while one was open for 10% -> 10% of each run, Pallas kernels for 0% -> 0%
where the time goes in v5:
time: 58.6 us; the launch traced here: 58.2 us
  starting transfers between devices  27.9 us (48%)
  waiting for transfers between devices  13.4 us (23%)
  matrix products  8.14 us (14%)
  local copies, waits for them, and re-layouts  5.14 us (9%)
  other arithmetic  3.14 us (5%)
    ppermute x4, starting transfers between devices, per_device(): fwd_in = lax.ppermute(fwd_out, 'tm', right_pairs)  20.5 us
    ppermute x4, waiting for transfers between devices, per_device(): bwd_in = lax.ppermute(bwd_out, 'tm', left_pairs)  7.58 us
    ppermute x4, starting transfers between devices, per_device(): bwd_in = lax.ppermute(bwd_out, 'tm', left_pairs)  5.29 us
    unnamed x21, local copies, waits for them, and re-layouts  3.61 us
    dot_general x4, matrix products, per_device(): bwd_out = jnp.einsum('mwa,mab->mwb', bwd_in, right_op, precision=HIGH)  3.28 us
    ppermute x4, waiting for transfers between devices, per_device(): fwd_in = lax.ppermute(fwd_out, 'tm', right_pairs)  3.13 us
    dot_general x3, matrix products, per_device(): fwd_new = jnp.einsum('mwb,mab->mwa', fwd_in, left_op, precision=HIGH)  2.86 us
    ppermute x3, waiting for transfers between devices, member_sum(): lax.ppermute(value, axes, [(i, i ^ d) for i in range(4)])  2.7 us
  transfers between devices with their start and end apart: 11, of which 8 were waited for; matrix products, arithmetic and copies ran while one was open for 10% of the time, Pallas kernels for 0%

profile of v5, /device:TPU:0, one launch (start us, length us, event | category | flops | bytes accessed | tf_op | source)
XLA Modules:
  0.0 58.2 jit_solution(16285724900365915855)
XLA Ops:
  0.0 1.3 %copy.14 = f32[1,1,2,256,256]{3,4,2,1,0:T(8,128)S(1)} copy(f32[1,1,2,256,256]{4,3,2,1,0:T(8,128)} %param.3) | data formatting | bytes 1048576 | tf_op args[0]
  2.1 1.4 %convolution_bitcast_fusion.6 = f32[1,128,512]{2,1,0:T(8,128)} fusion(f32[1,256,256]{1,2,0:T(8,128)S(1)} %get-tuple-element.18, f32[1,256,256]{1,2,0:T(8,128)S(1)} %fusion.47, f32[1,256,256]{1,2,0:T(8,128)S(1)} %get-tuple-element.17, f32[256,256]{1,0:T(8,128)S(1)} %bitcast.170, f32[256,256]{1,0:T(8,128)S(1)} %negate_bitcast_fusion, pred[]{:T(512)S(6)} %eq.16), kind=kOutput, calls=%fused_computation.11 | convolution fusion | flops 202244096 | bytes 1572865 | tf_op jit(solution)/shard_map/mwa,mab->mwb/dot_general | solution.py:92
  3.4 1.3 %collective-permute-start = (f32[1,128,512]{2,1,0:T(8,128)}, f32[1,128,512]{2,1,0:T(8,128)S(1)}, u32[]{:S(2)}, u32[]{:S(2)}) collective-permute-start(f32[1,128,512]{2,1,0:T(8,128)} %convolution_bitcast_fusion.6), channel_id=1, source_target_pairs={{4,0},{8,4},{12,8},{5,1},{9,5},{13,9},{6,2},{10,6},{14,10},{7,3},{... | collective-permute-start | bytes 786440 | tf_op jit(solution)/shard_map/ppermute | solution.py:72
  4.7 0.7 %slice_bitcast_fusion.5 = (f32[1,256,128]{1,2,0:T(8,128)S(1)}, f32[1,256,128]{1,2,0:T(8,128)}, f32[1,256,128]{1,2,0:T(8,128)S(1)}, f32[1,256,128]{1,2,0:T(8,128)S(1)}) fusion(f32[1,2,256,256]{2,3,1,0:T(8,128)S(1)} %bitcast.169), kind=kLoop, calls=%fused_computation.68 | loop fusion | bytes 1048576 | tf_op jit(solution)/shard_map/squeeze | solution.py:76
  5.4 6.3 %collective-permute-start.4 = (f32[1,128,512]{2,1,0:T(8,128)S(1)}, f32[1,128,512]{2,1,0:T(8,128)}, u32[]{:S(2)}, u32[]{:S(2)}) collective-permute-start(f32[1,128,512]{2,1,0:T(8,128)S(1)} %fusion.28), channel_id=1, source_target_pairs={{0,4},{4,8},{8,12},{1,5},{5,9},{9,13},{2,6},{6,10},{10,14},{3,7},{... | collective-permute-start | bytes 786440 | tf_op jit(solution)/shard_map/ppermute | solution.py:71
  11.8 3.1 %collective-permute-done = f32[1,128,512]{2,1,0:T(8,128)S(1)} collective-permute-done((f32[1,128,512]{2,1,0:T(8,128)}, f32[1,128,512]{2,1,0:T(8,128)S(1)}, u32[]{:S(2)}, u32[]{:S(2)}) %collective-permute-start) | collective-permute-done | bytes 262176 | tf_op jit(solution)/shard_map/ppermute | solution.py:72
  14.9 1.1 %copy-done.2 = f32[5,1,128,512]{3,2,1,0:T(8,128)} copy-done((f32[5,1,128,512]{3,2,1,0:T(8,128)}, f32[5,1,128,512]{3,2,1,0:T(8,128)S(1)}, u32[]{:S(2)}) %copy-start.2) | copy-done | bytes 1310744
  16.6 1.3 %collective-permute-start.1 = (f32[1,128,512]{2,1,0:T(8,128)S(1)}, f32[1,128,512]{2,1,0:T(8,128)S(1)}, u32[]{:S(2)}, u32[]{:S(2)}) collective-permute-start(f32[1,128,512]{2,1,0:T(8,128)S(1)} %convolution_bitcast_fusion.5), channel_id=1, source_target_pairs={{4,0},{8,4},{12,8},{5,1},{9,5},{13,9},{6,2},{10,6},{14,10},{7,3},{... | collective-permute-start | bytes 786440 | tf_op jit(solution)/shard_map/ppermute | solution.py:72
  17.9 1.4 %bitcast_dynamic-update-slice_fusion.3 = (f32[5,1,128,512]{3,2,1,0:T(8,128)S(1)}, f32[1,128,512]{2,1,0:T(8,128)S(1)}) fusion(f32[5,1,128,512]{3,2,1,0:T(8,128)S(1)} %bitcast_dynamic-update-slice_fusion, f32[1,256,256]{1,2,0:T(8,128)S(1)} %copy-done.5, f32[1,256,256]{1,2,0:T(8,128)S(1)} %get-tuple-element.17, f32[1,256,256]{1,2,0:T(8,128)S(1)} %fusion.47, ...), kind=kOutput, calls=%fused_computation.52 | convolution fusion | flops 202244096 | bytes 1835009 | tf_op jit(solution)/shard_map/mwb,mab->mwa/dot_general | solution.py:83
  19.3 4.6 %collective-permute-start.5 = (f32[1,128,512]{2,1,0:T(8,128)S(1)}, f32[1,128,512]{2,1,0:T(8,128)S(1)}, u32[]{:S(2)}, u32[]{:S(2)}) collective-permute-start(f32[1,128,512]{2,1,0:T(8,128)S(1)} %get-tuple-element.24), channel_id=1, source_target_pairs={{0,4},{4,8},{8,12},{1,5},{5,9},{9,13},{2,6},{6,10},{10,14},{3,7},{... | collective-permute-start | bytes 786440 | tf_op jit(solution)/shard_map/ppermute | solution.py:71
  23.9 2.1 %collective-permute-done.1 = f32[1,128,512]{2,1,0:T(8,128)S(1)} collective-permute-done((f32[1,128,512]{2,1,0:T(8,128)S(1)}, f32[1,128,512]{2,1,0:T(8,128)S(1)}, u32[]{:S(2)}, u32[]{:S(2)}) %collective-permute-start.1) | collective-permute-done | bytes 262176 | tf_op jit(solution)/shard_map/ppermute | solution.py:72
  26.7 1.4 %collective-permute-start.2 = (f32[1,128,512]{2,1,0:T(8,128)S(1)}, f32[1,128,512]{2,1,0:T(8,128)S(1)}, u32[]{:S(2)}, u32[]{:S(2)}) collective-permute-start(f32[1,128,512]{2,1,0:T(8,128)S(1)} %convolution_bitcast_fusion.4), channel_id=1, source_target_pairs={{4,0},{8,4},{12,8},{5,1},{9,5},{13,9},{6,2},{10,6},{14,10},{7,3},{... | collective-permute-start | bytes 786440 | tf_op jit(solution)/shard_map/ppermute | solution.py:72
  29.0 4.4 %collective-permute-start.6 = (f32[1,128,512]{2,1,0:T(8,128)S(1)}, f32[1,128,512]{2,1,0:T(8,128)S(1)}, u32[]{:S(2)}, u32[]{:S(2)}) collective-permute-start(f32[1,128,512]{2,1,0:T(8,128)S(1)} %bitcast.175), channel_id=1, source_target_pairs={{0,4},{4,8},{8,12},{1,5},{5,9},{9,13},{2,6},{6,10},{10,14},{3,7},{... | collective-permute-start | bytes 786440 | tf_op jit(solution)/shard_map/ppermute | solution.py:71
  33.4 1.8 %collective-permute-done.2 = f32[1,128,512]{2,1,0:T(8,128)S(1)} collective-permute-done((f32[1,128,512]{2,1,0:T(8,128)S(1)}, f32[1,128,512]{2,1,0:T(8,128)S(1)}, u32[]{:S(2)}, u32[]{:S(2)}) %collective-permute-start.2) | collective-permute-done | bytes 262176 | tf_op jit(solution)/shard_map/ppermute | solution.py:72
  35.9 1.3 %collective-permute-start.3 = (f32[1,128,512]{2,1,0:T(8,128)S(1)}, f32[1,128,512]{2,1,0:T(8,128)S(1)}, u32[]{:S(2)}, u32[]{:S(2)}) collective-permute-start(f32[1,128,512]{2,1,0:T(8,128)S(1)} %convolution_bitcast_fusion.3), channel_id=1, source_target_pairs={{4,0},{8,4},{12,8},{5,1},{9,5},{13,9},{6,2},{10,6},{14,10},{7,3},{... | collective-permute-start | bytes 786440 | tf_op jit(solution)/shard_map/ppermute | solution.py:72
  37.2 1.1 %bitcast_dynamic-update-slice_fusion.1 = (f32[5,1,128,512]{3,2,1,0:T(8,128)S(1)}, f32[128,512]{1,0:T(8,128)}) fusion(f32[5,1,128,512]{3,2,1,0:T(8,128)S(1)} %get-tuple-element.25, f32[1,256,256]{1,2,0:T(8,128)S(1)} %copy-done.5, f32[1,256,256]{1,2,0:T(8,128)S(1)} %get-tuple-element.17, f32[1,256,256]{1,2,0:T(8,128)S(1)} %fusion.47, ...), kind=kOutput, calls=%fused_computation.46 | convolution fusion | flops 202113024 | bytes 1572864 | tf_op jit(solution)/shard_map/mwb,mab->mwa/dot_general | solution.py:87
  38.4 5.2 %collective-permute-start.7 = (f32[1,128,512]{2,1,0:T(8,128)}, f32[1,128,512]{2,1,0:T(8,128)}, u32[]{:S(2)}, u32[]{:S(2)}) collective-permute-start(f32[1,128,512]{2,1,0:T(8,128)} %bitcast.39), channel_id=1, source_target_pairs={{0,4},{4,8},{8,12},{1,5},{5,9},{9,13},{2,6},{6,10},{10,14},{3,7},{... | collective-permute-start | bytes 786440 | tf_op jit(solution)/shard_map/ppermute | solution.py:71
  44.4 2.6 %collective-permute-done.7 = f32[1,128,512]{2,1,0:T(8,128)} collective-permute-done((f32[1,128,512]{2,1,0:T(8,128)}, f32[1,128,512]{2,1,0:T(8,128)}, u32[]{:S(2)}, u32[]{:S(2)}) %collective-permute-start.7) | collective-permute-done | bytes 262176 | tf_op jit(solution)/shard_map/ppermute | solution.py:71
  47.1 1.4 %fusion = f32[5,1,128,512]{3,2,1,0:T(8,128)S(1)} fusion(f32[5,1,128,512]{3,2,1,0:T(8,128)S(1)} %get-tuple-element.27, f32[1,128,512]{2,1,0:T(8,128)} %collective-permute-done.7, f32[1,256,256]{1,2,0:T(8,128)S(1)} %copy-done.6, f32[1,256,256]{1,2,0:T(8,128)S(1)} %get-tuple-element.17, f32[1,256,256]{1,2,0:T(8,128)S(1)} %fusion.47), kind=kOutput, calls=%fused_computation.6 | convolution fusion | flops 202113024 | bytes 1310720 | tf_op jit(solution)/shard_map/mwb,mab->mwa/dot_general | solution.py:87
  51.4 1.3 %subtract_bitcast_fusion = f32[1,4]{1,0:T(1,128)S(1)} fusion(f32[4]{0:T(128)S(1)} %get-tuple-element.6, f32[4]{0:T(128)S(1)} %get-tuple-element.5, f32[]{:T(128)} %get-tuple-element.9, f32[]{:T(128)} %get-tuple-element.13), kind=kLoop, calls=%fused_computation.72 | loop fusion | flops 12 | bytes 56 | tf_op jit(solution)/shard_map/sub | solution.py:108
  52.8 1.3 %collective-permute-start.8 = (f32[1,4]{1,0:T(1,128)S(1)}, f32[1,4]{1,0:T(1,128)S(1)}, u32[]{:S(2)}, u32[]{:S(2)}) collective-permute-start(f32[1,4]{1,0:T(1,128)S(1)} %subtract_bitcast_fusion), channel_id=1, source_target_pairs={{0,1},{1,0},{2,3},{3,2},{4,5},{5,4},{6,7},{7,6},{8,9},{9,8},{10,11... | collective-permute-start | bytes 56 | tf_op jit(solution)/shard_map/ppermute | solution.py:41
  54.1 0.8 %collective-permute-start.9 = (f32[1,4]{1,0:T(1,128)S(1)}, f32[1,4]{1,0:T(1,128)S(1)}, u32[]{:S(2)}, u32[]{:S(2)}) collective-permute-start(f32[1,4]{1,0:T(1,128)S(1)} %subtract_bitcast_fusion), channel_id=1, source_target_pairs={{0,2},{1,3},{2,0},{3,1},{4,6},{5,7},{6,4},{7,5},{8,10},{9,11},{10,... | collective-permute-start | bytes 56 | tf_op jit(solution)/shard_map/ppermute | solution.py:41
  54.9 0.8 %collective-permute-done.10 = f32[1,4]{1,0:T(1,128)S(1)} collective-permute-done((f32[1,4]{1,0:T(1,128)S(1)}, f32[1,4]{1,0:T(1,128)S(1)}, u32[]{:S(2)}, u32[]{:S(2)}) %collective-permute-start.10) | collective-permute-done | bytes 48 | tf_op jit(solution)/shard_map/ppermute | solution.py:41
  55.8 1.9 %collective-permute-done.9 = f32[1,4]{1,0:T(1,128)S(1)} collective-permute-done((f32[1,4]{1,0:T(1,128)S(1)}, f32[1,4]{1,0:T(1,128)S(1)}, u32[]{:S(2)}, u32[]{:S(2)}) %collective-permute-start.9) | collective-permute-done | bytes 48 | tf_op jit(solution)/shard_map/ppermute | solution.py:41
  (48 shorter events, 8.1 us)
Async XLA Ops:
  0.0 1.4 %copy-start.1 = (f32[2,256,256]{2,1,0:T(8,128)S(1)}, f32[2,256,256]{2,1,0:T(8,128)}, u32[]{:S(2)}) copy-start(f32[2,256,256]{2,1,0:T(8,128)} %param.5) | copy-start | bytes 1572868
  1.3 0.7 %copy-start.4 = (f32[1,256,256]{1,2,0:T(8,128)}, f32[1,256,256]{1,2,0:T(8,128)S(1)}, u32[]{:S(2)}) copy-start(f32[1,256,256]{1,2,0:T(8,128)S(1)} %get-tuple-element.18) | copy-start | bytes 786436
  3.4 11.4 %collective-permute-start = (f32[1,128,512]{2,1,0:T(8,128)}, f32[1,128,512]{2,1,0:T(8,128)S(1)}, u32[]{:S(2)}, u32[]{:S(2)}) collective-permute-start(f32[1,128,512]{2,1,0:T(8,128)} %convolution_bitcast_fusion.6), channel_id=1, source_target_pairs={{4,0},{8,4},{12,8},{5,1},{9,5},{13,9},{6,2},{10,6},{14,10},{7,3},{... | collective-permute-start | bytes 786440 | tf_op jit(solution)/shard_map/ppermute | solution.py:72
  5.4 12.5 %collective-permute-start.4 = (f32[1,128,512]{2,1,0:T(8,128)S(1)}, f32[1,128,512]{2,1,0:T(8,128)}, u32[]{:S(2)}, u32[]{:S(2)}) collective-permute-start(f32[1,128,512]{2,1,0:T(8,128)S(1)} %fusion.28), channel_id=1, source_target_pairs={{0,4},{4,8},{8,12},{1,5},{5,9},{9,13},{2,6},{6,10},{10,14},{3,7},{... | collective-permute-start | bytes 786440 | tf_op jit(solution)/shard_map/ppermute | solution.py:71
  11.7 4.2 %copy-start.5 = (f32[1,256,256]{1,2,0:T(8,128)S(1)}, f32[1,256,256]{1,2,0:T(8,128)}, u32[]{:S(2)}) copy-start(f32[1,256,256]{1,2,0:T(8,128)} %copy-done.4) | copy-start | bytes 786436
  11.8 6.1 %copy-start.7 = (f32[1,256,128]{1,2,0:T(8,128)S(1)}, f32[1,256,128]{1,2,0:T(8,128)}, u32[]{:S(2)}) copy-start(f32[1,256,128]{1,2,0:T(8,128)} %get-tuple-element.20) | copy-start | bytes 393220
  14.9 1.1 %copy-start.2 = (f32[5,1,128,512]{3,2,1,0:T(8,128)}, f32[5,1,128,512]{3,2,1,0:T(8,128)S(1)}, u32[]{:S(2)}) copy-start(f32[5,1,128,512]{3,2,1,0:T(8,128)S(1)} %get-tuple-element.11) | copy-start | bytes 3932164
  16.6 9.4 %collective-permute-start.1 = (f32[1,128,512]{2,1,0:T(8,128)S(1)}, f32[1,128,512]{2,1,0:T(8,128)S(1)}, u32[]{:S(2)}, u32[]{:S(2)}) collective-permute-start(f32[1,128,512]{2,1,0:T(8,128)S(1)} %convolution_bitcast_fusion.5), channel_id=1, source_target_pairs={{4,0},{8,4},{12,8},{5,1},{9,5},{13,9},{6,2},{10,6},{14,10},{7,3},{... | collective-permute-start | bytes 786440 | tf_op jit(solution)/shard_map/ppermute | solution.py:72
  19.3 9.3 %collective-permute-start.5 = (f32[1,128,512]{2,1,0:T(8,128)S(1)}, f32[1,128,512]{2,1,0:T(8,128)S(1)}, u32[]{:S(2)}, u32[]{:S(2)}) collective-permute-start(f32[1,128,512]{2,1,0:T(8,128)S(1)} %get-tuple-element.24), channel_id=1, source_target_pairs={{0,4},{4,8},{8,12},{1,5},{5,9},{9,13},{2,6},{6,10},{10,14},{3,7},{... | collective-permute-start | bytes 786440 | tf_op jit(solution)/shard_map/ppermute | solution.py:71
  26.6 6.7 %copy-start.3 = (f32[5,1,128,512]{3,2,1,0:T(8,128)S(1)}, f32[5,1,128,512]{3,2,1,0:T(8,128)}, u32[]{:S(2)}) copy-start(f32[5,1,128,512]{3,2,1,0:T(8,128)} %copy-done.2) | copy-start | bytes 3932164
  26.7 8.6 %collective-permute-start.2 = (f32[1,128,512]{2,1,0:T(8,128)S(1)}, f32[1,128,512]{2,1,0:T(8,128)S(1)}, u32[]{:S(2)}, u32[]{:S(2)}) collective-permute-start(f32[1,128,512]{2,1,0:T(8,128)S(1)} %convolution_bitcast_fusion.4), channel_id=1, source_target_pairs={{4,0},{8,4},{12,8},{5,1},{9,5},{13,9},{6,2},{10,6},{14,10},{7,3},{... | collective-permute-start | bytes 786440 | tf_op jit(solution)/shard_map/ppermute | solution.py:72
  29.0 8.3 %collective-permute-start.6 = (f32[1,128,512]{2,1,0:T(8,128)S(1)}, f32[1,128,512]{2,1,0:T(8,128)S(1)}, u32[]{:S(2)}, u32[]{:S(2)}) collective-permute-start(f32[1,128,512]{2,1,0:T(8,128)S(1)} %bitcast.175), channel_id=1, source_target_pairs={{0,4},{4,8},{8,12},{1,5},{5,9},{9,13},{2,6},{6,10},{10,14},{3,7},{... | collective-permute-start | bytes 786440 | tf_op jit(solution)/shard_map/ppermute | solution.py:71
  35.9 8.3 %collective-permute-start.3 = (f32[1,128,512]{2,1,0:T(8,128)S(1)}, f32[1,128,512]{2,1,0:T(8,128)S(1)}, u32[]{:S(2)}, u32[]{:S(2)}) collective-permute-start(f32[1,128,512]{2,1,0:T(8,128)S(1)} %convolution_bitcast_fusion.3), channel_id=1, source_target_pairs={{4,0},{8,4},{12,8},{5,1},{9,5},{13,9},{6,2},{10,6},{14,10},{7,3},{... | collective-permute-start | bytes 786440 | tf_op jit(solution)/shard_map/ppermute | solution.py:72
  38.4 8.7 %collective-permute-start.7 = (f32[1,128,512]{2,1,0:T(8,128)}, f32[1,128,512]{2,1,0:T(8,128)}, u32[]{:S(2)}, u32[]{:S(2)}) collective-permute-start(f32[1,128,512]{2,1,0:T(8,128)} %bitcast.39), channel_id=1, source_target_pairs={{0,4},{4,8},{8,12},{1,5},{5,9},{9,13},{2,6},{6,10},{10,14},{3,7},{... | collective-permute-start | bytes 786440 | tf_op jit(solution)/shard_map/ppermute | solution.py:71
  43.6 3.5 %copy-start.6 = (f32[1,256,256]{1,2,0:T(8,128)S(1)}, f32[1,256,256]{1,2,0:T(8,128)}, u32[]{:S(2)}) copy-start(f32[1,256,256]{1,2,0:T(8,128)} %copy-done.4) | copy-start | bytes 786436
  49.3 1.6 %copy-start = (f32[4,2,256,256]{3,2,1,0:T(8,128)S(1)}, f32[4,2,256,256]{3,2,1,0:T(8,128)}, u32[]{:S(2)}) copy-start(f32[4,2,256,256]{3,2,1,0:T(8,128)} %param.4) | copy-start | bytes 6291460
  52.7 3.0 %collective-permute-start.10 = (f32[1,4]{1,0:T(1,128)S(1)}, f32[1,4]{1,0:T(1,128)S(1)}, u32[]{:S(2)}, u32[]{:S(2)}) collective-permute-start(f32[1,4]{1,0:T(1,128)S(1)} %subtract_bitcast_fusion), channel_id=1, source_target_pairs={{0,3},{1,2},{2,1},{3,0},{4,7},{5,6},{6,5},{7,4},{8,11},{9,10},{10,... | collective-permute-start | bytes 56 | tf_op jit(solution)/shard_map/ppermute | solution.py:41
  52.8 3.0 %collective-permute-start.8 = (f32[1,4]{1,0:T(1,128)S(1)}, f32[1,4]{1,0:T(1,128)S(1)}, u32[]{:S(2)}, u32[]{:S(2)}) collective-permute-start(f32[1,4]{1,0:T(1,128)S(1)} %subtract_bitcast_fusion), channel_id=1, source_target_pairs={{0,1},{1,0},{2,3},{3,2},{4,5},{5,4},{6,7},{7,6},{8,9},{9,8},{10,11... | collective-permute-start | bytes 56 | tf_op jit(solution)/shard_map/ppermute | solution.py:41
  54.1 3.5 %collective-permute-start.9 = (f32[1,4]{1,0:T(1,128)S(1)}, f32[1,4]{1,0:T(1,128)S(1)}, u32[]{:S(2)}, u32[]{:S(2)}) collective-permute-start(f32[1,4]{1,0:T(1,128)S(1)} %subtract_bitcast_fusion), channel_id=1, source_target_pairs={{0,2},{1,3},{2,0},{3,1},{4,6},{5,7},{6,4},{7,5},{8,10},{9,11},{10,... | collective-permute-start | bytes 56 | tf_op jit(solution)/shard_map/ppermute | solution.py:41

commit v6 on v4

--- a/solution.py
+++ b/solution.py
@@ -17,6 +17,26 @@
     top = jnp.concatenate([u[:, 0], u[:, 1]], axis=-1)
     bottom = jnp.concatenate([-u[:, 1], u[:, 0]], axis=-1)
     return jnp.concatenate([top, bottom], axis=-2)
+
+
+def gauss_ops(u):
+    return jnp.stack([u[:, 0], u[:, 1], u[:, 0] + u[:, 1]], axis=1)
+
+
+def gauss_left(ops, x):
+    order = ops.shape[-1]
+    x_re, x_im = x[:, :order], x[:, order:]
+    rhs = jnp.stack([x_re, x_im, x_re + x_im], axis=1)
+    p = jnp.einsum("mtab,mtbw->mtaw", ops, rhs, precision=HIGH)
+    return jnp.concatenate([p[:, 0] - p[:, 1], p[:, 2] - p[:, 0] - p[:, 1]], axis=-2)
+
+
+def gauss_right(x, ops):
+    order = ops.shape[-1]
+    x_re, x_im = x[..., :order], x[..., order:]
+    lhs = jnp.stack([x_re, x_im, x_re + x_im], axis=1)
+    p = jnp.einsum("mtwa,mtab->mtwb", lhs, ops, precision=HIGH)
+    return jnp.concatenate([p[:, 0] - p[:, 1], p[:, 2] - p[:, 0] - p[:, 1]], axis=-1)
 
 
 def butterfly_sum(value, axes):
@@ -41,8 +61,7 @@
     blocks = lax.axis_size("tm")
     position = lax.axis_index("tm")
     unit = slices[:, 0]
-    left_op = block_left(unit)
-    right_op = block_right(unit)
+    ops = gauss_ops(unit)
     target_dag = jnp.concatenate([target[0].T, -target[1].T], axis=-1)
     right_pairs = [(i, i + 1) for i in range(blocks - 1)]
     left_pairs = [(i + 1, i) for i in range(blocks - 1)]
@@ -70,16 +89,16 @@
             else:
                 fwd_new = jnp.where(
                     is_first, own_cols,
-                    jnp.einsum("mab,mbw->maw", left_op, fwd_in, precision=HIGH),
+                    gauss_left(ops, fwd_in),
                 )
             bwd_in = jnp.where(is_last, rows, bwd_in)
         else:
-            fwd_new = jnp.einsum("mab,mbw->maw", left_op, fwd_in, precision=HIGH)
+            fwd_new = gauss_left(ops, fwd_in)
         fwd_steps.append(fwd_new)
         bwd_steps.append(bwd_in)
         fwd_out = fwd_new
         if step < steps - 1:
-            bwd_out = jnp.einsum("mwa,mab->mwb", bwd_in, right_op, precision=HIGH)
+            bwd_out = gauss_right(bwd_in, ops)
 
     fwd_all = lax.dynamic_slice_in_dim(jnp.stack(fwd_steps), position, chunks, 0)
     bwd_all = lax.dynamic_slice_in_dim(jnp.stack(bwd_steps), blocks - 1 - position, chunks, 0)

time: 58.9 us -> 54.7 us (0.929)
  matrix products: 7.91 us -> 3.93 us
  waiting for transfers between devices: 14.5 us -> 17.6 us
  starting transfers between devices: 27 us -> 24.9 us
  local copies, waits for them, and re-layouts: 4.44 us -> 3.32 us
    ppermute x4, waiting for transfers between devices: 4.92 us -> 9.45 us  [per_device(): fwd_in = lax.ppermute(fwd_out, 'tm', right_pairs)]
    dot_general x8, matrix products: 7.29 us -> 3.31 us  [the longest x4 1.9 us: gauss_left(): p = jnp.einsum('mtab,mtbw->mtaw', ops, rhs, precision=HIGH)]
    ppermute x4, starting transfers between devices: 20.3 us -> 18.1 us  [per_device(): fwd_in = lax.ppermute(fwd_out, 'tm', right_pairs)]
    ppermute x4, waiting for transfers between devices: 6.26 us -> 5.01 us  [per_device(): bwd_in = lax.ppermute(bwd_out, 'tm', left_pairs)]
    squeeze x1 -> x0, local copies, waits for them, and re-layouts: 1.12 us -> none  [block_right(): top = jnp.concatenate([u[:, 0], u[:, 1]], axis=-1)]
    neg x1 -> x0, other arithmetic: 1.07 us -> none  [block_right(): bottom = jnp.concatenate([-u[:, 1], u[:, 0]], axis=-1)]
    unnamed x22 -> x14, local copies, waits for them, and re-layouts: 2.02 us -> 1.5 us
  transfers between devices with their start and end apart: 10 -> 10, of which waited for: 8 -> 7; matrix products, arithmetic and copies ran while one was open for 10% -> 8% of each run, Pallas kernels for 0% -> 0%
where the time goes in v6:
time: 54.7 us; the launch traced here: 54.3 us
  starting transfers between devices  24.9 us (46%)
  waiting for transfers between devices  17.6 us (32%)
  other arithmetic  4 us (7%)
  matrix products  3.93 us (7%)
  local copies, waits for them, and re-layouts  3.32 us (6%)
  between operations  0.58 us (1%)
    ppermute x4, starting transfers between devices, per_device(): fwd_in = lax.ppermute(fwd_out, 'tm', right_pairs)  18.1 us
    ppermute x4, waiting for transfers between devices, per_device(): fwd_in = lax.ppermute(fwd_out, 'tm', right_pairs)  9.45 us
    ppermute x4, starting transfers between devices, per_device(): bwd_in = lax.ppermute(bwd_out, 'tm', left_pairs)  5.17 us
    ppermute x4, waiting for transfers between devices, per_device(): bwd_in = lax.ppermute(bwd_out, 'tm', left_pairs)  5.01 us
    ppermute x2, waiting for transfers between devices, butterfly_sum(): value = value + lax.ppermute(value, axis, pairs)  3.15 us
    dot_general x4, matrix products, gauss_left(): p = jnp.einsum('mtab,mtbw->mtaw', ops, rhs, precision=HIGH)  1.9 us
    ppermute x2, starting transfers between devices, butterfly_sum(): value = value + lax.ppermute(value, axis, pairs)  1.57 us
    unnamed x14, local copies, waits for them, and re-layouts  1.5 us
  transfers between devices with their start and end apart: 10, of which 7 were waited for; matrix products, arithmetic and copies ran while one was open for 8% of the time, Pallas kernels for 0%

profile of v6, /device:TPU:0, one launch (start us, length us, event | category | flops | bytes accessed | tf_op | source)
XLA Modules:
  0.0 54.3 jit_solution(15629419208088242413)
XLA Ops:
  0.0 1.2 %slice_bitcast_fusion.42 = (f32[1,256,128]{2,1,0:T(8,128)S(1)}, f32[1,256,128]{2,1,0:T(8,128)S(1)}, f32[1,1,256,128]{3,2,1,0:T(8,128)S(1)}, f32[1,256,128]{2,1,0...) fusion(f32[1,2,256,256]{3,2,1,0:T(8,128)} %bitcast.338), kind=kLoop, calls=%fused_computation.188 | loop fusion | bytes 1310720 | tf_op jit(solution)/shard_map/concatenate | solution.py:85
  1.3 4.9 %collective-permute-start.4 = (f32[1,512,128]{2,1,0:T(8,128)S(1)}, f32[1,512,128]{2,1,0:T(8,128)S(1)}, u32[]{:S(2)}, u32[]{:S(2)}) collective-permute-start(f32[1,512,128]{2,1,0:T(8,128)S(1)} %pad_maximum_fusion.5), channel_id=1, source_target_pairs={{0,4},{4,8},{8,12},{1,5},{5,9},{9,13},{2,6},{6,10},{10,14},{3,7},{... | collective-permute-start | bytes 786440 | tf_op jit(solution)/shard_map/ppermute | solution.py:81
  7.1 1.3 %collective-permute-start = (f32[1,128,512]{2,1,0:T(8,128)S(1)}, f32[1,128,512]{2,1,0:T(8,128)S(1)}, u32[]{:S(2)}, u32[]{:S(2)}) collective-permute-start(f32[1,128,512]{2,1,0:T(8,128)S(1)} %pad_maximum_fusion.1), channel_id=1, source_target_pairs={{4,0},{8,4},{12,8},{5,1},{9,5},{13,9},{6,2},{10,6},{14,10},{7,3},{... | collective-permute-start | bytes 786440 | tf_op jit(solution)/shard_map/ppermute | solution.py:82
  8.5 3.3 %collective-permute-done.4 = f32[1,512,128]{2,1,0:T(8,128)S(1)} collective-permute-done((f32[1,512,128]{2,1,0:T(8,128)S(1)}, f32[1,512,128]{2,1,0:T(8,128)S(1)}, u32[]{:S(2)}, u32[]{:S(2)}) %collective-permute-start.4) | collective-permute-done | bytes 262176 | tf_op jit(solution)/shard_map/ppermute | solution.py:81
  12.3 4.4 %collective-permute-start.5 = (f32[1,512,128]{2,1,0:T(8,128)S(1)}, f32[1,512,128]{2,1,0:T(8,128)S(1)}, u32[]{:S(2)}, u32[]{:S(2)}) collective-permute-start(f32[1,512,128]{2,1,0:T(8,128)S(1)} %maximum_select_fusion.1), channel_id=1, source_target_pairs={{0,4},{4,8},{8,12},{1,5},{5,9},{9,13},{2,6},{6,10},{10,14},{3,7},{... | collective-permute-start | bytes 786440 | tf_op jit(solution)/shard_map/ppermute | solution.py:81
  17.3 1.3 %collective-permute-start.1 = (f32[1,128,512]{2,1,0:T(8,128)S(1)}, f32[1,128,512]{2,1,0:T(8,128)S(1)}, u32[]{:S(2)}, u32[]{:S(2)}) collective-permute-start(f32[1,128,512]{2,1,0:T(8,128)S(1)} %pad_maximum_fusion.2), channel_id=1, source_target_pairs={{4,0},{8,4},{12,8},{5,1},{9,5},{13,9},{6,2},{10,6},{14,10},{7,3},{... | collective-permute-start | bytes 786440 | tf_op jit(solution)/shard_map/ppermute | solution.py:82
  18.7 2.7 %collective-permute-done.5 = f32[1,512,128]{2,1,0:T(8,128)S(1)} collective-permute-done((f32[1,512,128]{2,1,0:T(8,128)S(1)}, f32[1,512,128]{2,1,0:T(8,128)S(1)}, u32[]{:S(2)}, u32[]{:S(2)}) %collective-permute-start.5) | collective-permute-done | bytes 262176 | tf_op jit(solution)/shard_map/ppermute | solution.py:81
  22.0 4.4 %collective-permute-start.6 = (f32[1,512,128]{2,1,0:T(8,128)S(1)}, f32[1,512,128]{2,1,0:T(8,128)S(1)}, u32[]{:S(2)}, u32[]{:S(2)}) collective-permute-start(f32[1,512,128]{2,1,0:T(8,128)S(1)} %pad_maximum_fusion.6), channel_id=1, source_target_pairs={{0,4},{4,8},{8,12},{1,5},{5,9},{9,13},{2,6},{6,10},{10,14},{3,7},{... | collective-permute-start | bytes 786440 | tf_op jit(solution)/shard_map/ppermute | solution.py:81
  26.9 1.3 %collective-permute-start.2 = (f32[1,128,512]{2,1,0:T(8,128)S(1)}, f32[1,128,512]{2,1,0:T(8,128)S(1)}, u32[]{:S(2)}, u32[]{:S(2)}) collective-permute-start(f32[1,128,512]{2,1,0:T(8,128)S(1)} %pad_maximum_fusion.3), channel_id=1, source_target_pairs={{4,0},{8,4},{12,8},{5,1},{9,5},{13,9},{6,2},{10,6},{14,10},{7,3},{... | collective-permute-start | bytes 786440 | tf_op jit(solution)/shard_map/ppermute | solution.py:82
  28.2 2.0 %collective-permute-done.6 = f32[1,512,128]{2,1,0:T(8,128)S(1)} collective-permute-done((f32[1,512,128]{2,1,0:T(8,128)S(1)}, f32[1,512,128]{2,1,0:T(8,128)S(1)}, u32[]{:S(2)}, u32[]{:S(2)}) %collective-permute-start.6) | collective-permute-done | bytes 262176 | tf_op jit(solution)/shard_map/ppermute | solution.py:81
  30.8 4.4 %collective-permute-start.7 = (f32[1,512,128]{2,1,0:T(8,128)S(1)}, f32[1,512,128]{2,1,0:T(8,128)S(1)}, u32[]{:S(2)}, u32[]{:S(2)}) collective-permute-start(f32[1,512,128]{2,1,0:T(8,128)S(1)} %pad_maximum_fusion.7), channel_id=1, source_target_pairs={{0,4},{4,8},{8,12},{1,5},{5,9},{9,13},{2,6},{6,10},{10,14},{3,7},{... | collective-permute-start | bytes 786440 | tf_op jit(solution)/shard_map/ppermute | solution.py:81
  35.7 0.6 %copy-done.3 = f32[5,1,512,128]{3,2,1,0:T(8,128)} copy-done((f32[5,1,512,128]{3,2,1,0:T(8,128)}, f32[5,1,512,128]{3,2,1,0:T(8,128)S(1)}, u32[]{:S(2)}) %copy-start.3) | copy-done | bytes 1310744
  36.3 1.3 %collective-permute-start.3 = (f32[1,128,512]{2,1,0:T(8,128)S(1)}, f32[1,128,512]{2,1,0:T(8,128)S(1)}, u32[]{:S(2)}, u32[]{:S(2)}) collective-permute-start(f32[1,128,512]{2,1,0:T(8,128)S(1)} %pad_maximum_fusion.4), channel_id=1, source_target_pairs={{4,0},{8,4},{12,8},{5,1},{9,5},{13,9},{6,2},{10,6},{14,10},{7,3},{... | collective-permute-start | bytes 786440 | tf_op jit(solution)/shard_map/ppermute | solution.py:82
  37.7 1.4 %collective-permute-done.7 = f32[1,512,128]{2,1,0:T(8,128)S(1)} collective-permute-done((f32[1,512,128]{2,1,0:T(8,128)S(1)}, f32[1,512,128]{2,1,0:T(8,128)S(1)}, u32[]{:S(2)}, u32[]{:S(2)}) %collective-permute-start.7) | collective-permute-done | bytes 262176 | tf_op jit(solution)/shard_map/ppermute | solution.py:81
  39.6 5.0 %collective-permute-done.3 = f32[1,128,512]{2,1,0:T(8,128)S(1)} collective-permute-done((f32[1,128,512]{2,1,0:T(8,128)S(1)}, f32[1,128,512]{2,1,0:T(8,128)S(1)}, u32[]{:S(2)}, u32[]{:S(2)}) %collective-permute-start.3) | collective-permute-done | bytes 262176 | tf_op jit(solution)/shard_map/ppermute | solution.py:82
  45.0 0.6 %convolution_bitcast_fusion = f32[1,2,2,256,256]{3,4,1,2,0:T(8,128)S(1)} fusion(f32[2,128,2,256,1]{1,3,2,0,4:T(8,128)S(1)} %bitcast.351, f32[2,2,256,128]{3,2,1,0:T(8,128)S(1)} %bitcast.352), kind=kOutput, calls=%fused_computation | convolution fusion | flops 402653184 | bytes 2097152 | tf_op jit(solution)/shard_map/cmpaw,cmwqb->mpqab/dot_general | solution.py:107
  45.6 0.7 %select_reduce_fusion = (f32[]{:T(128)}, f32[256,256]{0,1:T(8,128)S(1)}, f32[]{:T(128)}, f32[256,256]{0,1:T(8,128)S(1)}) fusion(f32[1,2,2,256,256]{3,4,1,2,0:T(8,128)S(1)} %convolution_bitcast_fusion), kind=kLoop, calls=%fused_computation.95 | loop fusion | flops 458750 | bytes 1572872 | tf_op jit(solution)/shard_map/reduce_sum | solution.py:112
  46.6 0.6 %copy-done.1 = f32[4,2,256,256]{3,2,1,0:T(8,128)S(1)} copy-done((f32[4,2,256,256]{3,2,1,0:T(8,128)S(1)}, f32[4,2,256,256]{3,2,1,0:T(8,128)}, u32[]{:S(2)}) %copy-start.1) | copy-done | bytes 2097176
  47.2 0.5 fusion.1
  47.7 1.3 %subtract_bitcast_fusion = f32[1,4]{1,0:T(1,128)S(1)} fusion(f32[4]{0:T(128)S(1)} %get-tuple-element.6, f32[4]{0:T(128)S(1)} %get-tuple-element.5, f32[]{:T(128)} %get-tuple-element.9, f32[]{:T(128)} %get-tuple-element.13), kind=kLoop, calls=%fused_computation.176 | loop fusion | flops 12 | bytes 56 | tf_op jit(solution)/shard_map/sub | solution.py:117
  49.2 1.1 %collective-permute-done.8 = f32[1,4]{1,0:T(1,128)S(1)} collective-permute-done((f32[1,4]{1,0:T(1,128)S(1)}, f32[1,4]{1,0:T(1,128)S(1)}, u32[]{:S(2)}, u32[]{:S(2)}) %collective-permute-start.8) | collective-permute-done | bytes 48 | tf_op jit(solution)/shard_map/ppermute | solution.py:51
  50.3 1.5 %collective-permute-start.9 = (f32[1,4]{1,0:T(1,128)S(1)}, f32[1,4]{1,0:T(1,128)S(1)}, u32[]{:S(2)}, u32[]{:S(2)}) collective-permute-start(f32[1,4]{1,0:T(1,128)S(1)} %add.82), channel_id=1, source_target_pairs={{0,2},{2,0},{1,3},{3,1},{4,6},{6,4},{5,7},{7,5},{8,10},{10,8},{9,1... | collective-permute-start | bytes 56 | tf_op jit(solution)/shard_map/ppermute | solution.py:51
  51.8 2.0 %collective-permute-done.9 = f32[1,4]{1,0:T(1,128)S(1)} collective-permute-done((f32[1,4]{1,0:T(1,128)S(1)}, f32[1,4]{1,0:T(1,128)S(1)}, u32[]{:S(2)}, u32[]{:S(2)}) %collective-permute-start.9) | collective-permute-done | bytes 48 | tf_op jit(solution)/shard_map/ppermute | solution.py:51
  53.8 0.5 add_multiply_fusion
  (67 shorter events, 5.2 us)
Async XLA Ops:
  0.0 6.2 %copy-start = (f32[1,1,2,256,256]{4,3,2,1,0:T(8,128)S(1)}, f32[1,1,2,256,256]{4,3,2,1,0:T(8,128)}, u32[]{:S(2)}) copy-start(f32[1,1,2,256,256]{4,3,2,1,0:T(8,128)} %param.3) | copy-start | bytes 1572868
  0.0 6.3 %copy-start.2 = (f32[2,256,256]{2,1,0:T(8,128)S(1)}, f32[2,256,256]{2,1,0:T(8,128)}, u32[]{:S(2)}) copy-start(f32[2,256,256]{2,1,0:T(8,128)} %param.5) | copy-start | bytes 1572868
  1.3 10.5 %collective-permute-start.4 = (f32[1,512,128]{2,1,0:T(8,128)S(1)}, f32[1,512,128]{2,1,0:T(8,128)S(1)}, u32[]{:S(2)}, u32[]{:S(2)}) collective-permute-start(f32[1,512,128]{2,1,0:T(8,128)S(1)} %pad_maximum_fusion.5), channel_id=1, source_target_pairs={{0,4},{4,8},{8,12},{1,5},{5,9},{9,13},{2,6},{6,10},{10,14},{3,7},{... | collective-permute-start | bytes 786440 | tf_op jit(solution)/shard_map/ppermute | solution.py:81
  7.1 9.7 %collective-permute-start = (f32[1,128,512]{2,1,0:T(8,128)S(1)}, f32[1,128,512]{2,1,0:T(8,128)S(1)}, u32[]{:S(2)}, u32[]{:S(2)}) collective-permute-start(f32[1,128,512]{2,1,0:T(8,128)S(1)} %pad_maximum_fusion.1), channel_id=1, source_target_pairs={{4,0},{8,4},{12,8},{5,1},{9,5},{13,9},{6,2},{10,6},{14,10},{7,3},{... | collective-permute-start | bytes 786440 | tf_op jit(solution)/shard_map/ppermute | solution.py:82
  12.3 9.1 %collective-permute-start.5 = (f32[1,512,128]{2,1,0:T(8,128)S(1)}, f32[1,512,128]{2,1,0:T(8,128)S(1)}, u32[]{:S(2)}, u32[]{:S(2)}) collective-permute-start(f32[1,512,128]{2,1,0:T(8,128)S(1)} %maximum_select_fusion.1), channel_id=1, source_target_pairs={{0,4},{4,8},{8,12},{1,5},{5,9},{9,13},{2,6},{6,10},{10,14},{3,7},{... | collective-permute-start | bytes 786440 | tf_op jit(solution)/shard_map/ppermute | solution.py:81
  17.3 9.1 %collective-permute-start.1 = (f32[1,128,512]{2,1,0:T(8,128)S(1)}, f32[1,128,512]{2,1,0:T(8,128)S(1)}, u32[]{:S(2)}, u32[]{:S(2)}) collective-permute-start(f32[1,128,512]{2,1,0:T(8,128)S(1)} %pad_maximum_fusion.2), channel_id=1, source_target_pairs={{4,0},{8,4},{12,8},{5,1},{9,5},{13,9},{6,2},{10,6},{14,10},{7,3},{... | collective-permute-start | bytes 786440 | tf_op jit(solution)/shard_map/ppermute | solution.py:82
  22.0 8.3 %collective-permute-start.6 = (f32[1,512,128]{2,1,0:T(8,128)S(1)}, f32[1,512,128]{2,1,0:T(8,128)S(1)}, u32[]{:S(2)}, u32[]{:S(2)}) collective-permute-start(f32[1,512,128]{2,1,0:T(8,128)S(1)} %pad_maximum_fusion.6), channel_id=1, source_target_pairs={{0,4},{4,8},{8,12},{1,5},{5,9},{9,13},{2,6},{6,10},{10,14},{3,7},{... | collective-permute-start | bytes 786440 | tf_op jit(solution)/shard_map/ppermute | solution.py:81
  26.9 8.4 %collective-permute-start.2 = (f32[1,128,512]{2,1,0:T(8,128)S(1)}, f32[1,128,512]{2,1,0:T(8,128)S(1)}, u32[]{:S(2)}, u32[]{:S(2)}) collective-permute-start(f32[1,128,512]{2,1,0:T(8,128)S(1)} %pad_maximum_fusion.3), channel_id=1, source_target_pairs={{4,0},{8,4},{12,8},{5,1},{9,5},{13,9},{6,2},{10,6},{14,10},{7,3},{... | collective-permute-start | bytes 786440 | tf_op jit(solution)/shard_map/ppermute | solution.py:82
  30.8 8.3 %collective-permute-start.7 = (f32[1,512,128]{2,1,0:T(8,128)S(1)}, f32[1,512,128]{2,1,0:T(8,128)S(1)}, u32[]{:S(2)}, u32[]{:S(2)}) collective-permute-start(f32[1,512,128]{2,1,0:T(8,128)S(1)} %pad_maximum_fusion.7), channel_id=1, source_target_pairs={{0,4},{4,8},{8,12},{1,5},{5,9},{9,13},{2,6},{6,10},{10,14},{3,7},{... | collective-permute-start | bytes 786440 | tf_op jit(solution)/shard_map/ppermute | solution.py:81
  35.3 1.1 %copy-start.3 = (f32[5,1,512,128]{3,2,1,0:T(8,128)}, f32[5,1,512,128]{3,2,1,0:T(8,128)S(1)}, u32[]{:S(2)}) copy-start(f32[5,1,512,128]{3,2,1,0:T(8,128)S(1)} %bitcast_dynamic-update-slice_fusion) | copy-start | bytes 3932164
  36.3 8.3 %collective-permute-start.3 = (f32[1,128,512]{2,1,0:T(8,128)S(1)}, f32[1,128,512]{2,1,0:T(8,128)S(1)}, u32[]{:S(2)}, u32[]{:S(2)}) collective-permute-start(f32[1,128,512]{2,1,0:T(8,128)S(1)} %pad_maximum_fusion.4), channel_id=1, source_target_pairs={{4,0},{8,4},{12,8},{5,1},{9,5},{13,9},{6,2},{10,6},{14,10},{7,3},{... | collective-permute-start | bytes 786440 | tf_op jit(solution)/shard_map/ppermute | solution.py:82
  39.6 5.3 %copy-start.4 = (f32[5,1,512,128]{3,2,1,0:T(8,128)S(1)}, f32[5,1,512,128]{3,2,1,0:T(8,128)}, u32[]{:S(2)}) copy-start(f32[5,1,512,128]{3,2,1,0:T(8,128)} %copy-done.3) | copy-start | bytes 3932164
  45.6 1.6 %copy-start.1 = (f32[4,2,256,256]{3,2,1,0:T(8,128)S(1)}, f32[4,2,256,256]{3,2,1,0:T(8,128)}, u32[]{:S(2)}) copy-start(f32[4,2,256,256]{3,2,1,0:T(8,128)} %param.4) | copy-start | bytes 6291460
  49.1 1.2 %collective-permute-start.8 = (f32[1,4]{1,0:T(1,128)S(1)}, f32[1,4]{1,0:T(1,128)S(1)}, u32[]{:S(2)}, u32[]{:S(2)}) collective-permute-start(f32[1,4]{1,0:T(1,128)S(1)} %subtract_bitcast_fusion), channel_id=1, source_target_pairs={{0,1},{1,0},{2,3},{3,2},{4,5},{5,4},{6,7},{7,6},{8,9},{9,8},{10,11... | collective-permute-start | bytes 56 | tf_op jit(solution)/shard_map/ppermute | solution.py:51
  50.3 3.5 %collective-permute-start.9 = (f32[1,4]{1,0:T(1,128)S(1)}, f32[1,4]{1,0:T(1,128)S(1)}, u32[]{:S(2)}, u32[]{:S(2)}) collective-permute-start(f32[1,4]{1,0:T(1,128)S(1)} %add.82), channel_id=1, source_target_pairs={{0,2},{2,0},{1,3},{3,1},{4,6},{6,4},{5,7},{7,5},{8,10},{10,8},{9,1... | collective-permute-start | bytes 56 | tf_op jit(solution)/shard_map/ppermute | solution.py:51

commit v7 on v6

--- a/solution.py
+++ b/solution.py
@@ -63,8 +63,6 @@
     unit = slices[:, 0]
     ops = gauss_ops(unit)
     target_dag = jnp.concatenate([target[0].T, -target[1].T], axis=-1)
-    right_pairs = [(i, i + 1) for i in range(blocks - 1)]
-    left_pairs = [(i + 1, i) for i in range(blocks - 1)]
     is_first = position == 0
     is_last = position == blocks - 1
 
@@ -78,8 +76,10 @@
             fwd_in = jnp.zeros((members_here, 2 * order, width), jnp.float32)
             bwd_in = jnp.zeros((members_here, width, 2 * order), jnp.float32)
         else:
-            fwd_in = lax.ppermute(fwd_out, "tm", right_pairs)
-            bwd_in = lax.ppermute(bwd_out, "tm", left_pairs)
+            fwd_pairs = [(i, i + 1) for i in range(max(0, step - chunks), min(blocks - 1, step))]
+            bwd_pairs = [(j, j - 1) for j in range(max(1, blocks - step), min(blocks, blocks - step + chunks))]
+            fwd_in = lax.ppermute(fwd_out, "tm", fwd_pairs)
+            bwd_in = lax.ppermute(bwd_out, "tm", bwd_pairs)
         if step < chunks:
             cols = slice(step * width, (step + 1) * width)
             own_cols = jnp.concatenate([unit[:, 0, :, cols], unit[:, 1, :, cols]], axis=-2)

time: 54.7 us -> 52.3 us (0.956)
  starting transfers between devices: 24.9 us -> 16.2 us
  waiting for transfers between devices: 17.6 us -> 24.6 us
  local copies, waits for them, and re-layouts: 3.32 us -> 2.71 us
    ppermute x8, starting transfers between devices: 23.3 us -> 14.6 us  [the longest x4 10.7 us: per_device(): fwd_in = lax.ppermute(fwd_out, 'tm', fwd_pairs)]
    ppermute x8, waiting for transfers between devices: 14.5 us -> 21.4 us  [the longest x4 14.2 us: per_device(): bwd_in = lax.ppermute(bwd_out, 'tm', bwd_pairs)]
    unnamed x14, local copies, waits for them, and re-layouts: 1.5 us -> 0.89 us
  transfers between devices with their start and end apart: 10 -> 10, of which waited for: 7 -> 6; matrix products, arithmetic and copies ran while one was open for 8% -> 9% of each run, Pallas kernels for 0% -> 0%
where the time goes in v7:
time: 52.3 us; the launch traced here: 52 us
  waiting for transfers between devices  24.6 us (47%)
  starting transfers between devices  16.2 us (31%)
  other arithmetic  4 us (8%)
  matrix products  3.93 us (8%)
  local copies, waits for them, and re-layouts  2.71 us (5%)
  between operations  0.61 us (1%)
    ppermute x4, waiting for transfers between devices, per_device(): bwd_in = lax.ppermute(bwd_out, 'tm', bwd_pairs)  14.2 us
    ppermute x4, starting transfers between devices, per_device(): fwd_in = lax.ppermute(fwd_out, 'tm', fwd_pairs)  10.7 us
    ppermute x4, waiting for transfers between devices, per_device(): fwd_in = lax.ppermute(fwd_out, 'tm', fwd_pairs)  7.27 us
    ppermute x4, starting transfers between devices, per_device(): bwd_in = lax.ppermute(bwd_out, 'tm', bwd_pairs)  3.94 us
    ppermute x2, waiting for transfers between devices, butterfly_sum(): value = value + lax.ppermute(value, axis, pairs)  3.15 us
    dot_general x4, matrix products, gauss_left(): p = jnp.einsum('mtab,mtbw->mtaw', ops, rhs, precision=HIGH)  1.9 us
    ppermute x2, starting transfers between devices, butterfly_sum(): value = value + lax.ppermute(value, axis, pairs)  1.57 us
    dot_general x4, matrix products, gauss_right(): p = jnp.einsum('mtwa,mtab->mtwb', lhs, ops, precision=HIGH)  1.4 us
  transfers between devices with their start and end apart: 10, of which 6 were waited for; matrix products, arithmetic and copies ran while one was open for 9% of the time, Pallas kernels for 0%

profile of v7, /device:TPU:0, one launch (start us, length us, event | category | flops | bytes accessed | tf_op | source)
XLA Modules:
  0.0 52.0 jit_solution(15740444556421057700)
XLA Ops:
  0.0 1.2 %slice_bitcast_fusion.42 = (f32[1,256,128]{2,1,0:T(8,128)S(1)}, f32[1,256,128]{2,1,0:T(8,128)S(1)}, f32[1,1,256,128]{3,2,1,0:T(8,128)S(1)}, f32[1,256,128]{2,1,0...) fusion(f32[1,2,256,256]{3,2,1,0:T(8,128)} %bitcast.338), kind=kLoop, calls=%fused_computation.188 | loop fusion | bytes 1310720 | tf_op jit(solution)/shard_map/concatenate | solution.py:85
  1.3 4.9 %collective-permute-start.4 = (f32[1,512,128]{2,1,0:T(8,128)S(1)}, f32[1,512,128]{2,1,0:T(8,128)S(1)}, u32[]{:S(2)}, u32[]{:S(2)}) collective-permute-start(f32[1,512,128]{2,1,0:T(8,128)S(1)} %pad_maximum_fusion.5), channel_id=1, source_target_pairs={{0,4},{1,5},{2,6},{3,7},{16,20},{17,21},{18,22},{19,23}} | collective-permute-start | bytes 786440 | tf_op jit(solution)/shard_map/ppermute | solution.py:81
  7.1 0.7 %collective-permute-start = (f32[1,128,512]{2,1,0:T(8,128)S(1)}, f32[1,128,512]{2,1,0:T(8,128)S(1)}, u32[]{:S(2)}, u32[]{:S(2)}) collective-permute-start(f32[1,128,512]{2,1,0:T(8,128)S(1)} %pad_maximum_fusion.1), channel_id=1, source_target_pairs={{12,8},{13,9},{14,10},{15,11},{28,24},{29,25},{30,26},{31,27}} | collective-permute-start | bytes 786440 | tf_op jit(solution)/shard_map/ppermute | solution.py:82
  7.9 3.9 %collective-permute-done.4 = f32[1,512,128]{2,1,0:T(8,128)S(1)} collective-permute-done((f32[1,512,128]{2,1,0:T(8,128)S(1)}, f32[1,512,128]{2,1,0:T(8,128)S(1)}, u32[]{:S(2)}, u32[]{:S(2)}) %collective-permute-start.4) | collective-permute-done | bytes 262176 | tf_op jit(solution)/shard_map/ppermute | solution.py:81
  11.8 0.5 convolution_bitcast_fusion.4
  12.3 4.4 %collective-permute-start.5 = (f32[1,512,128]{2,1,0:T(8,128)S(1)}, f32[1,512,128]{2,1,0:T(8,128)S(1)}, u32[]{:S(2)}, u32[]{:S(2)}) collective-permute-start(f32[1,512,128]{2,1,0:T(8,128)S(1)} %maximum_select_fusion.1), channel_id=1, source_target_pairs={{0,4},{4,8},{1,5},{5,9},{2,6},{6,10},{3,7},{7,11},{16,20},{20,24},... | collective-permute-start | bytes 786440 | tf_op jit(solution)/shard_map/ppermute | solution.py:81
  17.3 0.7 %collective-permute-start.1 = (f32[1,128,512]{2,1,0:T(8,128)S(1)}, f32[1,128,512]{2,1,0:T(8,128)S(1)}, u32[]{:S(2)}, u32[]{:S(2)}) collective-permute-start(f32[1,128,512]{2,1,0:T(8,128)S(1)} %pad_maximum_fusion.2), channel_id=1, source_target_pairs={{8,4},{12,8},{9,5},{13,9},{10,6},{14,10},{11,7},{15,11},{24,20},{2... | collective-permute-start | bytes 786440 | tf_op jit(solution)/shard_map/ppermute | solution.py:82
  18.0 3.4 %collective-permute-done.5 = f32[1,512,128]{2,1,0:T(8,128)S(1)} collective-permute-done((f32[1,512,128]{2,1,0:T(8,128)S(1)}, f32[1,512,128]{2,1,0:T(8,128)S(1)}, u32[]{:S(2)}, u32[]{:S(2)}) %collective-permute-start.5) | collective-permute-done | bytes 262176 | tf_op jit(solution)/shard_map/ppermute | solution.py:81
  21.4 0.5 convolution_bitcast_fusion.3
  22.0 0.7 %collective-permute-start.6 = (f32[1,512,128]{2,1,0:T(8,128)S(1)}, f32[1,512,128]{2,1,0:T(8,128)S(1)}, u32[]{:S(2)}, u32[]{:S(2)}) collective-permute-start(f32[1,512,128]{2,1,0:T(8,128)S(1)} %pad_maximum_fusion.6), channel_id=1, source_target_pairs={{4,8},{8,12},{5,9},{9,13},{6,10},{10,14},{7,11},{11,15},{20,24},{2... | collective-permute-start | bytes 786440 | tf_op jit(solution)/shard_map/ppermute | solution.py:81
  23.2 1.3 %collective-permute-start.2 = (f32[1,128,512]{2,1,0:T(8,128)S(1)}, f32[1,128,512]{2,1,0:T(8,128)S(1)}, u32[]{:S(2)}, u32[]{:S(2)}) collective-permute-start(f32[1,128,512]{2,1,0:T(8,128)S(1)} %pad_maximum_fusion.3), channel_id=1, source_target_pairs={{4,0},{8,4},{5,1},{9,5},{6,2},{10,6},{7,3},{11,7},{20,16},{24,20},... | collective-permute-start | bytes 786440 | tf_op jit(solution)/shard_map/ppermute | solution.py:82
  25.1 0.7 %collective-permute-start.7 = (f32[1,512,128]{2,1,0:T(8,128)S(1)}, f32[1,512,128]{2,1,0:T(8,128)S(1)}, u32[]{:S(2)}, u32[]{:S(2)}) collective-permute-start(f32[1,512,128]{2,1,0:T(8,128)S(1)} %pad_maximum_fusion.7), channel_id=1, source_target_pairs={{8,12},{9,13},{10,14},{11,15},{24,28},{25,29},{26,30},{27,31}} | collective-permute-start | bytes 786440 | tf_op jit(solution)/shard_map/ppermute | solution.py:81
  25.8 7.8 %collective-permute-done.2 = f32[1,128,512]{2,1,0:T(8,128)S(1)} collective-permute-done((f32[1,128,512]{2,1,0:T(8,128)S(1)}, f32[1,128,512]{2,1,0:T(8,128)S(1)}, u32[]{:S(2)}, u32[]{:S(2)}) %collective-permute-start.2) | collective-permute-done | bytes 262176 | tf_op jit(solution)/shard_map/ppermute | solution.py:82
  34.1 1.3 %collective-permute-start.3 = (f32[1,128,512]{2,1,0:T(8,128)S(1)}, f32[1,128,512]{2,1,0:T(8,128)S(1)}, u32[]{:S(2)}, u32[]{:S(2)}) collective-permute-start(f32[1,128,512]{2,1,0:T(8,128)S(1)} %pad_maximum_fusion.4), channel_id=1, source_target_pairs={{4,0},{5,1},{6,2},{7,3},{20,16},{21,17},{22,18},{23,19}} | collective-permute-start | bytes 786440 | tf_op jit(solution)/shard_map/ppermute | solution.py:82
  36.0 6.4 %collective-permute-done.3 = f32[1,128,512]{2,1,0:T(8,128)S(1)} collective-permute-done((f32[1,128,512]{2,1,0:T(8,128)S(1)}, f32[1,128,512]{2,1,0:T(8,128)S(1)}, u32[]{:S(2)}, u32[]{:S(2)}) %collective-permute-start.3) | collective-permute-done | bytes 262176 | tf_op jit(solution)/shard_map/ppermute | solution.py:82
  42.7 0.6 %convolution_bitcast_fusion = f32[1,2,2,256,256]{3,4,1,2,0:T(8,128)S(1)} fusion(f32[2,128,2,256,1]{1,3,2,0,4:T(8,128)S(1)} %bitcast.351, f32[2,2,256,128]{3,2,1,0:T(8,128)S(1)} %bitcast.352), kind=kOutput, calls=%fused_computation | convolution fusion | flops 402653184 | bytes 2097152 | tf_op jit(solution)/shard_map/cmpaw,cmwqb->mpqab/dot_general | solution.py:107
  43.3 0.7 %select_reduce_fusion = (f32[]{:T(128)}, f32[256,256]{0,1:T(8,128)S(1)}, f32[]{:T(128)}, f32[256,256]{0,1:T(8,128)S(1)}) fusion(f32[1,2,2,256,256]{3,4,1,2,0:T(8,128)S(1)} %convolution_bitcast_fusion), kind=kLoop, calls=%fused_computation.95 | loop fusion | flops 458750 | bytes 1572872 | tf_op jit(solution)/shard_map/reduce_sum | solution.py:112
  44.3 0.6 %copy-done.1 = f32[4,2,256,256]{3,2,1,0:T(8,128)S(1)} copy-done((f32[4,2,256,256]{3,2,1,0:T(8,128)S(1)}, f32[4,2,256,256]{3,2,1,0:T(8,128)}, u32[]{:S(2)}) %copy-start.1) | copy-done | bytes 2097176
  44.9 0.5 %fusion.1 = (f32[4]{0:T(128)S(1)}, f32[4]{0:T(128)S(1)}) fusion(f32[4,2,256,256]{3,2,1,0:T(8,128)S(1)} %copy-done.1, f32[256,256]{1,0:T(8,128)S(1)} %copy.20, f32[256,256]{1,0:T(8,128)S(1)} %copy.18), kind=kLoop, calls=%fused_computation.12 | loop fusion | flops 2097144 | bytes 2621472 | tf_op jit(solution)/shard_map/reduce_sum | solution.py:116
  45.4 1.3 %subtract_bitcast_fusion = f32[1,4]{1,0:T(1,128)S(1)} fusion(f32[4]{0:T(128)S(1)} %get-tuple-element.6, f32[4]{0:T(128)S(1)} %get-tuple-element.5, f32[]{:T(128)} %get-tuple-element.9, f32[]{:T(128)} %get-tuple-element.13), kind=kLoop, calls=%fused_computation.176 | loop fusion | flops 12 | bytes 56 | tf_op jit(solution)/shard_map/sub | solution.py:117
  46.9 1.1 %collective-permute-done.8 = f32[1,4]{1,0:T(1,128)S(1)} collective-permute-done((f32[1,4]{1,0:T(1,128)S(1)}, f32[1,4]{1,0:T(1,128)S(1)}, u32[]{:S(2)}, u32[]{:S(2)}) %collective-permute-start.8) | collective-permute-done | bytes 48 | tf_op jit(solution)/shard_map/ppermute | solution.py:51
  48.0 1.5 %collective-permute-start.9 = (f32[1,4]{1,0:T(1,128)S(1)}, f32[1,4]{1,0:T(1,128)S(1)}, u32[]{:S(2)}, u32[]{:S(2)}) collective-permute-start(f32[1,4]{1,0:T(1,128)S(1)} %add.82), channel_id=1, source_target_pairs={{0,2},{2,0},{1,3},{3,1},{4,6},{6,4},{5,7},{7,5},{8,10},{10,8},{9,1... | collective-permute-start | bytes 56 | tf_op jit(solution)/shard_map/ppermute | solution.py:51
  49.5 2.0 %collective-permute-done.9 = f32[1,4]{1,0:T(1,128)S(1)} collective-permute-done((f32[1,4]{1,0:T(1,128)S(1)}, f32[1,4]{1,0:T(1,128)S(1)}, u32[]{:S(2)}, u32[]{:S(2)}) %collective-permute-start.9) | collective-permute-done | bytes 48 | tf_op jit(solution)/shard_map/ppermute | solution.py:51
  51.5 0.5 add_multiply_fusion
  (67 shorter events, 4.2 us)
Async XLA Ops:
  0.0 6.2 %copy-start = (f32[1,1,2,256,256]{4,3,2,1,0:T(8,128)S(1)}, f32[1,1,2,256,256]{4,3,2,1,0:T(8,128)}, u32[]{:S(2)}) copy-start(f32[1,1,2,256,256]{4,3,2,1,0:T(8,128)} %param.3) | copy-start | bytes 1572868
  0.0 6.3 %copy-start.2 = (f32[2,256,256]{2,1,0:T(8,128)S(1)}, f32[2,256,256]{2,1,0:T(8,128)}, u32[]{:S(2)}) copy-start(f32[2,256,256]{2,1,0:T(8,128)} %param.5) | copy-start | bytes 1572868
  1.3 10.5 %collective-permute-start.4 = (f32[1,512,128]{2,1,0:T(8,128)S(1)}, f32[1,512,128]{2,1,0:T(8,128)S(1)}, u32[]{:S(2)}, u32[]{:S(2)}) collective-permute-start(f32[1,512,128]{2,1,0:T(8,128)S(1)} %pad_maximum_fusion.5), channel_id=1, source_target_pairs={{0,4},{1,5},{2,6},{3,7},{16,20},{17,21},{18,22},{19,23}} | collective-permute-start | bytes 786440 | tf_op jit(solution)/shard_map/ppermute | solution.py:81
  7.1 9.6 %collective-permute-start = (f32[1,128,512]{2,1,0:T(8,128)S(1)}, f32[1,128,512]{2,1,0:T(8,128)S(1)}, u32[]{:S(2)}, u32[]{:S(2)}) collective-permute-start(f32[1,128,512]{2,1,0:T(8,128)S(1)} %pad_maximum_fusion.1), channel_id=1, source_target_pairs={{12,8},{13,9},{14,10},{15,11},{28,24},{29,25},{30,26},{31,27}} | collective-permute-start | bytes 786440 | tf_op jit(solution)/shard_map/ppermute | solution.py:82
  12.3 9.1 %collective-permute-start.5 = (f32[1,512,128]{2,1,0:T(8,128)S(1)}, f32[1,512,128]{2,1,0:T(8,128)S(1)}, u32[]{:S(2)}, u32[]{:S(2)}) collective-permute-start(f32[1,512,128]{2,1,0:T(8,128)S(1)} %maximum_select_fusion.1), channel_id=1, source_target_pairs={{0,4},{4,8},{1,5},{5,9},{2,6},{6,10},{3,7},{7,11},{16,20},{20,24},... | collective-permute-start | bytes 786440 | tf_op jit(solution)/shard_map/ppermute | solution.py:81
  17.3 5.4 %collective-permute-start.1 = (f32[1,128,512]{2,1,0:T(8,128)S(1)}, f32[1,128,512]{2,1,0:T(8,128)S(1)}, u32[]{:S(2)}, u32[]{:S(2)}) collective-permute-start(f32[1,128,512]{2,1,0:T(8,128)S(1)} %pad_maximum_fusion.2), channel_id=1, source_target_pairs={{8,4},{12,8},{9,5},{13,9},{10,6},{14,10},{11,7},{15,11},{24,20},{2... | collective-permute-start | bytes 786440 | tf_op jit(solution)/shard_map/ppermute | solution.py:82
  22.0 2.5 %collective-permute-start.6 = (f32[1,512,128]{2,1,0:T(8,128)S(1)}, f32[1,512,128]{2,1,0:T(8,128)S(1)}, u32[]{:S(2)}, u32[]{:S(2)}) collective-permute-start(f32[1,512,128]{2,1,0:T(8,128)S(1)} %pad_maximum_fusion.6), channel_id=1, source_target_pairs={{4,8},{8,12},{5,9},{9,13},{6,10},{10,14},{7,11},{11,15},{20,24},{2... | collective-permute-start | bytes 786440 | tf_op jit(solution)/shard_map/ppermute | solution.py:81
  23.2 10.4 %collective-permute-start.2 = (f32[1,128,512]{2,1,0:T(8,128)S(1)}, f32[1,128,512]{2,1,0:T(8,128)S(1)}, u32[]{:S(2)}, u32[]{:S(2)}) collective-permute-start(f32[1,128,512]{2,1,0:T(8,128)S(1)} %pad_maximum_fusion.3), channel_id=1, source_target_pairs={{4,0},{8,4},{5,1},{9,5},{6,2},{10,6},{7,3},{11,7},{20,16},{24,20},... | collective-permute-start | bytes 786440 | tf_op jit(solution)/shard_map/ppermute | solution.py:82
  25.1 10.3 %collective-permute-start.7 = (f32[1,512,128]{2,1,0:T(8,128)S(1)}, f32[1,512,128]{2,1,0:T(8,128)S(1)}, u32[]{:S(2)}, u32[]{:S(2)}) collective-permute-start(f32[1,512,128]{2,1,0:T(8,128)S(1)} %pad_maximum_fusion.7), channel_id=1, source_target_pairs={{8,12},{9,13},{10,14},{11,15},{24,28},{25,29},{26,30},{27,31}} | collective-permute-start | bytes 786440 | tf_op jit(solution)/shard_map/ppermute | solution.py:81
  25.8 8.2 %copy-start.3 = (f32[5,1,512,128]{3,2,1,0:T(8,128)}, f32[5,1,512,128]{3,2,1,0:T(8,128)S(1)}, u32[]{:S(2)}) copy-start(f32[5,1,512,128]{3,2,1,0:T(8,128)S(1)} %bitcast_dynamic-update-slice_fusion) | copy-start | bytes 3932164
  34.1 8.3 %collective-permute-start.3 = (f32[1,128,512]{2,1,0:T(8,128)S(1)}, f32[1,128,512]{2,1,0:T(8,128)S(1)}, u32[]{:S(2)}, u32[]{:S(2)}) collective-permute-start(f32[1,128,512]{2,1,0:T(8,128)S(1)} %pad_maximum_fusion.4), channel_id=1, source_target_pairs={{4,0},{5,1},{6,2},{7,3},{20,16},{21,17},{22,18},{23,19}} | collective-permute-start | bytes 786440 | tf_op jit(solution)/shard_map/ppermute | solution.py:82
  35.9 6.7 %copy-start.4 = (f32[5,1,512,128]{3,2,1,0:T(8,128)S(1)}, f32[5,1,512,128]{3,2,1,0:T(8,128)}, u32[]{:S(2)}) copy-start(f32[5,1,512,128]{3,2,1,0:T(8,128)} %copy-done.3) | copy-start | bytes 3932164
  43.3 1.6 %copy-start.1 = (f32[4,2,256,256]{3,2,1,0:T(8,128)S(1)}, f32[4,2,256,256]{3,2,1,0:T(8,128)}, u32[]{:S(2)}) copy-start(f32[4,2,256,256]{3,2,1,0:T(8,128)} %param.4) | copy-start | bytes 6291460
  46.8 1.2 %collective-permute-start.8 = (f32[1,4]{1,0:T(1,128)S(1)}, f32[1,4]{1,0:T(1,128)S(1)}, u32[]{:S(2)}, u32[]{:S(2)}) collective-permute-start(f32[1,4]{1,0:T(1,128)S(1)} %subtract_bitcast_fusion), channel_id=1, source_target_pairs={{0,1},{1,0},{2,3},{3,2},{4,5},{5,4},{6,7},{7,6},{8,9},{9,8},{10,11... | collective-permute-start | bytes 56 | tf_op jit(solution)/shard_map/ppermute | solution.py:51
  48.0 3.5 %collective-permute-start.9 = (f32[1,4]{1,0:T(1,128)S(1)}, f32[1,4]{1,0:T(1,128)S(1)}, u32[]{:S(2)}, u32[]{:S(2)}) collective-permute-start(f32[1,4]{1,0:T(1,128)S(1)} %add.82), channel_id=1, source_target_pairs={{0,2},{2,0},{1,3},{3,1},{4,6},{6,4},{5,7},{7,5},{8,10},{10,8},{9,1... | collective-permute-start | bytes 56 | tf_op jit(solution)/shard_map/ppermute | solution.py:51
